TPU v7x, 256 devices: a whole 4x4x8 slice. The times are simulated.
256 devices in a mesh: dp: 4 (over y), expert: 64 (over z, x, core).
Axes of the slice: x: 4, y: 4, z: 8, core: 2. Of those that a mesh axis runs over, the one named last changes fastest.
Arguments:
- tokens: bfloat16 [4096, 2048], P('expert'), may hold values from -6 to 6
- attn_gain: float32 [2048], replicated, may hold values from 0.5 to 1.5
- w_query: bfloat16 [2048, 2048], P('expert', 'dp'), may hold values from -0.125 to 0.125
- w_key: bfloat16 [2048, 2048], P('expert', 'dp'), may hold values from -0.125 to 0.125
- w_value: bfloat16 [2048, 2048], P('expert', 'dp'), may hold values from -0.125 to 0.125
- w_out: bfloat16 [2048, 2048], P('expert', 'dp'), may hold values from -0.125 to 0.125
- cache: bfloat16 [131072, 4096], P('expert', 'dp')
- page_table: int32 [64, 16], P('expert'), may hold values from 0 to 15, each once within a row
- cache_len: int32 [64, 4], P('expert'), may hold values from 1 to 512, 1024 in all within a row
- new_len: int32 [64, 4], P('expert'), may hold values from 1 to 32, 64 in all within a row
- kv_owner: int32 [4096, 1], P('expert'), may hold values from 0 to 63; in each aligned block of 64 rows (0 to 63, 64 to 127, ...) at most 2 rows name the same one
- moe_gain: float32 [2048], replicated, may hold values from 0.5 to 1.5
- w_gate: bfloat16 [64, 2048, 1024], P('expert', None, 'dp'), may hold values from -0.125 to 0.125
- w_up: bfloat16 [64, 2048, 1024], P('expert', None, 'dp'), may hold values from -0.125 to 0.125
- w_down: bfloat16 [64, 1024, 2048], P('expert', 'dp'), may hold values from -0.1875 to 0.1875
- expert_ids: int32 [4096, 8], P('expert'), may hold values from 0 to 63, all different within a row; in each aligned block of 64 rows (0 to 63, 64 to 127, ...) at most 16 rows name the same one
- gate_weights: float32 [4096, 8], P('expert'), may hold values from 0.05 to 0.5
Outputs:
- out: bfloat16 [4096, 2048], P('expert')
- new_rows: bfloat16 [8192, 4096], P('expert', 'dp')
Inputs may be any that keep to these rules, and one draw needn't show every extreme that they name: `page_table`: each row of one index of the expert axis lists every local page once; request r reserves the pages in entries r * 4 to (r+1) * 4 - 1. `cache_len`: the lengths of one index sum to 4 * 4 * 128 // 2, and one of them equals 512. `new_len`: the new tokens of one index sum to 64 and stand request by request; one request has exactly 64 // 2. `kv_owner`: among the rows of one device no owner is named more than 2 times; some owner is named exactly 2 times. `expert_ids`: each row names distinct experts; among the rows of one device no expert is named more than 16 times, a bound that some block reaches.
All inputs are finite; a program needn't handle non-finite values.
Results may differ from a plain program's by a relative error of at most 0.012.
The roundings to bfloat16 on the way count: a program that leaves them out, or rounds other values in their place, can miss the bound.
Values may be sent and summed in bfloat16 or wider, within the bound.
No kernel may reach another device: no remote copies, remote signals or barrier semaphores. Data moves between devices by JAX's collectives and lax.ppermute only.
A program may use at most 64 MiB of HBM per device.

v0:
```python
import jax
import jax.numpy as jnp
from jax import lax
from jax.sharding import PartitionSpec as P

HD = 128
PAGE = 128


EPSILON = 1e-05


def norm_rows(row_data, gain_vec):
    mean_sq = jnp.mean(row_data * row_data, axis=-1, keepdims=True)
    return (row_data * lax.rsqrt(mean_sq + EPSILON) * gain_vec).astype(jnp.bfloat16)


def route_rank(route_ids, block_rows, id_range):
    row_total = route_ids.shape[0]
    labels = jnp.arange(id_range, dtype=jnp.int32)
    counts = jnp.sum((route_ids[:, :, None] == labels[None, None, :]).astype(jnp.int32), axis=1)
    counts = counts.reshape(row_total // block_rows, block_rows, id_range)
    before = (jnp.cumsum(counts, axis=1) - counts).reshape(row_total, id_range)
    return jnp.take_along_axis(before, route_ids, axis=1)


def key_masks(table_row, cache_lens, new_lens, row_count, page_size):
    req_count = cache_lens.shape[0]
    pages_here = table_row.shape[0]
    per_request = pages_here // req_count
    slot_ids = jnp.arange(pages_here, dtype=jnp.int32)
    matches = (table_row[:, None] == slot_ids[None, :]).astype(jnp.int32)
    slot_of_page = jnp.sum(matches * slot_ids[:, None], axis=0)
    page_request = slot_of_page // per_request
    page_start = slot_of_page % per_request * page_size
    key_request = jnp.repeat(page_request, page_size)
    key_position = jnp.repeat(page_start, page_size) + jnp.tile(
        jnp.arange(page_size, dtype=jnp.int32), pages_here
    )
    request_ids = jnp.arange(req_count, dtype=jnp.int32)
    key_length = jnp.sum(
        (key_request[:, None] == request_ids[None, :]).astype(jnp.int32) * cache_lens[None, :],
        axis=1,
    )
    request_ends = jnp.cumsum(new_lens)
    tok_ids = jnp.arange(row_count, dtype=jnp.int32)
    tok_request = jnp.sum((tok_ids[:, None] >= request_ends[None, :]).astype(jnp.int32), axis=1)
    cached = (tok_request[:, None] == key_request[None, :]) & (key_position < key_length)[None, :]
    fresh_mask = tok_request[:, None] == tok_request[None, :]
    return jnp.concatenate([cached, fresh_mask], axis=1)


def expert_block(routed, w_gate, w_up, w_down):
    gate_proj = jnp.einsum("necd,edf->necf", routed, w_gate, preferred_element_type=jnp.float32)
    up_proj = jnp.einsum("necd,edf->necf", routed, w_up, preferred_element_type=jnp.float32)
    active = (jax.nn.silu(gate_proj) * up_proj).astype(jnp.bfloat16)
    return jnp.einsum("necf,efd->necd", active, w_down, preferred_element_type=jnp.float32).astype(
        jnp.bfloat16
    )


def local(
    tokens,
    attn_gain,
    w_query,
    w_key,
    w_value,
    w_out,
    cache,
    page_table,
    cache_len,
    new_len,
    kv_owner,
    moe_gain,
    w_gate,
    w_up,
    w_down,
    expert_ids,
    gate_weights,
):
    row_count, model_width = tokens.shape
    n_expert = lax.axis_size("expert")
    local_experts = w_gate.shape[0]
    experts_all = n_expert * local_experts
    top_count = expert_ids.shape[1]
    capacity = min(row_count, 2 * row_count * top_count // experts_all)
    kv_cap = max(2, 2 * row_count // n_expert)
    head_group = w_query.shape[1] // HD
    full_query, full_key, full_value, full_out = (
        lax.all_gather(w_query, "expert", axis=0, tiled=True),
        lax.all_gather(w_key, "expert", axis=0, tiled=True),
        lax.all_gather(w_value, "expert", axis=0, tiled=True),
        lax.all_gather(w_out, "expert", axis=0, tiled=True),
    )
    resid_in = tokens.astype(jnp.float32)
    normed = norm_rows(resid_in, attn_gain)
    queries = jnp.dot(normed, full_query, preferred_element_type=jnp.float32).astype(jnp.bfloat16)
    new_keys = jnp.dot(normed, full_key, preferred_element_type=jnp.float32).astype(jnp.bfloat16)
    new_values = jnp.dot(normed, full_value, preferred_element_type=jnp.float32).astype(
        jnp.bfloat16
    )
    cache_count = cache.shape[0]
    split_cache = cache.reshape(cache_count, 2, head_group, HD)
    all_keys = jnp.concatenate(
        [split_cache[:, 0], new_keys.reshape(row_count, head_group, HD)], axis=0
    )
    all_values = jnp.concatenate(
        [split_cache[:, 1], new_values.reshape(row_count, head_group, HD)], axis=0
    )
    scores = jnp.einsum(
        "thc,rhc->htr",
        queries.reshape(row_count, head_group, HD),
        all_keys,
        preferred_element_type=jnp.float32,
    ) * HD ** (-0.5)
    valid_mask = key_masks(page_table[0], cache_len[0], new_len[0], row_count, PAGE)
    scores = jnp.where(valid_mask[None, :, :], scores, -1e30)
    highest = jnp.max(scores, axis=-1, keepdims=True)
    weights = jnp.exp(scores - highest)
    probs = (weights / jnp.sum(weights, axis=-1, keepdims=True)).astype(jnp.bfloat16)
    heads_out = (
        jnp.einsum("htr,rhc->thc", probs, all_values, preferred_element_type=jnp.float32)
        .astype(jnp.bfloat16)
        .reshape(row_count, head_group * HD)
    )
    attn_part = jnp.einsum("tc,dc->td", heads_out, full_out, preferred_element_type=jnp.float32)
    attn_out = lax.psum(attn_part.astype(jnp.bfloat16), "dp").astype(jnp.float32)
    residual = resid_in + attn_out
    moe_in = norm_rows(residual, moe_gain)
    kv_row = jnp.concatenate([new_keys, new_values], axis=1)
    kv_rank = route_rank(kv_owner, row_count, n_expert)[:, 0]
    kv_buffer = (
        jnp.zeros((n_expert, kv_cap, kv_row.shape[1]), jnp.bfloat16)
        .at[kv_owner[:, 0], kv_rank]
        .set(kv_row)
    )
    slot_rank = route_rank(expert_ids, row_count, experts_all)
    spread_rows = jnp.broadcast_to(moe_in[:, None, :], (row_count, top_count, model_width))
    tok_buffer = (
        jnp.zeros((experts_all, capacity, model_width), jnp.bfloat16)
        .at[expert_ids, slot_rank]
        .set(spread_rows)
    )
    tok_buffer = tok_buffer.reshape(n_expert, local_experts, capacity, model_width)
    got_rows, got_kv = (
        lax.all_to_all(tok_buffer, "expert", split_axis=0, concat_axis=0, tiled=True),
        lax.all_to_all(kv_buffer, "expert", split_axis=0, concat_axis=0, tiled=True),
    )
    partial_value = expert_block(got_rows, w_gate, w_up, w_down)
    returned = lax.all_to_all(
        partial_value, "expert", split_axis=0, concat_axis=0, tiled=True
    ).reshape(experts_all, capacity, model_width)
    picked = returned[expert_ids, slot_rank].astype(jnp.float32)
    moe_part = jnp.sum(picked * gate_weights[:, :, None], axis=1)
    moe_total = lax.psum(moe_part.astype(jnp.bfloat16), "dp").astype(jnp.float32)
    out = (residual + moe_total).astype(jnp.bfloat16)
    new_rows = got_kv.reshape(n_expert * kv_cap, kv_row.shape[1])
    return (out, new_rows)


def solution(mesh):
    placed = (
        P("expert", None),
        P(),
        P("expert", "dp"),
        P("expert", "dp"),
        P("expert", "dp"),
        P("expert", "dp"),
        P("expert", "dp"),
        P("expert", None),
        P("expert", None),
        P("expert", None),
        P("expert", None),
        P(),
        P("expert", None, "dp"),
        P("expert", None, "dp"),
        P("expert", "dp", None),
        P("expert", None),
        P("expert", None),
    )
    return jax.shard_map(
        local,
        mesh=mesh,
        in_specs=placed,
        out_specs=(P("expert", None), P("expert", "dp")),
        check_vma=False,
    )
```

profile of v0, /device:TPU:2, one launch (start us, length us, event | category | flops | bytes accessed | tf_op | source)
XLA Modules:
  0.0 760.5 jit_solution(5198881147081987779)
XLA Ops:
  7.2 0.7 all-gather.9.cloned.1.call-update
  8.0 0.7 all-gather.5.cloned.1.call-update
  8.7 0.7 all-gather.7.cloned.1.call-update
  9.4 0.5 all-gather.11.cloned.1.call-update
  10.0 0.7 select_reduce_fusion.1
  10.8 0.8 reduce-window.8
  11.6 0.1 convert_reduce_fusion.1
  11.7 6.5 copy.68
  18.2 4.0 fusion.85
  22.2 3.9 copy.82
  26.2 2.5 copy.83
  28.7 0.7 copy.75
  29.5 0.1 select_reduce_fusion
  29.6 0.2 fusion.45
  29.8 0.1 broadcast_compare_fusion
  29.8 0.1 bitcast_compare_fusion
  29.9 0.2 compare_and_fusion
  30.1 0.7 pad_add_fusion
  30.8 59.4 %all-gather.9.cloned.1.call-done = bf16[2048,512]{1,0:T(8,128)(2,1)} async-done(((bf16[32,512]{1,0:T(8,128)(2,1)}), bf16[2048,512]{1,0:T(8,128)(2,1)}) %all-gather.9.cloned.1.call-update) | async-done | bytes 2097168 | tf_op jit(solution)/shard_map/all_gather | solution.py:91
  90.1 2.1 convolution_convert_fusion.1
  92.3 0.6 copy_bitcast_fusion.1
  92.9 75.0 %all-gather.5.cloned.1.call-done = bf16[2048,512]{1,0:T(8,128)(2,1)} async-done(((bf16[32,512]{1,0:T(8,128)(2,1)}), bf16[2048,512]{1,0:T(8,128)(2,1)}) %all-gather.5.cloned.1.call-update) | async-done | bytes 2097168 | tf_op jit(solution)/shard_map/all_gather | solution.py:92
  167.9 2.1 convolution_convert_fusion.3
  170.0 0.6 copy_bitcast_fusion
  170.6 75.0 %all-gather.7.cloned.1.call-done = bf16[2048,512]{1,0:T(8,128)(2,1)} async-done(((bf16[32,512]{1,0:T(8,128)(2,1)}), bf16[2048,512]{1,0:T(8,128)(2,1)}) %all-gather.7.cloned.1.call-update) | async-done | bytes 2097168 | tf_op jit(solution)/shard_map/all_gather | solution.py:90
  245.6 2.7 fusion.37
  248.3 4.2 fusion.86
  252.6 2.8 fusion.34
  255.3 67.8 %all-gather.11.cloned.1.call-done = bf16[2048,512]{1,0:T(8,128)(2,1)} async-done(((bf16[32,512]{1,0:T(8,128)(2,1)}), bf16[2048,512]{1,0:T(8,128)(2,1)}) %all-gather.11.cloned.1.call-update) | async-done | bytes 2097168 | tf_op jit(solution)/shard_map/all_gather | solution.py:93
  323.2 3.1 convolution_convert_fusion
  326.3 0.2 convert_reduce_fusion
  326.5 0.1 reduce_window_sum.24
  326.6 0.1 copy.76
  326.7 0.1 reshape.213
  326.8 3.8 gather_fusion.1
  330.5 0.1 reshape.216
  330.7 0.1 copy.78
  330.8 0.1 reshape.227
  330.9 41.1 %all-reduce.3.cloned.1.call-done = bf16[64,2048]{1,0:T(8,128)(2,1)} async-done(((bf16[64,2048]{1,0:T(8,128)(2,1)}), bf16[64,2048]{1,0:T(8,128)(2,1)}) %all-reduce.3.cloned.1.call-update) | async-done | bytes 262160 | tf_op jit(solution)/shard_map/psum | solution.py:127
  372.0 1.1 multiply_reduce_fusion
  373.2 1.1 multiply_convert_fusion
  374.2 0.3 broadcast_bitcast_fusion
  374.5 2.5 broadcast_in_dim.35
  377.0 88.4 %scatter_fusion = bf16[64,16,2048]{2,1,0:T(8,128)(2,1)} fusion(bf16[64,16,2048]{2,1,0:T(8,128)(2,1)} %broadcast_in_dim.35, s32[512]{0:T(512)S(1)} %reshape.227, bf16[512,2048]{1,0:T(8,128)(2,1)S(1)} %broadcast_bitcast_fusion), kind=kCustom, calls=%fused_computation.3 | custom fusion | bytes 6295552 | tf_op jit(solution)/shard_map/scatter | solution.py:142
  465.5 106.8 %all_to_all.15 = bf16[64,1,16,2048]{3,2,1,0:T(8,128)(2,1)S(1)} all-to-all(bf16[64,1,16,2048]{3,2,1,0:T(8,128)(2,1)} %bitcast.152), channel_id=1, replica_groups=mesh['dp'=4,'expert'=64] {'expert'}, dimensions={0} | all-to-all | bytes 8388608 | tf_op jit(solution)/shard_map/all_to_all | solution.py:146
  572.3 2.0 copy-done.2
  574.2 1.3 fusion.16
  575.5 8.5 %convert_bitcast_fusion = bf16[64,1,16,2048]{3,2,1,0:T(8,128)(2,1)} fusion(bf16[1,256,2048]{2,1,0:T(8,128)(2,1)S(1)} %copy-done, bf16[64,1,16,2048]{3,2,1,0:T(8,128)(2,1)} %copy-done.2, bf16[1,2048,256]{2,1,0:T(8,128)(2,1)S(1)} %copy-done.12, f32[64,1,16,256]{3,2,0,1:T(8,128)S(1)} %fusion.16), kind=kOutput, calls=%fused_computation.15 | convolution fusion | flops 2151153664 | bytes 11534336 | tf_op jit(solution)/shard_map/necf,efd->necd/dot_general | solution.py:57
  584.0 5.8 all-to-all-start.1
  589.9 0.1 reduce_window_sum.25
  590.0 0.1 fusion.65
  590.1 0.8 gather_fusion.2
  590.9 0.8 broadcast_in_dim.40
  591.8 9.3 %scatter_fusion.1 = bf16[64,2,1024]{2,1,0:T(2,128)(2,1)} fusion(bf16[64,2,1024]{2,1,0:T(2,128)(2,1)} %broadcast_in_dim.40, s32[64]{0:T(128)S(1)} %fusion.73, bf16[64,1024]{1,0:T(8,128)(2,1)S(1)} %pad_maximum_fusion), kind=kCustom, calls=%fused_computation.4 | custom fusion | bytes 393728 | tf_op jit(solution)/shard_map/scatter | solution.py:135
  601.1 84.8 %all-to-all-done.1 = bf16[64,1,16,2048]{3,2,1,0:T(8,128)(2,1)} async-done(((bf16[64,1,16,2048]{3,2,1,0:T(8,128)(2,1)}), bf16[64,1,16,2048]{3,2,1,0:T(8,128)(2,1)}, u32[]{:S(2)}, u32[]{:S(2)}) %all-to-all-start.1) | async-done | bytes 4194336 | tf_op jit(solution)/shard_map/all_to_all | solution.py:150
  685.9 5.6 all-to-all-start.2
  691.6 0.1 copy.80
  691.7 0.1 reshape.207
  691.8 0.1 copy.81
  691.9 10.0 %gather_fusion = bf16[512,2048]{1,0:T(8,128)(2,1)S(1)} fusion(bf16[64,16,2048]{2,1,0:T(8,128)(2,1)} %bitcast.34, s32[512]{0:T(512)S(1)} %reshape.207), kind=kCustom, calls=%fused_computation | custom fusion | bytes 4198400 | tf_op jit(solution)/shard_map/gather | solution.py:153
  701.8 2.5 fusion.3
  704.4 1.8 reshape.206
  706.2 45.6 %all-reduce.5.cloned.1.call-done = bf16[64,2048]{1,0:T(8,128)(2,1)} async-done(((bf16[64,2048]{1,0:T(8,128)(2,1)}), bf16[64,2048]{1,0:T(8,128)(2,1)}) %all-reduce.5.cloned.1.call-update) | async-done | bytes 262160 | tf_op jit(solution)/shard_map/psum | solution.py:155
  751.8 1.8 add_convert_fusion
  (49 shorter events, 0.6 us)
Async XLA Ops:
  7.2 568.3 %copy-start = (bf16[1,256,2048]{2,1,0:T(8,128)(2,1)S(1)}, bf16[1,256,2048]{2,1,0:T(8,128)(2,1)}, u32[]{:S(2)}) copy-start(bf16[1,256,2048]{2,1,0:T(8,128)(2,1)} %param.31) | copy-start | bytes 3145732
  7.2 83.0 %all-gather.9.cloned.1.call-start = ((), (), s32[]{:S(2)}) async-start(), calls=%async_computation.5 | async-start | bytes 2129920 | tf_op jit(solution)/shard_map/all_gather | solution.py:91
  7.9 160.0 %all-gather.5.cloned.1.call-start = ((), (), s32[]{:S(2)}) async-start(), calls=%async_computation.3 | async-start | bytes 2129920 | tf_op jit(solution)/shard_map/all_gather | solution.py:92
  8.7 237.0 %all-gather.7.cloned.1.call-start = ((), (), s32[]{:S(2)}) async-start(), calls=%async_computation.4 | async-start | bytes 2129920 | tf_op jit(solution)/shard_map/all_gather | solution.py:90
  9.4 313.8 %all-gather.11.cloned.1.call-start = ((), (), s32[]{:S(2)}) async-start(), calls=%async_computation.6 | async-start | bytes 2129920 | tf_op jit(solution)/shard_map/all_gather | solution.py:93
  10.0 362.0 %all-reduce.3.cloned.1.call-start = ((), (), s32[]{:S(2)}) async-start(), calls=%async_computation.7 | async-start | bytes 524288 | tf_op jit(solution)/shard_map/psum | solution.py:127
  26.2 2.5 copy-start.6
  26.2 3.3 copy-start.10
  26.2 3.4 copy-start.1
  26.2 63.9 %copy-start.5 = (f32[2048]{0:T(1024)S(1)}, f32[2048]{0:T(1024)}, u32[]{:S(2)}) copy-start(f32[2048]{0:T(1024)} %param.18) | copy-start | bytes 24580
  248.3 4.2 copy-start.3
  255.3 71.0 %copy-start.4 = (s32[64,8]{1,0:T(8,128)S(1)}, s32[64,8]{1,0:T(8,128)}, u32[]{:S(2)}) copy-start(s32[64,8]{1,0:T(8,128)} %copy.75) | copy-start | bytes 6148
  326.8 46.4 %copy-start.7 = (f32[2048]{0:T(1024)S(1)}, f32[2048]{0:T(1024)}, u32[]{:S(2)}) copy-start(f32[2048]{0:T(1024)} %param.28) | copy-start | bytes 24580
  465.5 108.8 %copy-start.11 = (bf16[1,2048,256]{2,1,0:T(8,128)(2,1)S(1)}, bf16[1,2048,256]{2,1,0:T(8,128)(2,1)}, u32[]{:S(2)}) copy-start(bf16[1,2048,256]{2,1,0:T(8,128)(2,1)} %param.29) | copy-start | bytes 3145732
  572.3 2.0 copy-start.2
  574.2 1.3 copy-start.12
  584.0 5.8 copy-start.9
  584.0 101.9 %all-to-all-start.1 = ((bf16[64,1,16,2048]{3,2,1,0:T(8,128)(2,1)}), bf16[64,1,16,2048]{3,2,1,0:T(8,128)(2,1)}, u32[]{:S(2)}, u32[]{:S(2)}) async-start(bf16[64,1,16,2048]{3,2,1,0:T(8,128)(2,1)} %convert_bitcast_fusion), calls=%async_computation.1 | async-start | bytes 8388608 | tf_op jit(solution)/shard_map/all_to_all | solution.py:150
  589.8 102.0 %copy-start.8 = (f32[64,8]{0,1:T(8,128)S(1)}, f32[64,8]{0,1:T(8,128)}, u32[]{:S(2)}) copy-start(f32[64,8]{0,1:T(8,128)} %param.33) | copy-start | bytes 6148
  685.9 18.5 %all-to-all-start.2 = ((bf16[64,2,1024]{2,1,0:T(2,128)(2,1)}), bf16[64,2,1024]{2,1,0:T(2,128)(2,1)}, u32[]{:S(2)}, u32[]{:S(2)}) async-start(bf16[64,2,1024]{2,1,0:T(2,128)(2,1)} %scatter_fusion.1), calls=%async_computation.2 | async-start | bytes 524288 | tf_op jit(solution)/shard_map/all_to_all | solution.py:147
  691.5 60.3 %all-reduce.5.cloned.1.call-start = ((), (), s32[]{:S(2)}) async-start(), calls=%async_computation.8 | async-start | bytes 524288 | tf_op jit(solution)/shard_map/psum | solution.py:155
Sparse Core Ops, SparseCore 0:
  10.8 79.3 all-gather.8
  92.9 74.9 all-gather.4
  170.6 74.9 all-gather.6
  248.2 74.9 all-gather.10
  326.4 45.5 all-reduce.2
  704.5 47.2 all-reduce.4
where the time goes:
time: 765 us; the launch traced here: 760 us
  waiting for transfers between devices  451 us (59%)
  local copies, waits for them, and re-layouts  139 us (18%)
  blocking collectives  107 us (14%)
  matrix products  26.8 us (4%)
  between operations  14.4 us (2%)
  starting transfers between devices  11.6 us (2%)
  other arithmetic  10.1 us (1%)
    all_to_all x1, blocking collectives, local(): lax.all_to_all(tok_buffer, 'expert', split_axis=0, concat_axis=0, tiled=T...  107 us
    scatter x1, local copies, waits for them, and re-layouts, local(): tok_buffer = jnp.zeros((experts_all, capacity, model_width), jnp.bfloat16...  88.4 us
    all_to_all x1, waiting for transfers between devices, local(): lax.all_to_all(partial_value, 'expert', split_axis=0, concat_axis=0, tile...  84.8 us
    all_gather x1, waiting for transfers between devices, local(): lax.all_gather(w_value, 'expert', axis=0, tiled=True)  75 us
    all_gather x1, waiting for transfers between devices, local(): lax.all_gather(w_query, 'expert', axis=0, tiled=True)  75 us
    all_gather x1, waiting for transfers between devices, local(): lax.all_gather(w_out, 'expert', axis=0, tiled=True)  67.8 us
    all_gather x1, waiting for transfers between devices, local(): lax.all_gather(w_key, 'expert', axis=0, tiled=True)  59.4 us
    psum x1, waiting for transfers between devices, local(): lax.psum(moe_part.astype(jnp.bfloat16), 'dp').astype(jnp.float32)  45.6 us
  transfers between devices with their start and end apart: 8, of which 7 were waited for; matrix products, arithmetic and copies ran while one was open for 9% of the time, Pallas kernels for 0%

commit v1 on v0

--- a/solution.py
+++ b/solution.py
@@ -48,6 +48,31 @@
     cached = (tok_request[:, None] == key_request[None, :]) & (key_position < key_length)[None, :]
     fresh_mask = tok_request[:, None] == tok_request[None, :]
     return jnp.concatenate([cached, fresh_mask], axis=1)
+
+
+def dp_sum(part):
+    n_dp = lax.axis_size("dp")
+    me = lax.axis_index("dp")
+    held = [part] + [
+        lax.ppermute(part, "dp", [(i, (i + s) % n_dp) for i in range(n_dp)])
+        for s in range(1, n_dp)
+    ]
+    held = jnp.stack(held).astype(jnp.float32)
+    order = (me - jnp.arange(n_dp, dtype=jnp.int32)) % n_dp
+    ordered = held[order]
+    total = ordered[0]
+    for j in range(1, n_dp):
+        total = total + ordered[j]
+    return total
+
+
+def one_hot_rows(slots, slot_count):
+    hits = slots[None, :, :] == jnp.arange(slot_count, dtype=jnp.int32)[:, None, None]
+    return jnp.any(hits, axis=2).astype(jnp.bfloat16)
+
+
+def place_rows(pick, rows):
+    return jnp.dot(pick, rows, preferred_element_type=jnp.float32).astype(jnp.bfloat16)
 
 
 def expert_block(routed, w_gate, w_up, w_down):
@@ -86,11 +111,14 @@
     capacity = min(row_count, 2 * row_count * top_count // experts_all)
     kv_cap = max(2, 2 * row_count // n_expert)
     head_group = w_query.shape[1] // HD
+    stacked = lax.all_gather(
+        jnp.stack([w_query, w_key, w_value, w_out]), "expert", axis=1, tiled=True
+    )
     full_query, full_key, full_value, full_out = (
-        lax.all_gather(w_query, "expert", axis=0, tiled=True),
-        lax.all_gather(w_key, "expert", axis=0, tiled=True),
-        lax.all_gather(w_value, "expert", axis=0, tiled=True),
-        lax.all_gather(w_out, "expert", axis=0, tiled=True),
+        stacked[0],
+        stacked[1],
+        stacked[2],
+        stacked[3],
     )
     resid_in = tokens.astype(jnp.float32)
     normed = norm_rows(resid_in, attn_gain)
@@ -124,24 +152,20 @@
         .reshape(row_count, head_group * HD)
     )
     attn_part = jnp.einsum("tc,dc->td", heads_out, full_out, preferred_element_type=jnp.float32)
-    attn_out = lax.psum(attn_part.astype(jnp.bfloat16), "dp").astype(jnp.float32)
+    attn_out = dp_sum(attn_part.astype(jnp.bfloat16))
     residual = resid_in + attn_out
     moe_in = norm_rows(residual, moe_gain)
     kv_row = jnp.concatenate([new_keys, new_values], axis=1)
     kv_rank = route_rank(kv_owner, row_count, n_expert)[:, 0]
-    kv_buffer = (
-        jnp.zeros((n_expert, kv_cap, kv_row.shape[1]), jnp.bfloat16)
-        .at[kv_owner[:, 0], kv_rank]
-        .set(kv_row)
-    )
+    kv_slot = kv_owner[:, 0] * kv_cap + kv_rank
+    kv_pick = one_hot_rows(kv_slot[:, None], n_expert * kv_cap)
+    kv_buffer = place_rows(kv_pick, kv_row).reshape(n_expert, kv_cap, kv_row.shape[1])
     slot_rank = route_rank(expert_ids, row_count, experts_all)
-    spread_rows = jnp.broadcast_to(moe_in[:, None, :], (row_count, top_count, model_width))
-    tok_buffer = (
-        jnp.zeros((experts_all, capacity, model_width), jnp.bfloat16)
-        .at[expert_ids, slot_rank]
-        .set(spread_rows)
-    )
-    tok_buffer = tok_buffer.reshape(n_expert, local_experts, capacity, model_width)
+    tok_slot = expert_ids * capacity + slot_rank
+    tok_pick = one_hot_rows(tok_slot, experts_all * capacity)
+    tok_buffer = place_rows(tok_pick, moe_in).reshape(
+        n_expert, local_experts, capacity, model_width
+    )
     got_rows, got_kv = (
         lax.all_to_all(tok_buffer, "expert", split_axis=0, concat_axis=0, tiled=True),
         lax.all_to_all(kv_buffer, "expert", split_axis=0, concat_axis=0, tiled=True),
@@ -150,9 +174,21 @@
     returned = lax.all_to_all(
         partial_value, "expert", split_axis=0, concat_axis=0, tiled=True
     ).reshape(experts_all, capacity, model_width)
-    picked = returned[expert_ids, slot_rank].astype(jnp.float32)
+    back_pick = (
+        tok_slot.reshape(-1)[:, None] == jnp.arange(experts_all * capacity, dtype=jnp.int32)[None, :]
+    ).astype(jnp.bfloat16)
+    picked = (
+        jnp.dot(
+            back_pick,
+            returned.reshape(experts_all * capacity, model_width),
+            preferred_element_type=jnp.float32,
+        )
+        .astype(jnp.bfloat16)
+        .astype(jnp.float32)
+        .reshape(row_count, top_count, model_width)
+    )
     moe_part = jnp.sum(picked * gate_weights[:, :, None], axis=1)
-    moe_total = lax.psum(moe_part.astype(jnp.bfloat16), "dp").astype(jnp.float32)
+    moe_total = dp_sum(moe_part.astype(jnp.bfloat16))
     out = (residual + moe_total).astype(jnp.bfloat16)
     new_rows = got_kv.reshape(n_expert * kv_cap, kv_row.shape[1])
     return (out, new_rows)

time: 765 us -> 397 us (0.52)
  waiting for transfers between devices: 451 us -> 184 us
  local copies, waits for them, and re-layouts: 139 us -> 32.6 us
    all_gather x4 -> x1, waiting for transfers between devices: 277 us -> 64.7 us  [local(): lax.all_gather(jnp.stack([w_query, w_key, w_value, w_out]), 'expert', axi...]
    scatter x2 -> x0, local copies, waits for them, and re-layouts: 97.7 us -> none  [the longest x1 88.4 us: local(): tok_buffer = jnp.zeros((experts_all, capacity, model_width), jnp.bfloat16...]
    psum x2 -> x0, waiting for transfers between devices: 86.7 us -> none  [the longest x1 45.6 us: local(): lax.psum(moe_part.astype(jnp.bfloat16), 'dp').astype(jnp.float32)]
    ppermute x0 -> x6, waiting for transfers between devices: none -> 20.9 us  [dp_sum(): lax.ppermute(part, 'dp', [(i, (i + s) % n_dp) for i in range(n_dp)])]
    all_to_all x1, waiting for transfers between devices: 84.8 us -> 93.8 us  [local(): lax.all_to_all(partial_value, 'expert', split_axis=0, concat_axis=0, tile...]
    unnamed x32 -> x58, local copies, waits for them, and re-layouts: 15.7 us -> 16.5 us
  transfers between devices with their start and end apart: 8 -> 9, of which waited for: 7 -> 8; matrix products, arithmetic and copies ran while one was open for 9% -> 8% of each run, Pallas kernels for 0% -> 0%
where the time goes in v1:
time: 397 us; the launch traced here: 396 us
  waiting for transfers between devices  184 us (46%)
  blocking collectives  103 us (26%)
  local copies, waits for them, and re-layouts  32.6 us (8%)
  matrix products  32.2 us (8%)
  starting transfers between devices  18 us (5%)
  between operations  14.4 us (4%)
  other arithmetic  10.7 us (3%)
    all_to_all x1, blocking collectives, local(): lax.all_to_all(tok_buffer, 'expert', split_axis=0, concat_axis=0, tiled=T...  103 us
    all_to_all x1, waiting for transfers between devices, local(): lax.all_to_all(partial_value, 'expert', split_axis=0, concat_axis=0, tile...  93.8 us
    all_gather x1, waiting for transfers between devices, local(): lax.all_gather(jnp.stack([w_query, w_key, w_value, w_out]), 'expert', axi...  64.7 us
    ppermute x6, waiting for transfers between devices, dp_sum(): lax.ppermute(part, 'dp', [(i, (i + s) % n_dp) for i in range(n_dp)])  20.9 us
    unnamed x58, local copies, waits for them, and re-layouts  16.5 us
    dot_general x1, matrix products, expert_block(): jnp.einsum('necf,efd->necd', active, w_down, preferred_element_type=jnp.f...  8.47 us
  transfers between devices with their start and end apart: 9, of which 8 were waited for; matrix products, arithmetic and copies ran while one was open for 8% of the time, Pallas kernels for 0%

profile of v1, /device:TPU:2, one launch (start us, length us, event | category | flops | bytes accessed | tf_op | source)
XLA Modules:
  0.0 395.5 jit_solution(14502627948421482185)
XLA Ops:
  7.2 1.6 pad_maximum_fusion
  8.8 6.5 %copy.77 = bf16[2048,1024]{0,1:T(8,128)(2,1)} copy(bf16[2048,1024]{1,0:T(8,128)(2,1)} %param.23) | data formatting | bytes 8388608 | tf_op args[6]
  15.3 4.0 %fusion.100 = (bf16[2048,1,4,128]{0,3,2,1:T(8,128)(2,1)S(1)}, bf16[2048,1,4,128]{0,3,2,1:T(8,128)(2,1)}) fusion(bf16[2048,2,4,128]{0,3,2,1:T(8,128)(2,1)} %bitcast.176), kind=kLoop, calls=%fused_computation.139 | loop fusion | bytes 8388608 | tf_op jit(solution)/shard_map/slice | solution.py:133
  19.3 4.0 copy.93
  23.3 2.5 copy.92
  25.7 0.1 copy.84
  25.8 0.2 reduce-window.8
  26.0 0.2 convert_reduce_fusion
  26.2 0.1 reduce_window_sum.24
  26.3 0.1 copy.85
  26.4 0.1 reshape.323
  26.5 3.8 gather_fusion.2
  30.4 0.1 convert_reduce_fusion.1
  30.5 0.1 select_reduce_fusion.1
  30.7 0.1 select_reduce_fusion
  30.8 0.2 fusion.54
  31.2 0.2 compare_and_fusion
  31.3 64.7 %all-gather.2.cloned.1.call-done = bf16[4,2048,512]{2,1,0:T(8,128)(2,1)} async-done(((bf16[4,32,512]{2,1,0:T(8,128)(2,1)}), bf16[4,2048,512]{2,1,0:T(8,128)(2,1)}) %all-gather.2.cloned.1.call-update) | async-done | bytes 8388624 | tf_op jit(solution)/shard_map/all_gather | solution.py:114
  96.0 2.1 fusion.38
  98.2 0.7 copy_bitcast_fusion
  98.8 2.1 fusion.37
  101.0 0.6 copy_bitcast_fusion.1
  101.6 2.7 fusion.45
  104.4 4.3 %fusion.101 = (f32[4,64]{1,0:T(4,128)S(1)}, f32[4,64,2112]{2,1,0:T(8,128)}) fusion(bf16[64,4,128]{2,0,1:T(8,128)(2,1)} %copy_bitcast_fusion.1, bf16[2048,4,128]{2,0,1:T(8,128)(2,1)} %bitcast.179, pred[64,2112]{1,0:T(8,128)(4,1)S(1)} %pad_add_fusion, bf16[8,4,8,128]{3,2,1,0:T(8,128)(2,1)} %fusion.45), kind=kOutput, calls=%fused_computation.140 | convolution fusion | flops 144902208 | bytes 4527104 | tf_op jit(solution)/shard_map/sub | solution.py:147
  108.6 2.2 fusion.42
  110.8 2.3 convolution_convert_fusion.2
  113.1 2.8 collective-permute-start.2
  115.9 0.8 collective-permute-start.1
  116.7 0.9 collective-permute-start
  117.7 0.1 copy.87
  117.8 0.7 fusion.20
  118.5 9.1 %collective-permute-done.2 = bf16[64,2048]{1,0:T(8,128)(2,1)S(1)} collective-permute-done((bf16[64,2048]{1,0:T(8,128)(2,1)S(1)}, bf16[64,2048]{1,0:T(8,128)(2,1)S(1)}, u32[]{:S(2)}, u32[]{:S(2)}) %collective-permute-start.2) | collective-permute-done | bytes 262176 | tf_op jit(solution)/shard_map/ppermute | solution.py:57
  127.6 3.7 collective-permute-done
  131.3 0.7 copy-done.10
  131.9 1.4 maximum_convert_fusion
  133.3 2.0 gather_fusion
  135.3 1.8 multiply_reduce_fusion
  137.1 1.3 convolution_convert_fusion
  138.5 103.5 %all_to_all.15 = bf16[64,1,16,2048]{3,2,1,0:T(8,128)(2,1)S(1)} all-to-all(bf16[64,1,16,2048]{3,2,1,0:T(8,128)(2,1)S(1)} %bitcast.177), channel_id=1, replica_groups=mesh['dp'=4,'expert'=64] {'expert'}, dimensions={0} | all-to-all | bytes 8388608 | tf_op jit(solution)/shard_map/all_to_all | solution.py:170
  241.9 2.0 copy-done.2
  243.9 1.3 fusion.21
  245.2 8.5 %convert_bitcast_fusion = bf16[64,1,16,2048]{3,2,1,0:T(8,128)(2,1)} fusion(bf16[1,256,2048]{2,1,0:T(8,128)(2,1)S(1)} %copy-done, bf16[64,1,16,2048]{3,2,1,0:T(8,128)(2,1)} %copy-done.2, bf16[1,2048,256]{2,1,0:T(8,128)(2,1)S(1)} %copy-done.22, f32[64,1,16,256]{3,2,0,1:T(8,128)S(1)} %fusion.21), kind=kOutput, calls=%fused_computation.14 | convolution fusion | flops 2151153664 | bytes 11534336 | tf_op jit(solution)/shard_map/necf,efd->necd/dot_general | solution.py:82
  253.7 5.8 %all-to-all-start.1 = ((bf16[64,1,16,2048]{3,2,1,0:T(8,128)(2,1)}), bf16[64,1,16,2048]{3,2,1,0:T(8,128)(2,1)}, u32[]{:S(2)}, u32[]{:S(2)}) async-start(bf16[64,1,16,2048]{3,2,1,0:T(8,128)(2,1)} %convert_bitcast_fusion), calls=%async_computation.1 | async-start | bytes 8388608 | tf_op jit(solution)/shard_map/all_to_all | solution.py:174
  259.4 0.1 eq.157
  259.5 0.1 copy.91
  259.7 0.1 reduce_window_sum.25
  259.9 0.8 gather_fusion.3
  260.7 0.2 convolution_convert_fusion.3
  261.0 0.8 reshape.303
  261.8 93.8 %all-to-all-done.1 = bf16[64,1,16,2048]{3,2,1,0:T(8,128)(2,1)} async-done(((bf16[64,1,16,2048]{3,2,1,0:T(8,128)(2,1)}), bf16[64,1,16,2048]{3,2,1,0:T(8,128)(2,1)}, u32[]{:S(2)}, u32[]{:S(2)}) %all-to-all-start.1) | async-done | bytes 4194336 | tf_op jit(solution)/shard_map/all_to_all | solution.py:174
  355.6 5.4 %all-to-all-start.2 = ((bf16[64,2,1024]{2,1,0:T(2,128)(2,1)}), bf16[64,2,1024]{2,1,0:T(2,128)(2,1)S(1)}, u32[]{:S(2)}, u32[]{:S(2)}) async-start(bf16[64,2,1024]{2,1,0:T(2,128)(2,1)} %reshape.303), calls=%async_computation.2 | async-start | bytes 524288 | tf_op jit(solution)/shard_map/all_to_all | solution.py:171
  361.0 5.3 %fusion.3 = bf16[64,2048]{1,0:T(8,128)(2,1)S(1)} fusion(f32[64,8]{1,0:T(8,128)S(1)} %copy.91, bf16[1024,2048]{1,0:T(8,128)(2,1)} %bitcast.47, s32[512]{0:T(512)S(1)} %eq.157), kind=kOutput, calls=%fused_computation.9 | convolution fusion | flops 2152071168 | bytes 4460544 | tf_op jit(solution)/shard_map/dot_general | solution.py:181
  366.3 0.7 collective-permute-start.5
  367.0 0.8 collective-permute-start.4
  367.8 0.8 collective-permute-start.3
  368.6 4.7 %all-to-all-done.2 = bf16[64,2,1024]{2,1,0:T(2,128)(2,1)S(1)} async-done(((bf16[64,2,1024]{2,1,0:T(2,128)(2,1)}), bf16[64,2,1024]{2,1,0:T(2,128)(2,1)S(1)}, u32[]{:S(2)}, u32[]{:S(2)}) %all-to-all-start.2) | async-done | bytes 262176 | tf_op jit(solution)/shard_map/all_to_all | solution.py:171
  373.2 0.8 reshape.304
  374.0 1.5 collective-permute-done.5
  375.6 2.2 collective-permute-done.4
  377.7 4.4 %collective-permute-done.3 = bf16[64,2048]{1,0:T(8,128)(2,1)S(1)} collective-permute-done((bf16[64,2048]{1,0:T(8,128)(2,1)S(1)}, bf16[64,2048]{1,0:T(8,128)(2,1)S(1)}, u32[]{:S(2)}, u32[]{:S(2)}) %collective-permute-start.3) | collective-permute-done | bytes 262176 | tf_op jit(solution)/shard_map/ppermute | solution.py:57
  382.2 0.7 copy-done.11
  382.9 1.3 maximum_convert_fusion.1
  384.2 2.0 gather_fusion.1
  386.2 2.5 fusion.59
  (73 shorter events, 0.8 us)
Async XLA Ops:
  7.2 238.0 %copy-start = (bf16[1,256,2048]{2,1,0:T(8,128)(2,1)S(1)}, bf16[1,256,2048]{2,1,0:T(8,128)(2,1)}, u32[]{:S(2)}) copy-start(bf16[1,256,2048]{2,1,0:T(8,128)(2,1)} %param.31) | copy-start | bytes 3145732
  7.2 88.9 %all-gather.2.cloned.1.call-start = ((), (), s32[]{:S(2)}) async-start(), calls=%async_computation.3 | async-start | bytes 8519680 | tf_op jit(solution)/shard_map/all_gather | solution.py:114
  23.2 2.5 copy-start.16
  23.2 2.6 copy-start.24
  26.5 4.1 %copy-start.25 = (s32[1,16]{1,0:T(1,128)S(1)}, s32[1,16]{1,0:T(1,128)}, u32[]{:S(2)}) copy-start(s32[1,16]{1,0:T(1,128)} %param.24) | copy-start | bytes 196
  26.5 4.2 %copy-start.20 = (s32[1,4]{1,0:T(1,128)S(1)}, s32[1,4]{1,0:T(1,128)}, u32[]{:S(2)}) copy-start(s32[1,4]{1,0:T(1,128)} %param.25) | copy-start | bytes 52
  26.5 4.3 %copy-start.4 = (bf16[64,2048]{1,0:T(8,128)(2,1)S(1)}, bf16[64,2048]{1,0:T(8,128)(2,1)}, u32[]{:S(2)}) copy-start(bf16[64,2048]{1,0:T(8,128)(2,1)} %param.17) | copy-start | bytes 786436
  26.5 69.5 %copy-start.23 = (f32[2048]{0:T(1024)S(1)}, f32[2048]{0:T(1024)}, u32[]{:S(2)}) copy-start(f32[2048]{0:T(1024)} %param.18) | copy-start | bytes 24580
  98.2 6.2 %copy-start.12 = (bf16[64,512]{1,0:T(8,128)(2,1)}, bf16[64,512]{1,0:T(8,128)(2,1)S(1)}, u32[]{:S(2)}) copy-start(bf16[64,512]{1,0:T(8,128)(2,1)S(1)} %fusion.38) | copy-start | bytes 196612
  100.9 3.4 copy-start.14
  104.3 4.3 %copy-start.3 = (bf16[2048,1,4,128]{3,0,2,1:T(8,128)(2,1)S(1)}, bf16[2048,1,4,128]{3,0,2,1:T(8,128)(2,1)}, u32[]{:S(2)}) copy-start(bf16[2048,1,4,128]{3,0,2,1:T(8,128)(2,1)} %copy.93) | copy-start | bytes 6291460
  113.1 18.1 %copy-start.5 = (bf16[64,2048]{1,0:T(8,128)(2,1)}, bf16[64,2048]{1,0:T(8,128)(2,1)S(1)}, u32[]{:S(2)}) copy-start(bf16[64,2048]{1,0:T(8,128)(2,1)S(1)} %convolution_convert_fusion.2) | copy-start | bytes 786436
  113.1 14.4 %collective-permute-start.2 = (bf16[64,2048]{1,0:T(8,128)(2,1)S(1)}, bf16[64,2048]{1,0:T(8,128)(2,1)S(1)}, u32[]{:S(2)}, u32[]{:S(2)}) collective-permute-start(bf16[64,2048]{1,0:T(8,128)(2,1)S(1)} %convolution_convert_fusion.2), channel_id=1, source_target_pairs={{0,192},{64,0},{128,64},{192,128},{1,193},{65,1},{129,65},{193,129... | collective-permute-start | bytes 786440 | tf_op jit(solution)/shard_map/ppermute | solution.py:57
  115.9 11.6 %collective-permute-start.1 = (bf16[64,2048]{1,0:T(8,128)(2,1)S(1)}, bf16[64,2048]{1,0:T(8,128)(2,1)S(1)}, u32[]{:S(2)}, u32[]{:S(2)}) collective-permute-start(bf16[64,2048]{1,0:T(8,128)(2,1)S(1)} %convolution_convert_fusion.2), channel_id=1, source_target_pairs={{0,128},{64,192},{128,0},{192,64},{1,129},{65,193},{129,1},{193,65... | collective-permute-start | bytes 786440 | tf_op jit(solution)/shard_map/ppermute | solution.py:57
  116.7 14.5 %collective-permute-start = (bf16[64,2048]{1,0:T(8,128)(2,1)S(1)}, bf16[64,2048]{1,0:T(8,128)(2,1)S(1)}, u32[]{:S(2)}, u32[]{:S(2)}) collective-permute-start(bf16[64,2048]{1,0:T(8,128)(2,1)S(1)} %convolution_convert_fusion.2), channel_id=1, source_target_pairs={{0,64},{64,128},{128,192},{192,0},{1,65},{65,129},{129,193},{193,1... | collective-permute-start | bytes 786440 | tf_op jit(solution)/shard_map/ppermute | solution.py:57
  127.6 3.7 copy-start.6
  127.6 3.7 copy-start.8
  131.2 0.7 copy-start.10
  135.3 1.8 copy-start.17
  137.1 1.4 copy-start.1
  138.5 105.4 %copy-start.21 = (bf16[1,2048,256]{2,1,0:T(8,128)(2,1)S(1)}, bf16[1,2048,256]{2,1,0:T(8,128)(2,1)}, u32[]{:S(2)}) copy-start(bf16[1,2048,256]{2,1,0:T(8,128)(2,1)} %param.29) | copy-start | bytes 3145732
  241.9 2.0 copy-start.2
  243.9 1.3 copy-start.22
  253.7 5.9 %copy-start.18 = (f32[64,8]{0,1:T(8,128)S(1)}, f32[64,8]{0,1:T(8,128)}, u32[]{:S(2)}) copy-start(f32[64,8]{0,1:T(8,128)} %param.33) | copy-start | bytes 6148
  253.7 6.0 %copy-start.19 = (s32[64,1]{0,1:T(1,128)S(1)}, s32[64,1]{0,1:T(1,128)}, u32[]{:S(2)}) copy-start(s32[64,1]{0,1:T(1,128)} %param.27) | copy-start | bytes 772
  253.7 7.1 %copy-start.13 = (bf16[64,512]{1,0:T(8,128)(2,1)S(1)}, bf16[64,512]{1,0:T(8,128)(2,1)}, u32[]{:S(2)}) copy-start(bf16[64,512]{1,0:T(8,128)(2,1)} %copy-done.12) | copy-start | bytes 196612
  253.7 7.1 %copy-start.15 = (bf16[64,512]{1,0:T(8,128)(2,1)S(1)}, bf16[64,512]{1,0:T(8,128)(2,1)}, u32[]{:S(2)}) copy-start(bf16[64,512]{1,0:T(8,128)(2,1)} %copy-done.14) | copy-start | bytes 196612
  253.7 101.9 %all-to-all-start.1 = ((bf16[64,1,16,2048]{3,2,1,0:T(8,128)(2,1)}), bf16[64,1,16,2048]{3,2,1,0:T(8,128)(2,1)}, u32[]{:S(2)}, u32[]{:S(2)}) async-start(bf16[64,1,16,2048]{3,2,1,0:T(8,128)(2,1)} %convert_bitcast_fusion), calls=%async_computation.1 | async-start | bytes 8388608 | tf_op jit(solution)/shard_map/all_to_all | solution.py:174
  355.6 17.6 %all-to-all-start.2 = ((bf16[64,2,1024]{2,1,0:T(2,128)(2,1)}), bf16[64,2,1024]{2,1,0:T(2,128)(2,1)S(1)}, u32[]{:S(2)}, u32[]{:S(2)}) async-start(bf16[64,2,1024]{2,1,0:T(2,128)(2,1)} %reshape.303), calls=%async_computation.2 | async-start | bytes 524288 | tf_op jit(solution)/shard_map/all_to_all | solution.py:171
  366.3 9.3 %collective-permute-start.5 = (bf16[64,2048]{1,0:T(8,128)(2,1)S(1)}, bf16[64,2048]{1,0:T(8,128)(2,1)S(1)}, u32[]{:S(2)}, u32[]{:S(2)}) collective-permute-start(bf16[64,2048]{1,0:T(8,128)(2,1)S(1)} %fusion.3), channel_id=1, source_target_pairs={{0,192},{64,0},{128,64},{192,128},{1,193},{65,1},{129,65},{193,129... | collective-permute-start | bytes 786440 | tf_op jit(solution)/shard_map/ppermute | solution.py:57
  367.0 10.7 %collective-permute-start.4 = (bf16[64,2048]{1,0:T(8,128)(2,1)S(1)}, bf16[64,2048]{1,0:T(8,128)(2,1)S(1)}, u32[]{:S(2)}, u32[]{:S(2)}) collective-permute-start(bf16[64,2048]{1,0:T(8,128)(2,1)S(1)} %fusion.3), channel_id=1, source_target_pairs={{0,128},{64,192},{128,0},{192,64},{1,129},{65,193},{129,1},{193,65... | collective-permute-start | bytes 786440 | tf_op jit(solution)/shard_map/ppermute | solution.py:57
  367.8 14.4 %collective-permute-start.3 = (bf16[64,2048]{1,0:T(8,128)(2,1)S(1)}, bf16[64,2048]{1,0:T(8,128)(2,1)S(1)}, u32[]{:S(2)}, u32[]{:S(2)}) collective-permute-start(bf16[64,2048]{1,0:T(8,128)(2,1)S(1)} %fusion.3), channel_id=1, source_target_pairs={{0,64},{64,128},{128,192},{192,0},{1,65},{65,129},{129,193},{193,1... | collective-permute-start | bytes 786440 | tf_op jit(solution)/shard_map/ppermute | solution.py:57
  375.6 6.6 %copy-start.7 = (bf16[64,2048]{1,0:T(8,128)(2,1)}, bf16[64,2048]{1,0:T(8,128)(2,1)S(1)}, u32[]{:S(2)}) copy-start(bf16[64,2048]{1,0:T(8,128)(2,1)S(1)} %collective-permute-done.5) | copy-start | bytes 786436
  377.7 4.5 %copy-start.9 = (bf16[64,2048]{1,0:T(8,128)(2,1)}, bf16[64,2048]{1,0:T(8,128)(2,1)S(1)}, u32[]{:S(2)}) copy-start(bf16[64,2048]{1,0:T(8,128)(2,1)S(1)} %collective-permute-done.4) | copy-start | bytes 786436
  382.2 0.7 copy-start.11
Sparse Core Ops, SparseCore 0:
  11.4 84.6 all-gather.1

commit v2 on v1

--- a/solution.py
+++ b/solution.py
@@ -2,6 +2,7 @@
 import jax.numpy as jnp
 from jax import lax
 from jax.sharding import PartitionSpec as P
+
 
 HD = 128
 PAGE = 128
@@ -76,15 +77,28 @@
 
 
 def expert_block(routed, w_gate, w_up, w_down):
-    gate_proj = jnp.einsum("necd,edf->necf", routed, w_gate, preferred_element_type=jnp.float32)
-    up_proj = jnp.einsum("necd,edf->necf", routed, w_up, preferred_element_type=jnp.float32)
-    active = (jax.nn.silu(gate_proj) * up_proj).astype(jnp.bfloat16)
-    return jnp.einsum("necf,efd->necd", active, w_down, preferred_element_type=jnp.float32).astype(
-        jnp.bfloat16
-    )
-
-
-def local(
+    n_dp = lax.axis_size("dp")
+    sources, local_experts, slots, width = routed.shape
+    held = [(jnp.stack([w_gate, w_up]), w_down)]
+    for s in range(1, n_dp):
+        pairs = [(i, (i + s) % n_dp) for i in range(n_dp)]
+        held.append(tuple(lax.ppermute(a, "dp", pairs) for a in held[0]))
+    outs = []
+    for e in range(local_experts):
+        rows = routed[:, e].reshape(sources * slots, width)
+        total = None
+        for gate_up, down in held:
+            gate_proj = jnp.dot(rows, gate_up[0, e], preferred_element_type=jnp.float32)
+            up_proj = jnp.dot(rows, gate_up[1, e], preferred_element_type=jnp.float32)
+            active = (jax.nn.silu(gate_proj) * up_proj).astype(jnp.bfloat16)
+            part = jnp.dot(active, down[e], preferred_element_type=jnp.float32)
+            part = part.astype(jnp.bfloat16).astype(jnp.float32)
+            total = part if total is None else total + part
+        outs.append(total.reshape(sources, slots, width))
+    return jnp.stack(outs, axis=1)
+
+
+def local_body(
     tokens,
     attn_gain,
     w_query,
@@ -160,32 +174,28 @@
     kv_slot = kv_owner[:, 0] * kv_cap + kv_rank
     kv_pick = one_hot_rows(kv_slot[:, None], n_expert * kv_cap)
     kv_buffer = place_rows(kv_pick, kv_row).reshape(n_expert, kv_cap, kv_row.shape[1])
+    n_dp = lax.axis_size("dp")
+    me_dp = lax.axis_index("dp")
+    quarter = capacity // n_dp
     slot_rank = route_rank(expert_ids, row_count, experts_all)
-    tok_slot = expert_ids * capacity + slot_rank
-    tok_pick = one_hot_rows(tok_slot, experts_all * capacity)
+    in_quarter = slot_rank // quarter == me_dp
+    q_slot = jnp.where(in_quarter, expert_ids * quarter + slot_rank % quarter, -1)
+    tok_pick = one_hot_rows(q_slot, experts_all * quarter)
     tok_buffer = place_rows(tok_pick, moe_in).reshape(
-        n_expert, local_experts, capacity, model_width
-    )
-    got_rows, got_kv = (
-        lax.all_to_all(tok_buffer, "expert", split_axis=0, concat_axis=0, tiled=True),
-        lax.all_to_all(kv_buffer, "expert", split_axis=0, concat_axis=0, tiled=True),
-    )
-    partial_value = expert_block(got_rows, w_gate, w_up, w_down)
+        n_expert, local_experts, quarter, model_width
+    )
+    got_rows = lax.all_to_all(tok_buffer, "expert", split_axis=0, concat_axis=0, tiled=True)
+    got_kv = lax.all_to_all(kv_buffer, "expert", split_axis=0, concat_axis=0, tiled=True)
+    contrib = expert_block(got_rows, w_gate, w_up, w_down)
     returned = lax.all_to_all(
-        partial_value, "expert", split_axis=0, concat_axis=0, tiled=True
-    ).reshape(experts_all, capacity, model_width)
+        contrib.astype(jnp.bfloat16), "expert", split_axis=0, concat_axis=0, tiled=True
+    ).reshape(experts_all * quarter, model_width)
     back_pick = (
-        tok_slot.reshape(-1)[:, None] == jnp.arange(experts_all * capacity, dtype=jnp.int32)[None, :]
+        q_slot.reshape(-1)[:, None]
+        == jnp.arange(experts_all * quarter, dtype=jnp.int32)[None, :]
     ).astype(jnp.bfloat16)
-    picked = (
-        jnp.dot(
-            back_pick,
-            returned.reshape(experts_all * capacity, model_width),
-            preferred_element_type=jnp.float32,
-        )
-        .astype(jnp.bfloat16)
-        .astype(jnp.float32)
-        .reshape(row_count, top_count, model_width)
+    picked = jnp.dot(back_pick, returned, preferred_element_type=jnp.float32).reshape(
+        row_count, top_count, model_width
     )
     moe_part = jnp.sum(picked * gate_weights[:, :, None], axis=1)
     moe_total = dp_sum(moe_part.astype(jnp.bfloat16))
@@ -215,7 +225,7 @@
         P("expert", None),
     )
     return jax.shard_map(
-        local,
+        local_body,
         mesh=mesh,
         in_specs=placed,
         out_specs=(P("expert", None), P("expert", "dp")),

time: 397 us -> 372 us (0.937)
  blocking collectives: 103 us -> 0 us
  waiting for transfers between devices: 184 us -> 232 us
  starting transfers between devices: 18 us -> 40.6 us
  matrix products: 32.2 us -> 40.6 us
    all_to_all x1 -> x0, blocking collectives: 103 us -> none  [local(): lax.all_to_all(tok_buffer, 'expert', split_axis=0, concat_axis=0, tiled=T...]
    ppermute x0 -> x6, waiting for transfers between devices: none -> 93.9 us  [expert_block(): held.append(tuple((lax.ppermute(a, 'dp', pairs) for a in held[0])))]
    all_to_all x2 -> x3, waiting for transfers between devices: 98.5 us -> 51.9 us  [the longest x1 26.6 us: local_body(): lax.all_to_all(contrib.astype(jnp.bfloat16), 'expert', split_axis=0, conc...]
    all_to_all x2 -> x3, starting transfers between devices: 11.2 us -> 23.6 us  [the longest x1 10.4 us: local_body(): lax.all_to_all(contrib.astype(jnp.bfloat16), 'expert', split_axis=0, conc...]
    dot_general x8 -> x14, matrix products: 26.4 us -> 35.7 us  [the longest x4 16.5 us: expert_block(): part = jnp.dot(active, down[e], preferred_element_type=jnp.float32)]
    ppermute x0 -> x6, starting transfers between devices: none -> 6.33 us  [expert_block(): held.append(tuple((lax.ppermute(a, 'dp', pairs) for a in held[0])))]
    unnamed x58 -> x38, local copies, waits for them, and re-layouts: 16.5 us -> 14 us
  transfers between devices with their start and end apart: 9 -> 16, of which waited for: 8 -> 12; matrix products, arithmetic and copies ran while one was open for 8% -> 13% of each run, Pallas kernels for 0% -> 0%
where the time goes in v2:
time: 372 us; the launch traced here: 371 us
  waiting for transfers between devices  232 us (62%)
  starting transfers between devices  40.6 us (11%)
  matrix products  40.6 us (11%)
  local copies, waits for them, and re-layouts  33.1 us (9%)
  between operations  14.4 us (4%)
  other arithmetic  9.85 us (3%)
    ppermute x6, waiting for transfers between devices, expert_block(): held.append(tuple((lax.ppermute(a, 'dp', pairs) for a in held[0])))  93.9 us
    all_gather x1, waiting for transfers between devices, local_body(): lax.all_gather(jnp.stack([w_query, w_key, w_value, w_out]), 'expert', axi...  64.7 us
    all_to_all x1, waiting for transfers between devices, local_body(): lax.all_to_all(contrib.astype(jnp.bfloat16), 'expert', split_axis=0, conc...  26.6 us
    ppermute x6, waiting for transfers between devices, dp_sum(): lax.ppermute(part, 'dp', [(i, (i + s) % n_dp) for i in range(n_dp)])  21.5 us
    all_to_all x1, waiting for transfers between devices, local_body(): lax.all_to_all(tok_buffer, 'expert', split_axis=0, concat_axis=0, tiled=T...  21 us
    dot_general x4, matrix products, expert_block(): part = jnp.dot(active, down[e], preferred_element_type=jnp.float32)  16.5 us
    unnamed x38, local copies, waits for them, and re-layouts  14 us
    ppermute x6, starting transfers between devices, dp_sum(): lax.ppermute(part, 'dp', [(i, (i + s) % n_dp) for i in range(n_dp)])  10.6 us
  transfers between devices with their start and end apart: 16, of which 12 were waited for; matrix products, arithmetic and copies ran while one was open for 13% of the time, Pallas kernels for 0%

profile of v2, /device:TPU:2, one launch (start us, length us, event | category | flops | bytes accessed | tf_op | source)
XLA Modules:
  0.0 370.6 jit_solution(2618008075070840456)
XLA Ops:
  7.2 1.5 pad_maximum_fusion.1
  8.7 6.5 %copy.78 = bf16[2048,1024]{0,1:T(8,128)(2,1)} copy(bf16[2048,1024]{1,0:T(8,128)(2,1)} %param.23) | data formatting | bytes 8388608 | tf_op args[6]
  15.2 4.0 %fusion.113 = (bf16[2048,1,4,128]{0,3,2,1:T(8,128)(2,1)S(1)}, bf16[2048,1,4,128]{0,3,2,1:T(8,128)(2,1)}) fusion(bf16[2048,2,4,128]{0,3,2,1:T(8,128)(2,1)} %bitcast.168), kind=kLoop, calls=%fused_computation.182 | loop fusion | bytes 8388608 | tf_op jit(solution)/shard_map/slice | solution.py:147
  19.2 4.0 %copy.94 = bf16[2048,1,4,128]{3,0,2,1:T(8,128)(2,1)} copy(bf16[2048,1,4,128]{0,3,2,1:T(8,128)(2,1)} %get-tuple-element.5) | data formatting | bytes 4194304
  23.2 2.5 copy.93
  25.8 0.2 reduce-window.8
  26.5 3.8 %gather_fusion.2 = s32[512]{0:T(512)S(1)} fusion(s32[64,64]{1,0:T(8,128)S(1)} %sub.50, s32[512]{0:T(512)S(1)} %reshape.327), kind=kCustom, calls=%fused_computation.2 | custom fusion | bytes 8192 | tf_op jit(solution)/shard_map/jit(take_along_axis)/gather | solution.py:25
  31.3 64.7 %all-gather.2.cloned.1.call-done = bf16[4,2048,512]{2,1,0:T(8,128)(2,1)} async-done(((bf16[4,32,512]{2,1,0:T(8,128)(2,1)}), bf16[4,2048,512]{2,1,0:T(8,128)(2,1)}) %all-gather.2.cloned.1.call-update) | async-done | bytes 8388624 | tf_op jit(solution)/shard_map/all_gather | solution.py:128
  96.0 2.1 fusion.25
  98.2 2.1 fusion.24
  100.3 2.1 fusion.32
  102.4 4.2 %fusion.114 = (f32[4,64]{1,0:T(4,128)S(1)}, f32[4,64,2112]{2,1,0:T(8,128)}) fusion(bf16[64,4,128]{2,0,1:T(8,128)(2,1)S(1)} %copy_bitcast_fusion.1, bf16[2048,4,128]{2,0,1:T(8,128)(2,1)} %bitcast.172, pred[64,2112]{1,0:T(8,128)(4,1)S(1)} %pad_add_fusion, bf16[8,4,8,128]{3,2,1,0:T(8,128)(2,1)S(1)} %fusion.32), kind=kOutput, calls=%fused_computation.183 | convolution fusion | flops 144902208 | bytes 4527104 | tf_op jit(solution)/shard_map/sub | solution.py:161
  106.6 2.2 fusion.29
  108.8 2.3 convolution_convert_fusion.5
  111.2 2.8 collective-permute-start.2
  114.0 0.8 collective-permute-start.1
  114.8 0.9 collective-permute-start
  115.8 0.6 pad_clamp_fusion
  116.4 0.2 fusion.56
  116.6 9.0 %collective-permute-done.2 = bf16[64,2048]{1,0:T(8,128)(2,1)S(1)} collective-permute-done((bf16[64,2048]{1,0:T(8,128)(2,1)S(1)}, bf16[64,2048]{1,0:T(8,128)(2,1)S(1)}, u32[]{:S(2)}, u32[]{:S(2)}) %collective-permute-start.2) | collective-permute-done | bytes 262176 | tf_op jit(solution)/shard_map/ppermute | solution.py:58
  125.6 3.7 collective-permute-done
  129.4 2.1 gather_fusion
  131.6 1.8 multiply_reduce_fusion.1
  133.4 0.8 copy-done
  134.2 0.5 convolution_convert_fusion.4
  134.7 1.3 reshape.306
  136.0 7.5 %all-to-all-start = ((bf16[64,1,4,2048]{3,2,1,0:T(4,128)(2,1)}), bf16[64,1,4,2048]{3,2,1,0:T(4,128)(2,1)S(1)}, u32[]{:S(2)}, u32[]{:S(2)}) async-start(bf16[64,1,4,2048]{3,2,1,0:T(4,128)(2,1)} %bitcast.26), calls=%async_computation | async-start | bytes 2097152 | tf_op jit(solution)/shard_map/all_to_all | solution.py:187
  143.5 1.5 pad_maximum_fusion
  145.0 0.6 collective-permute-start.7
  145.6 0.8 collective-permute-start.5
  146.4 0.8 collective-permute-start.3
  147.2 2.5 collective-permute-start.8
  149.7 1.5 collective-permute-start.6
  151.2 21.0 %all-to-all-done = bf16[64,1,4,2048]{3,2,1,0:T(4,128)(2,1)S(1)} async-done(((bf16[64,1,4,2048]{3,2,1,0:T(4,128)(2,1)}), bf16[64,1,4,2048]{3,2,1,0:T(4,128)(2,1)S(1)}, u32[]{:S(2)}, u32[]{:S(2)}) %all-to-all-start) | async-done | bytes 1048608 | tf_op jit(solution)/shard_map/all_to_all | solution.py:187
  172.2 0.3 reshape_squeeze.3
  172.5 0.4 fusion.45
  172.9 2.8 fusion.4
  175.8 18.1 %collective-permute-done.7 = bf16[2,1,2048,256]{3,2,1,0:T(8,128)(2,1)} collective-permute-done((bf16[2,1,2048,256]{3,2,1,0:T(8,128)(2,1)}, bf16[2,1,2048,256]{3,2,1,0:T(8,128)(2,1)}, u32[]{:S(2)}, u32[]{:S(2)}) %collective-permute-start.7) | collective-permute-done | bytes 2097184 | tf_op jit(solution)/shard_map/ppermute | solution.py:85
  194.0 2.4 fusion.33
  196.3 1.7 fusion.35
  198.0 43.0 %collective-permute-done.3 = bf16[2,1,2048,256]{3,2,1,0:T(8,128)(2,1)} collective-permute-done((bf16[2,1,2048,256]{3,2,1,0:T(8,128)(2,1)}, bf16[2,1,2048,256]{3,2,1,0:T(8,128)(2,1)}, u32[]{:S(2)}, u32[]{:S(2)}) %collective-permute-start.3) | collective-permute-done | bytes 2097184 | tf_op jit(solution)/shard_map/ppermute | solution.py:85
  241.0 2.4 fusion.37
  243.3 17.9 %collective-permute-done.8 = bf16[1,256,2048]{2,1,0:T(8,128)(2,1)} collective-permute-done((bf16[1,256,2048]{2,1,0:T(8,128)(2,1)}, bf16[1,256,2048]{2,1,0:T(8,128)(2,1)}, u32[]{:S(2)}, u32[]{:S(2)}) %collective-permute-start.8) | collective-permute-done | bytes 1048608 | tf_op jit(solution)/shard_map/ppermute | solution.py:85
  261.3 4.3 %fusion.11 = f32[256,2048]{1,0:T(8,128)} fusion(bf16[1,256,2048]{2,1,0:T(8,128)(2,1)} %collective-permute-done.8, f32[256,256]{1,0:T(8,128)} %fusion.33, bf16[256,2048]{1,0:T(8,128)(2,1)S(1)} %reshape_squeeze.3, bf16[2,1,2048,256]{3,2,1,0:T(8,128)(2,1)} %collective-permute-done.7), kind=kOutput, calls=%fused_computation.21 | convolution fusion | flops 538312704 | bytes 5505024 | tf_op jit(solution)/shard_map/dot_general | solution.py:94
  265.6 4.2 %fusion.10 = f32[256,2048]{1,0:T(8,128)} fusion(bf16[1,256,2048]{2,1,0:T(8,128)(2,1)} %collective-permute-done.6, f32[256,256]{1,0:T(8,128)S(1)} %fusion.35, bf16[256,2048]{1,0:T(8,128)(2,1)S(1)} %reshape_squeeze.3, bf16[2,1,2048,256]{3,2,1,0:T(8,128)(2,1)} %collective-permute-done.5), kind=kOutput, calls=%fused_computation.20 | convolution fusion | flops 538312704 | bytes 5505024 | tf_op jit(solution)/shard_map/dot_general | solution.py:94
  269.7 15.0 %collective-permute-done.4 = bf16[1,256,2048]{2,1,0:T(8,128)(2,1)} collective-permute-done((bf16[1,256,2048]{2,1,0:T(8,128)(2,1)}, bf16[1,256,2048]{2,1,0:T(8,128)(2,1)}, u32[]{:S(2)}, u32[]{:S(2)}) %collective-permute-start.4) | collective-permute-done | bytes 1048608 | tf_op jit(solution)/shard_map/ppermute | solution.py:85
  284.7 5.3 %fusion.9 = bf16[256,2048]{1,0:T(8,128)(2,1)} fusion(f32[256,2048]{1,0:T(8,128)} %fusion.11, f32[256,2048]{1,0:T(8,128)} %fusion.10, f32[256,2048]{1,0:T(8,128)S(1)} %fusion.4, bf16[1,256,2048]{2,1,0:T(8,128)(2,1)} %collective-permute-done.4, f32[256,256]{1,0:T(8,128)} %fusion.37, bf16[256,2048]{1,0:T(8,128)(2,1)S(1)} %reshape_squeeze.3, ...), kind=kOutput, calls=%fused_computation.19 | convolution fusion | flops 540409856 | bytes 10747904 | tf_op jit(solution)/shard_map/dot_general | solution.py:94
  289.9 2.3 convert_element_type.158
  292.2 10.4 %all-to-all-start.1 = ((bf16[64,1,4,2048]{3,2,1,0:T(4,128)(2,1)}), bf16[64,1,4,2048]{3,2,1,0:T(4,128)(2,1)S(1)}, u32[]{:S(2)}, u32[]{:S(2)}) async-start(bf16[64,1,4,2048]{3,2,1,0:T(4,128)(2,1)} %bitcast.41), calls=%async_computation.1 | async-start | bytes 2097152 | tf_op jit(solution)/shard_map/all_to_all | solution.py:190
  303.0 0.8 gather_fusion.3
  303.8 0.2 convolution_convert_fusion.6
  304.0 0.8 reshape.309
  304.8 26.6 %all-to-all-done.1 = bf16[64,1,4,2048]{3,2,1,0:T(4,128)(2,1)S(1)} async-done(((bf16[64,1,4,2048]{3,2,1,0:T(4,128)(2,1)}), bf16[64,1,4,2048]{3,2,1,0:T(4,128)(2,1)S(1)}, u32[]{:S(2)}, u32[]{:S(2)}) %all-to-all-start.1) | async-done | bytes 1048608 | tf_op jit(solution)/shard_map/all_to_all | solution.py:190
  331.4 5.7 %all-to-all-start.2 = ((bf16[64,2,1024]{2,1,0:T(2,128)(2,1)}), bf16[64,2,1024]{2,1,0:T(2,128)(2,1)S(1)}, u32[]{:S(2)}, u32[]{:S(2)}) async-start(bf16[64,2,1024]{2,1,0:T(2,128)(2,1)} %reshape.309), calls=%async_computation.2 | async-start | bytes 524288 | tf_op jit(solution)/shard_map/all_to_all | solution.py:188
  337.2 0.3 reshape.346
  337.5 1.5 multiply_reduce_fusion
  339.0 5.1 %collective-permute-start.11 = (bf16[64,2048]{1,0:T(8,128)(2,1)S(1)}, bf16[64,2048]{1,0:T(8,128)(2,1)S(1)}, u32[]{:S(2)}, u32[]{:S(2)}) collective-permute-start(bf16[64,2048]{1,0:T(8,128)(2,1)S(1)} %multiply_reduce_fusion), channel_id=1, source_target_pairs={{0,192},{64,0},{128,64},{192,128},{1,193},{65,1},{129,65},{193,129... | collective-permute-start | bytes 786440 | tf_op jit(solution)/shard_map/ppermute | solution.py:58
  344.1 1.0 collective-permute-start.9
  345.1 4.2 %all-to-all-done.2 = bf16[64,2,1024]{2,1,0:T(2,128)(2,1)S(1)} async-done(((bf16[64,2,1024]{2,1,0:T(2,128)(2,1)}), bf16[64,2,1024]{2,1,0:T(2,128)(2,1)S(1)}, u32[]{:S(2)}, u32[]{:S(2)}) %all-to-all-start.2) | async-done | bytes 262176 | tf_op jit(solution)/shard_map/all_to_all | solution.py:188
  349.3 0.8 reshape.310
  350.1 5.5 %collective-permute-done.11 = bf16[64,2048]{1,0:T(8,128)(2,1)S(1)} collective-permute-done((bf16[64,2048]{1,0:T(8,128)(2,1)S(1)}, bf16[64,2048]{1,0:T(8,128)(2,1)S(1)}, u32[]{:S(2)}, u32[]{:S(2)}) %collective-permute-start.11) | collective-permute-done | bytes 262176 | tf_op jit(solution)/shard_map/ppermute | solution.py:58
  355.6 3.4 collective-permute-done.9
  359.2 2.3 gather_fusion.1
  361.4 2.4 fusion.52
  (76 shorter events, 2.7 us)
Async XLA Ops:
  7.2 88.9 %all-gather.2.cloned.1.call-start = ((), (), s32[]{:S(2)}) async-start(), calls=%async_computation.3 | async-start | bytes 8519680 | tf_op jit(solution)/shard_map/all_gather | solution.py:128
  23.2 2.5 copy-start.8
  23.2 2.6 copy-start.14
  26.4 4.1 %copy-start.15 = (s32[1,16]{1,0:T(1,128)S(1)}, s32[1,16]{1,0:T(1,128)}, u32[]{:S(2)}) copy-start(s32[1,16]{1,0:T(1,128)} %param.24) | copy-start | bytes 196
  26.4 4.2 %copy-start.12 = (s32[1,4]{1,0:T(1,128)S(1)}, s32[1,4]{1,0:T(1,128)}, u32[]{:S(2)}) copy-start(s32[1,4]{1,0:T(1,128)} %param.25) | copy-start | bytes 52
  26.4 4.3 %copy-start.5 = (bf16[64,2048]{1,0:T(8,128)(2,1)S(1)}, bf16[64,2048]{1,0:T(8,128)(2,1)}, u32[]{:S(2)}) copy-start(bf16[64,2048]{1,0:T(8,128)(2,1)} %param.17) | copy-start | bytes 786436
  26.4 69.6 %copy-start.13 = (f32[2048]{0:T(1024)S(1)}, f32[2048]{0:T(1024)}, u32[]{:S(2)}) copy-start(f32[2048]{0:T(1024)} %param.18) | copy-start | bytes 24580
  102.4 4.2 %copy-start.4 = (bf16[2048,1,4,128]{3,0,2,1:T(8,128)(2,1)S(1)}, bf16[2048,1,4,128]{3,0,2,1:T(8,128)(2,1)}, u32[]{:S(2)}) copy-start(bf16[2048,1,4,128]{3,0,2,1:T(8,128)(2,1)} %copy.94) | copy-start | bytes 6291460
  111.2 14.4 %collective-permute-start.2 = (bf16[64,2048]{1,0:T(8,128)(2,1)S(1)}, bf16[64,2048]{1,0:T(8,128)(2,1)S(1)}, u32[]{:S(2)}, u32[]{:S(2)}) collective-permute-start(bf16[64,2048]{1,0:T(8,128)(2,1)S(1)} %convolution_convert_fusion.5), channel_id=1, source_target_pairs={{0,192},{64,0},{128,64},{192,128},{1,193},{65,1},{129,65},{193,129... | collective-permute-start | bytes 786440 | tf_op jit(solution)/shard_map/ppermute | solution.py:58
  114.0 11.6 %collective-permute-start.1 = (bf16[64,2048]{1,0:T(8,128)(2,1)S(1)}, bf16[64,2048]{1,0:T(8,128)(2,1)S(1)}, u32[]{:S(2)}, u32[]{:S(2)}) collective-permute-start(bf16[64,2048]{1,0:T(8,128)(2,1)S(1)} %convolution_convert_fusion.5), channel_id=1, source_target_pairs={{0,128},{64,192},{128,0},{192,64},{1,129},{65,193},{129,1},{193,65... | collective-permute-start | bytes 786440 | tf_op jit(solution)/shard_map/ppermute | solution.py:58
  114.8 14.5 %collective-permute-start = (bf16[64,2048]{1,0:T(8,128)(2,1)S(1)}, bf16[64,2048]{1,0:T(8,128)(2,1)S(1)}, u32[]{:S(2)}, u32[]{:S(2)}) collective-permute-start(bf16[64,2048]{1,0:T(8,128)(2,1)S(1)} %convolution_convert_fusion.5), channel_id=1, source_target_pairs={{0,64},{64,128},{128,192},{192,0},{1,65},{65,129},{129,193},{193,1... | collective-permute-start | bytes 786440 | tf_op jit(solution)/shard_map/ppermute | solution.py:58
  115.8 13.5 %copy-start.6 = (s32[64,8]{1,0:T(8,128)}, s32[64,8]{1,0:T(8,128)S(1)}, u32[]{:S(2)}) copy-start(s32[64,8]{1,0:T(8,128)S(1)} %copy.88) | copy-start | bytes 6148
  131.6 2.6 copy-start.9
  133.4 0.8 copy-start
  134.7 8.8 %copy-start.2 = (bf16[1,2048,256]{2,1,0:T(8,128)(2,1)S(1)}, bf16[1,2048,256]{2,1,0:T(8,128)(2,1)}, u32[]{:S(2)}) copy-start(bf16[1,2048,256]{2,1,0:T(8,128)(2,1)} %param.29) | copy-start | bytes 3145732
  135.9 7.5 %copy-start.3 = (bf16[1,2048,256]{2,1,0:T(8,128)(2,1)S(1)}, bf16[1,2048,256]{2,1,0:T(8,128)(2,1)}, u32[]{:S(2)}) copy-start(bf16[1,2048,256]{2,1,0:T(8,128)(2,1)} %param.30) | copy-start | bytes 3145732
  136.0 36.3 %all-to-all-start = ((bf16[64,1,4,2048]{3,2,1,0:T(4,128)(2,1)}), bf16[64,1,4,2048]{3,2,1,0:T(4,128)(2,1)S(1)}, u32[]{:S(2)}, u32[]{:S(2)}) async-start(bf16[64,1,4,2048]{3,2,1,0:T(4,128)(2,1)} %bitcast.26), calls=%async_computation | async-start | bytes 2097152 | tf_op jit(solution)/shard_map/all_to_all | solution.py:187
  145.0 48.8 %collective-permute-start.7 = (bf16[2,1,2048,256]{3,2,1,0:T(8,128)(2,1)}, bf16[2,1,2048,256]{3,2,1,0:T(8,128)(2,1)}, u32[]{:S(2)}, u32[]{:S(2)}) collective-permute-start(bf16[2,1,2048,256]{3,2,1,0:T(8,128)(2,1)} %pad_maximum_fusion), channel_id=1, source_target_pairs={{0,192},{64,0},{128,64},{192,128},{1,193},{65,1},{129,65},{193,129... | collective-permute-start | bytes 6291464 | tf_op jit(solution)/shard_map/ppermute | solution.py:85
  145.6 50.7 %collective-permute-start.5 = (bf16[2,1,2048,256]{3,2,1,0:T(8,128)(2,1)}, bf16[2,1,2048,256]{3,2,1,0:T(8,128)(2,1)}, u32[]{:S(2)}, u32[]{:S(2)}) collective-permute-start(bf16[2,1,2048,256]{3,2,1,0:T(8,128)(2,1)} %pad_maximum_fusion), channel_id=1, source_target_pairs={{0,128},{64,192},{128,0},{192,64},{1,129},{65,193},{129,1},{193,65... | collective-permute-start | bytes 6291464 | tf_op jit(solution)/shard_map/ppermute | solution.py:85
  146.4 94.6 %collective-permute-start.3 = (bf16[2,1,2048,256]{3,2,1,0:T(8,128)(2,1)}, bf16[2,1,2048,256]{3,2,1,0:T(8,128)(2,1)}, u32[]{:S(2)}, u32[]{:S(2)}) collective-permute-start(bf16[2,1,2048,256]{3,2,1,0:T(8,128)(2,1)} %pad_maximum_fusion), channel_id=1, source_target_pairs={{0,64},{64,128},{128,192},{192,0},{1,65},{65,129},{129,193},{193,1... | collective-permute-start | bytes 6291464 | tf_op jit(solution)/shard_map/ppermute | solution.py:85
  147.2 114.1 %collective-permute-start.8 = (bf16[1,256,2048]{2,1,0:T(8,128)(2,1)}, bf16[1,256,2048]{2,1,0:T(8,128)(2,1)}, u32[]{:S(2)}, u32[]{:S(2)}) collective-permute-start(bf16[1,256,2048]{2,1,0:T(8,128)(2,1)} %param.31), channel_id=1, source_target_pairs={{0,192},{64,0},{128,64},{192,128},{1,193},{65,1},{129,65},{193,129... | collective-permute-start | bytes 3145736 | tf_op jit(solution)/shard_map/ppermute | solution.py:85
  149.7 115.9 %collective-permute-start.6 = (bf16[1,256,2048]{2,1,0:T(8,128)(2,1)}, bf16[1,256,2048]{2,1,0:T(8,128)(2,1)}, u32[]{:S(2)}, u32[]{:S(2)}) collective-permute-start(bf16[1,256,2048]{2,1,0:T(8,128)(2,1)} %param.31), channel_id=1, source_target_pairs={{0,128},{64,192},{128,0},{192,64},{1,129},{65,193},{129,1},{193,65... | collective-permute-start | bytes 3145736 | tf_op jit(solution)/shard_map/ppermute | solution.py:85
  193.8 90.9 %collective-permute-start.4 = (bf16[1,256,2048]{2,1,0:T(8,128)(2,1)}, bf16[1,256,2048]{2,1,0:T(8,128)(2,1)}, u32[]{:S(2)}, u32[]{:S(2)}) collective-permute-start(bf16[1,256,2048]{2,1,0:T(8,128)(2,1)} %param.31), channel_id=1, source_target_pairs={{0,64},{64,128},{128,192},{192,0},{1,65},{65,129},{129,193},{193,1... | collective-permute-start | bytes 3145736 | tf_op jit(solution)/shard_map/ppermute | solution.py:85
  289.9 12.7 %copy-start.11 = (s32[64,1]{0,1:T(1,128)S(1)}, s32[64,1]{0,1:T(1,128)}, u32[]{:S(2)}) copy-start(s32[64,1]{0,1:T(1,128)} %param.27) | copy-start | bytes 772
  292.2 44.9 %copy-start.10 = (f32[64,8]{0,1:T(8,128)S(1)}, f32[64,8]{0,1:T(8,128)}, u32[]{:S(2)}) copy-start(f32[64,8]{0,1:T(8,128)} %param.33) | copy-start | bytes 6148
  292.2 39.2 %all-to-all-start.1 = ((bf16[64,1,4,2048]{3,2,1,0:T(4,128)(2,1)}), bf16[64,1,4,2048]{3,2,1,0:T(4,128)(2,1)S(1)}, u32[]{:S(2)}, u32[]{:S(2)}) async-start(bf16[64,1,4,2048]{3,2,1,0:T(4,128)(2,1)} %bitcast.41), calls=%async_computation.1 | async-start | bytes 2097152 | tf_op jit(solution)/shard_map/all_to_all | solution.py:190
  302.9 34.6 %copy-start.7 = (s32[64,8]{1,0:T(8,128)S(1)}, s32[64,8]{1,0:T(8,128)}, u32[]{:S(2)}) copy-start(s32[64,8]{1,0:T(8,128)} %copy-done.6) | copy-start | bytes 6148
  331.4 17.9 %all-to-all-start.2 = ((bf16[64,2,1024]{2,1,0:T(2,128)(2,1)}), bf16[64,2,1024]{2,1,0:T(2,128)(2,1)S(1)}, u32[]{:S(2)}, u32[]{:S(2)}) async-start(bf16[64,2,1024]{2,1,0:T(2,128)(2,1)} %reshape.309), calls=%async_computation.2 | async-start | bytes 524288 | tf_op jit(solution)/shard_map/all_to_all | solution.py:188
  339.0 16.6 %collective-permute-start.11 = (bf16[64,2048]{1,0:T(8,128)(2,1)S(1)}, bf16[64,2048]{1,0:T(8,128)(2,1)S(1)}, u32[]{:S(2)}, u32[]{:S(2)}) collective-permute-start(bf16[64,2048]{1,0:T(8,128)(2,1)S(1)} %multiply_reduce_fusion), channel_id=1, source_target_pairs={{0,192},{64,0},{128,64},{192,128},{1,193},{65,1},{129,65},{193,129... | collective-permute-start | bytes 786440 | tf_op jit(solution)/shard_map/ppermute | solution.py:58
  344.1 11.5 %collective-permute-start.10 = (bf16[64,2048]{1,0:T(8,128)(2,1)S(1)}, bf16[64,2048]{1,0:T(8,128)(2,1)S(1)}, u32[]{:S(2)}, u32[]{:S(2)}) collective-permute-start(bf16[64,2048]{1,0:T(8,128)(2,1)S(1)} %multiply_reduce_fusion), channel_id=1, source_target_pairs={{0,128},{64,192},{128,0},{192,64},{1,129},{65,193},{129,1},{193,65... | collective-permute-start | bytes 786440 | tf_op jit(solution)/shard_map/ppermute | solution.py:58
  344.1 14.9 %collective-permute-start.9 = (bf16[64,2048]{1,0:T(8,128)(2,1)S(1)}, bf16[64,2048]{1,0:T(8,128)(2,1)S(1)}, u32[]{:S(2)}, u32[]{:S(2)}) collective-permute-start(bf16[64,2048]{1,0:T(8,128)(2,1)S(1)} %multiply_reduce_fusion), channel_id=1, source_target_pairs={{0,64},{64,128},{128,192},{192,0},{1,65},{65,129},{129,193},{193,1... | collective-permute-start | bytes 786440 | tf_op jit(solution)/shard_map/ppermute | solution.py:58
  359.2 2.3 copy-start.1
Sparse Core Ops, SparseCore 0:
  11.4 84.6 all-gather.1

commit v3 on v2

--- a/solution.py
+++ b/solution.py
@@ -79,10 +79,14 @@
 def expert_block(routed, w_gate, w_up, w_down):
     n_dp = lax.axis_size("dp")
     sources, local_experts, slots, width = routed.shape
+    me_dp = lax.axis_index("dp")
+    down_all = lax.all_gather(w_down, "dp", axis=0, tiled=False)
     held = [(jnp.stack([w_gate, w_up]), w_down)]
     for s in range(1, n_dp):
         pairs = [(i, (i + s) % n_dp) for i in range(n_dp)]
-        held.append(tuple(lax.ppermute(a, "dp", pairs) for a in held[0]))
+        gate_up = lax.ppermute(held[0][0], "dp", pairs)
+        down = lax.dynamic_index_in_dim(down_all, (me_dp - s) % n_dp, 0, keepdims=False)
+        held.append((gate_up, down))
     outs = []
     for e in range(local_experts):
         rows = routed[:, e].reshape(sources * slots, width)
@@ -184,8 +188,17 @@
     tok_buffer = place_rows(tok_pick, moe_in).reshape(
         n_expert, local_experts, quarter, model_width
     )
-    got_rows = lax.all_to_all(tok_buffer, "expert", split_axis=0, concat_axis=0, tiled=True)
-    got_kv = lax.all_to_all(kv_buffer, "expert", split_axis=0, concat_axis=0, tiled=True)
+    kv_width = kv_cap * kv_row.shape[1]
+    if kv_width == model_width and local_experts == 1:
+        send = jnp.concatenate(
+            [tok_buffer, kv_buffer.reshape(n_expert, 1, 1, model_width)], axis=2
+        )
+        got = lax.all_to_all(send, "expert", split_axis=0, concat_axis=0, tiled=True)
+        got_rows = got[:, :, :quarter]
+        got_kv = got[:, 0, quarter].reshape(n_expert, kv_cap, kv_row.shape[1])
+    else:
+        got_rows = lax.all_to_all(tok_buffer, "expert", split_axis=0, concat_axis=0, tiled=True)
+        got_kv = lax.all_to_all(kv_buffer, "expert", split_axis=0, concat_axis=0, tiled=True)
     contrib = expert_block(got_rows, w_gate, w_up, w_down)
     returned = lax.all_to_all(
         contrib.astype(jnp.bfloat16), "expert", split_axis=0, concat_axis=0, tiled=True

time: 372 us -> 349 us (0.938)
  waiting for transfers between devices: 232 us -> 206 us
  starting transfers between devices: 40.6 us -> 31.7 us
  other arithmetic: 9.85 us -> 15.6 us
  local copies, waits for them, and re-layouts: 33.1 us -> 37.8 us
    ppermute x6 -> x3, waiting for transfers between devices: 93.9 us -> 41.9 us  [expert_block(): gate_up = lax.ppermute(held[0][0], 'dp', pairs)]
    all_to_all x2 -> x1, waiting for transfers between devices: 25.3 us -> 43.9 us  [local_body(): lax.all_to_all(send, 'expert', split_axis=0, concat_axis=0, tiled=True)]
    ppermute x6, waiting for transfers between devices: 21.5 us -> 30.6 us  [dp_sum(): lax.ppermute(part, 'dp', [(i, (i + s) % n_dp) for i in range(n_dp)])]
    all_to_all x2 -> x1, starting transfers between devices: 13.2 us -> 7.43 us  [local_body(): lax.all_to_all(send, 'expert', split_axis=0, concat_axis=0, tiled=True)]
    all_gather x1, waiting for transfers between devices: 64.7 us -> 60.1 us  [local_body(): lax.all_gather(jnp.stack([w_query, w_key, w_value, w_out]), 'expert', axi...]
    unnamed x38 -> x40, local copies, waits for them, and re-layouts: 14 us -> 16.8 us
  transfers between devices with their start and end apart: 16 -> 13, of which waited for: 12 -> 10; matrix products, arithmetic and copies ran while one was open for 13% -> 19% of each run, Pallas kernels for 0% -> 0%
where the time goes in v3:
time: 349 us; the launch traced here: 347 us
  waiting for transfers between devices  206 us (59%)
  matrix products  41.4 us (12%)
  local copies, waits for them, and re-layouts  37.8 us (11%)
  starting transfers between devices  31.7 us (9%)
  other arithmetic  15.6 us (4%)
  between operations  14.4 us (4%)
    all_gather x1, waiting for transfers between devices, local_body(): lax.all_gather(jnp.stack([w_query, w_key, w_value, w_out]), 'expert', axi...  60.1 us
    all_to_all x1, waiting for transfers between devices, local_body(): lax.all_to_all(send, 'expert', split_axis=0, concat_axis=0, tiled=True)  43.9 us
    ppermute x3, waiting for transfers between devices, expert_block(): gate_up = lax.ppermute(held[0][0], 'dp', pairs)  41.9 us
    ppermute x6, waiting for transfers between devices, dp_sum(): lax.ppermute(part, 'dp', [(i, (i + s) % n_dp) for i in range(n_dp)])  30.6 us
    all_to_all x1, waiting for transfers between devices, local_body(): lax.all_to_all(contrib.astype(jnp.bfloat16), 'expert', split_axis=0, conc...  28.7 us
    unnamed x40, local copies, waits for them, and re-layouts  16.8 us
    dot_general x4, matrix products, expert_block(): part = jnp.dot(active, down[e], preferred_element_type=jnp.float32)  16.6 us
    all_to_all x1, starting transfers between devices, local_body(): lax.all_to_all(contrib.astype(jnp.bfloat16), 'expert', split_axis=0, conc...  10.3 us
  transfers between devices with their start and end apart: 13, of which 10 were waited for; matrix products, arithmetic and copies ran while one was open for 19% of the time, Pallas kernels for 0%

profile of v3, /device:TPU:2, one launch (start us, length us, event | category | flops | bytes accessed | tf_op | source)
XLA Modules:
  0.0 346.8 jit_solution(8637047747414375127)
XLA Ops:
  7.2 1.5 pad_maximum_fusion.2
  8.8 0.7 all-gather.6.cloned.1.call-update
  9.5 0.8 copy.107
  10.2 0.7 bitcast_or_fusion
  10.9 1.1 fusion.50
  12.1 6.5 %copy.100 = bf16[2048,1024]{0,1:T(8,128)(2,1)} copy(bf16[2048,1024]{1,0:T(8,128)(2,1)} %param.23) | data formatting | bytes 8388608 | tf_op args[6]
  18.6 4.0 %fusion.119 = (bf16[2048,1,4,128]{0,3,2,1:T(8,128)(2,1)S(1)}, bf16[2048,1,4,128]{0,3,2,1:T(8,128)(2,1)}) fusion(bf16[2048,2,4,128]{0,3,2,1:T(8,128)(2,1)} %bitcast.168), kind=kLoop, calls=%fused_computation.190 | loop fusion | bytes 8388608 | tf_op jit(solution)/shard_map/slice | solution.py:151
  22.6 3.9 %copy.117 = bf16[2048,1,4,128]{3,0,2,1:T(8,128)(2,1)} copy(bf16[2048,1,4,128]{0,3,2,1:T(8,128)(2,1)} %get-tuple-element.5) | data formatting | bytes 4194304
  26.5 2.5 copy.116
  30.3 0.8 gather_fusion.3
  31.6 3.8 %gather_fusion.2 = s32[512]{0:T(512)S(1)} fusion(s32[64,64]{1,0:T(8,128)S(1)} %sub.59, s32[512]{0:T(512)S(1)} %reshape.322), kind=kCustom, calls=%fused_computation.2 | custom fusion | bytes 8192 | tf_op jit(solution)/shard_map/jit(take_along_axis)/gather | solution.py:25
  35.6 0.2 fusion.59
  35.9 60.1 %all-gather.4.cloned.1.call-done = bf16[4,2048,512]{2,1,0:T(8,128)(2,1)} async-done(((bf16[4,32,512]{2,1,0:T(8,128)(2,1)}), bf16[4,2048,512]{2,1,0:T(8,128)(2,1)}) %all-gather.4.cloned.1.call-update) | async-done | bytes 8388624 | tf_op jit(solution)/shard_map/all_gather | solution.py:132
  96.0 2.1 fusion.24
  98.2 2.3 fusion.32
  100.5 2.4 fusion.120
  102.9 2.3 fusion.25
  105.2 2.2 fusion.29
  107.4 2.6 convolution_convert_fusion.5
  110.0 2.8 collective-permute-start.2
  112.8 0.8 collective-permute-start.1
  113.6 0.9 collective-permute-start
  115.0 10.7 %collective-permute-done.2 = bf16[64,2048]{1,0:T(8,128)(2,1)S(1)} collective-permute-done((bf16[64,2048]{1,0:T(8,128)(2,1)S(1)}, bf16[64,2048]{1,0:T(8,128)(2,1)S(1)}, u32[]{:S(2)}, u32[]{:S(2)}) %collective-permute-start.2) | collective-permute-done | bytes 262176 | tf_op jit(solution)/shard_map/ppermute | solution.py:58
  125.7 3.4 collective-permute-done.1
  129.1 7.8 %collective-permute-done = bf16[64,2048]{1,0:T(8,128)(2,1)S(1)} collective-permute-done((bf16[64,2048]{1,0:T(8,128)(2,1)S(1)}, bf16[64,2048]{1,0:T(8,128)(2,1)S(1)}, u32[]{:S(2)}, u32[]{:S(2)}) %collective-permute-start) | collective-permute-done | bytes 262176 | tf_op jit(solution)/shard_map/ppermute | solution.py:58
  136.9 0.7 copy-done.8
  137.6 1.2 maximum_convert_fusion
  138.8 2.0 gather_fusion
  140.8 1.8 multiply_reduce_fusion.1
  142.6 0.8 copy-done.1
  143.4 0.5 convolution_convert_fusion.4
  143.9 0.4 reshape.303
  144.4 2.4 pad_maximum_fusion
  146.7 7.4 %all-to-all-start = ((bf16[64,1,5,2048]{3,2,1,0:T(8,128)(2,1)}), bf16[64,1,5,2048]{3,2,1,0:T(8,128)(2,1)S(1)}, u32[]{:S(2)}, u32[]{:S(2)}) async-start(bf16[64,1,5,2048]{3,2,1,0:T(8,128)(2,1)} %pad_maximum_fusion), calls=%async_computation | async-start | bytes 4194304 | tf_op jit(solution)/shard_map/all_to_all | solution.py:196
  154.2 2.8 pad_maximum_fusion.1
  157.0 3.7 %collective-permute-start.5 = (bf16[2,1,2048,256]{3,2,1,0:T(8,128)(2,1)}, bf16[2,1,2048,256]{3,2,1,0:T(8,128)(2,1)}, u32[]{:S(2)}, u32[]{:S(2)}) collective-permute-start(bf16[2,1,2048,256]{3,2,1,0:T(8,128)(2,1)} %pad_maximum_fusion.1), channel_id=1, source_target_pairs={{0,192},{64,0},{128,64},{192,128},{1,193},{65,1},{129,65},{193,129... | collective-permute-start | bytes 6291464 | tf_op jit(solution)/shard_map/ppermute | solution.py:87
  160.7 0.8 collective-permute-start.4
  161.6 43.9 %all-to-all-done = bf16[64,1,5,2048]{3,2,1,0:T(8,128)(2,1)S(1)} async-done(((bf16[64,1,5,2048]{3,2,1,0:T(8,128)(2,1)}), bf16[64,1,5,2048]{3,2,1,0:T(8,128)(2,1)S(1)}, u32[]{:S(2)}, u32[]{:S(2)}) %all-to-all-start) | async-done | bytes 1310752 | tf_op jit(solution)/shard_map/all_to_all | solution.py:196
  205.4 1.3 copy-done
  206.8 0.5 slice.106
  207.3 0.3 reshape_squeeze.3
  207.5 1.7 fusion.45
  209.2 41.9 %collective-permute-done.5 = bf16[2,1,2048,256]{3,2,1,0:T(8,128)(2,1)} collective-permute-done((bf16[2,1,2048,256]{3,2,1,0:T(8,128)(2,1)}, bf16[2,1,2048,256]{3,2,1,0:T(8,128)(2,1)}, u32[]{:S(2)}, u32[]{:S(2)}) %collective-permute-start.5) | collective-permute-done | bytes 2097184 | tf_op jit(solution)/shard_map/ppermute | solution.py:87
  251.1 2.4 fusion.33
  253.5 2.4 fusion.35
  255.9 2.4 fusion.37
  258.2 2.9 fusion.11
  261.2 4.3 %fusion.10 = f32[256,2048]{1,0:T(8,128)} fusion(bf16[4,256,2048]{2,1,0:T(8,128)(2,1)} %all-gather.6.cloned.1.call-done, s32[]{:T(128)S(6)} %select_n.114, f32[256,256]{1,0:T(8,128)} %fusion.35, bf16[256,2048]{1,0:T(8,128)(2,1)S(1)} %reshape_squeeze.3, bf16[2,1,2048,256]{3,2,1,0:T(8,128)(2,1)} %collective-permute-done.4), kind=kOutput, calls=%fused_computation.20 | convolution fusion | flops 538312704 | bytes 5505028 | tf_op jit(solution)/shard_map/dot_general | solution.py:98
  265.5 4.3 %fusion.9 = f32[256,2048]{1,0:T(8,128)} fusion(bf16[4,256,2048]{2,1,0:T(8,128)(2,1)} %all-gather.6.cloned.1.call-done, s32[]{:T(128)S(6)} %select_n.112, f32[256,256]{1,0:T(8,128)} %fusion.37, bf16[256,2048]{1,0:T(8,128)(2,1)S(1)} %reshape_squeeze.3, bf16[2,1,2048,256]{3,2,1,0:T(8,128)(2,1)} %collective-permute-done.3), kind=kOutput, calls=%fused_computation.19 | convolution fusion | flops 538312704 | bytes 5505028 | tf_op jit(solution)/shard_map/dot_general | solution.py:98
  269.7 5.1 %fusion.8 = bf16[256,2048]{1,0:T(8,128)(2,1)} fusion(f32[256,2048]{1,0:T(8,128)S(1)} %fusion.11, f32[256,2048]{1,0:T(8,128)} %fusion.10, f32[256,2048]{1,0:T(8,128)} %fusion.9, bf16[256,2048]{1,0:T(8,128)(2,1)S(1)} %reshape_squeeze.3, bf16[1,256,2048]{2,1,0:T(8,128)(2,1)} %param.31, bf16[1,2048,256]{2,1,0:T(8,128)(2,1)} %param.30, f32[256,256]{1,0:T(8,128)S(1)} %fusion.45), kind=kOutput, calls=%fused_computation.18 | convolution fusion | flops 540409856 | bytes 10747904 | tf_op jit(solution)/shard_map/dot_general | solution.py:98
  274.9 2.3 convert_element_type.160
  277.1 10.3 %all-to-all-start.1 = ((bf16[64,1,4,2048]{3,2,1,0:T(4,128)(2,1)}), bf16[64,1,4,2048]{3,2,1,0:T(4,128)(2,1)S(1)}, u32[]{:S(2)}, u32[]{:S(2)}) async-start(bf16[64,1,4,2048]{3,2,1,0:T(4,128)(2,1)} %bitcast.47), calls=%async_computation.1 | async-start | bytes 2097152 | tf_op jit(solution)/shard_map/all_to_all | solution.py:203
  287.5 28.7 %all-to-all-done.1 = bf16[64,1,4,2048]{3,2,1,0:T(4,128)(2,1)S(1)} async-done(((bf16[64,1,4,2048]{3,2,1,0:T(4,128)(2,1)}), bf16[64,1,4,2048]{3,2,1,0:T(4,128)(2,1)S(1)}, u32[]{:S(2)}, u32[]{:S(2)}) %all-to-all-start.1) | async-done | bytes 1048608 | tf_op jit(solution)/shard_map/all_to_all | solution.py:203
  316.2 0.3 reshape.348
  316.5 1.5 multiply_reduce_fusion
  318.0 3.8 %collective-permute-start.8 = (bf16[64,2048]{1,0:T(8,128)(2,1)S(1)}, bf16[64,2048]{1,0:T(8,128)(2,1)S(1)}, u32[]{:S(2)}, u32[]{:S(2)}) collective-permute-start(bf16[64,2048]{1,0:T(8,128)(2,1)S(1)} %multiply_reduce_fusion), channel_id=1, source_target_pairs={{0,192},{64,0},{128,64},{192,128},{1,193},{65,1},{129,65},{193,129... | collective-permute-start | bytes 786440 | tf_op jit(solution)/shard_map/ppermute | solution.py:58
  321.8 1.0 collective-permute-start.6
  322.7 3.2 slice_reduce_fusion
  325.9 0.8 reshape_reshape_squeeze.3
  326.7 5.3 %collective-permute-done.8 = bf16[64,2048]{1,0:T(8,128)(2,1)S(1)} collective-permute-done((bf16[64,2048]{1,0:T(8,128)(2,1)S(1)}, bf16[64,2048]{1,0:T(8,128)(2,1)S(1)}, u32[]{:S(2)}, u32[]{:S(2)}) %collective-permute-start.8) | collective-permute-done | bytes 262176 | tf_op jit(solution)/shard_map/ppermute | solution.py:58
  332.0 0.5 collective-permute-done.7
  332.4 2.9 collective-permute-done.6
  335.6 2.0 gather_fusion.1
  337.6 2.4 fusion.55
  (76 shorter events, 2.8 us)
Async XLA Ops:
  7.2 88.9 %all-gather.4.cloned.1.call-start = ((), (), s32[]{:S(2)}) async-start(), calls=%async_computation.2 | async-start | bytes 8519680 | tf_op jit(solution)/shard_map/all_gather | solution.py:132
  8.7 249.5 %all-gather.6.cloned.1.call-start = ((), (), s32[]{:S(2)}) async-start(), calls=%async_computation.3 | async-start | bytes 5242880 | tf_op jit(solution)/shard_map/all_gather | solution.py:83
  26.5 2.6 copy-start.15
  26.5 2.9 copy-start.16
  26.5 3.1 copy-start.13
  26.5 3.4 copy-start.12
  31.6 4.0 %copy-start.9 = (s32[64,8]{0,1:T(8,128)S(1)}, s32[64,8]{0,1:T(8,128)}, u32[]{:S(2)}) copy-start(s32[64,8]{0,1:T(8,128)} %param.32) | copy-start | bytes 6148
  31.6 64.5 %copy-start.6 = (bf16[64,2048]{1,0:T(8,128)(2,1)S(1)}, bf16[64,2048]{1,0:T(8,128)(2,1)}, u32[]{:S(2)}) copy-start(bf16[64,2048]{1,0:T(8,128)(2,1)} %param.17) | copy-start | bytes 786436
  31.6 64.5 %copy-start.14 = (f32[2048]{0:T(1024)S(1)}, f32[2048]{0:T(1024)}, u32[]{:S(2)}) copy-start(f32[2048]{0:T(1024)} %param.18) | copy-start | bytes 24580
  98.2 2.3 copy-start.5
  102.9 2.3 copy-start.4
  110.0 15.7 %collective-permute-start.2 = (bf16[64,2048]{1,0:T(8,128)(2,1)S(1)}, bf16[64,2048]{1,0:T(8,128)(2,1)S(1)}, u32[]{:S(2)}, u32[]{:S(2)}) collective-permute-start(bf16[64,2048]{1,0:T(8,128)(2,1)S(1)} %convolution_convert_fusion.5), channel_id=1, source_target_pairs={{0,192},{64,0},{128,64},{192,128},{1,193},{65,1},{129,65},{193,129... | collective-permute-start | bytes 786440 | tf_op jit(solution)/shard_map/ppermute | solution.py:58
  112.8 16.3 %collective-permute-start.1 = (bf16[64,2048]{1,0:T(8,128)(2,1)S(1)}, bf16[64,2048]{1,0:T(8,128)(2,1)S(1)}, u32[]{:S(2)}, u32[]{:S(2)}) collective-permute-start(bf16[64,2048]{1,0:T(8,128)(2,1)S(1)} %convolution_convert_fusion.5), channel_id=1, source_target_pairs={{0,128},{64,192},{128,0},{192,64},{1,129},{65,193},{129,1},{193,65... | collective-permute-start | bytes 786440 | tf_op jit(solution)/shard_map/ppermute | solution.py:58
  113.6 23.3 %collective-permute-start = (bf16[64,2048]{1,0:T(8,128)(2,1)S(1)}, bf16[64,2048]{1,0:T(8,128)(2,1)S(1)}, u32[]{:S(2)}, u32[]{:S(2)}) collective-permute-start(bf16[64,2048]{1,0:T(8,128)(2,1)S(1)} %convolution_convert_fusion.5), channel_id=1, source_target_pairs={{0,64},{64,128},{128,192},{192,0},{1,65},{65,129},{129,193},{193,1... | collective-permute-start | bytes 786440 | tf_op jit(solution)/shard_map/ppermute | solution.py:58
  129.1 7.8 %copy-start.7 = (bf16[64,2048]{1,0:T(8,128)(2,1)}, bf16[64,2048]{1,0:T(8,128)(2,1)S(1)}, u32[]{:S(2)}) copy-start(bf16[64,2048]{1,0:T(8,128)(2,1)S(1)} %collective-permute-done.1) | copy-start | bytes 786436
  136.9 0.7 copy-start.8
  140.8 2.6 copy-start.10
  142.6 0.8 copy-start.1
  146.7 7.4 %copy-start.3 = (bf16[1,2048,256]{2,1,0:T(8,128)(2,1)S(1)}, bf16[1,2048,256]{2,1,0:T(8,128)(2,1)}, u32[]{:S(2)}) copy-start(bf16[1,2048,256]{2,1,0:T(8,128)(2,1)} %param.29) | copy-start | bytes 3145732
  146.7 58.7 %all-to-all-start = ((bf16[64,1,5,2048]{3,2,1,0:T(8,128)(2,1)}), bf16[64,1,5,2048]{3,2,1,0:T(8,128)(2,1)S(1)}, u32[]{:S(2)}, u32[]{:S(2)}) async-start(bf16[64,1,5,2048]{3,2,1,0:T(8,128)(2,1)} %pad_maximum_fusion), calls=%async_computation | async-start | bytes 4194304 | tf_op jit(solution)/shard_map/all_to_all | solution.py:196
  157.0 94.2 %collective-permute-start.5 = (bf16[2,1,2048,256]{3,2,1,0:T(8,128)(2,1)}, bf16[2,1,2048,256]{3,2,1,0:T(8,128)(2,1)}, u32[]{:S(2)}, u32[]{:S(2)}) collective-permute-start(bf16[2,1,2048,256]{3,2,1,0:T(8,128)(2,1)} %pad_maximum_fusion.1), channel_id=1, source_target_pairs={{0,192},{64,0},{128,64},{192,128},{1,193},{65,1},{129,65},{193,129... | collective-permute-start | bytes 6291464 | tf_op jit(solution)/shard_map/ppermute | solution.py:87
  160.7 92.8 %collective-permute-start.4 = (bf16[2,1,2048,256]{3,2,1,0:T(8,128)(2,1)}, bf16[2,1,2048,256]{3,2,1,0:T(8,128)(2,1)}, u32[]{:S(2)}, u32[]{:S(2)}) collective-permute-start(bf16[2,1,2048,256]{3,2,1,0:T(8,128)(2,1)} %pad_maximum_fusion.1), channel_id=1, source_target_pairs={{0,128},{64,192},{128,0},{192,64},{1,129},{65,193},{129,1},{193,65... | collective-permute-start | bytes 6291464 | tf_op jit(solution)/shard_map/ppermute | solution.py:87
  161.5 94.4 %collective-permute-start.3 = (bf16[2,1,2048,256]{3,2,1,0:T(8,128)(2,1)}, bf16[2,1,2048,256]{3,2,1,0:T(8,128)(2,1)}, u32[]{:S(2)}, u32[]{:S(2)}) collective-permute-start(bf16[2,1,2048,256]{3,2,1,0:T(8,128)(2,1)} %pad_maximum_fusion.1), channel_id=1, source_target_pairs={{0,64},{64,128},{128,192},{192,0},{1,65},{65,129},{129,193},{193,1... | collective-permute-start | bytes 6291464 | tf_op jit(solution)/shard_map/ppermute | solution.py:87
  205.4 1.4 copy-start
  274.9 12.6 %copy-start.11 = (f32[64,8]{0,1:T(8,128)S(1)}, f32[64,8]{0,1:T(8,128)}, u32[]{:S(2)}) copy-start(f32[64,8]{0,1:T(8,128)} %param.33) | copy-start | bytes 6148
  277.1 39.1 %all-to-all-start.1 = ((bf16[64,1,4,2048]{3,2,1,0:T(4,128)(2,1)}), bf16[64,1,4,2048]{3,2,1,0:T(4,128)(2,1)S(1)}, u32[]{:S(2)}, u32[]{:S(2)}) async-start(bf16[64,1,4,2048]{3,2,1,0:T(4,128)(2,1)} %bitcast.47), calls=%async_computation.1 | async-start | bytes 2097152 | tf_op jit(solution)/shard_map/all_to_all | solution.py:203
  318.0 14.0 %collective-permute-start.8 = (bf16[64,2048]{1,0:T(8,128)(2,1)S(1)}, bf16[64,2048]{1,0:T(8,128)(2,1)S(1)}, u32[]{:S(2)}, u32[]{:S(2)}) collective-permute-start(bf16[64,2048]{1,0:T(8,128)(2,1)S(1)} %multiply_reduce_fusion), channel_id=1, source_target_pairs={{0,192},{64,0},{128,64},{192,128},{1,193},{65,1},{129,65},{193,129... | collective-permute-start | bytes 786440 | tf_op jit(solution)/shard_map/ppermute | solution.py:58
  321.8 10.7 %collective-permute-start.7 = (bf16[64,2048]{1,0:T(8,128)(2,1)S(1)}, bf16[64,2048]{1,0:T(8,128)(2,1)S(1)}, u32[]{:S(2)}, u32[]{:S(2)}) collective-permute-start(bf16[64,2048]{1,0:T(8,128)(2,1)S(1)} %multiply_reduce_fusion), channel_id=1, source_target_pairs={{0,128},{64,192},{128,0},{192,64},{1,129},{65,193},{129,1},{193,65... | collective-permute-start | bytes 786440 | tf_op jit(solution)/shard_map/ppermute | solution.py:58
  321.8 13.6 %collective-permute-start.6 = (bf16[64,2048]{1,0:T(8,128)(2,1)S(1)}, bf16[64,2048]{1,0:T(8,128)(2,1)S(1)}, u32[]{:S(2)}, u32[]{:S(2)}) collective-permute-start(bf16[64,2048]{1,0:T(8,128)(2,1)S(1)} %multiply_reduce_fusion), channel_id=1, source_target_pairs={{0,64},{64,128},{128,192},{192,0},{1,65},{65,129},{129,193},{193,1... | collective-permute-start | bytes 786440 | tf_op jit(solution)/shard_map/ppermute | solution.py:58
  335.6 2.0 copy-start.2
Sparse Core Ops, SparseCore 0:
  11.4 84.6 all-gather.3
  97.8 60.1 all-gather.5

commit v4 on v3

--- a/solution.py
+++ b/solution.py
@@ -79,13 +79,11 @@
 def expert_block(routed, w_gate, w_up, w_down):
     n_dp = lax.axis_size("dp")
     sources, local_experts, slots, width = routed.shape
-    me_dp = lax.axis_index("dp")
-    down_all = lax.all_gather(w_down, "dp", axis=0, tiled=False)
     held = [(jnp.stack([w_gate, w_up]), w_down)]
     for s in range(1, n_dp):
         pairs = [(i, (i + s) % n_dp) for i in range(n_dp)]
         gate_up = lax.ppermute(held[0][0], "dp", pairs)
-        down = lax.dynamic_index_in_dim(down_all, (me_dp - s) % n_dp, 0, keepdims=False)
+        down = lax.ppermute(held[0][1], "dp", pairs)
         held.append((gate_up, down))
     outs = []
     for e in range(local_experts):
@@ -189,11 +187,14 @@
         n_expert, local_experts, quarter, model_width
     )
     kv_width = kv_cap * kv_row.shape[1]
-    if kv_width == model_width and local_experts == 1:
+    if kv_width == model_width and local_experts == 1 and (quarter + 1) * model_width % 2048 == 0:
         send = jnp.concatenate(
             [tok_buffer, kv_buffer.reshape(n_expert, 1, 1, model_width)], axis=2
         )
-        got = lax.all_to_all(send, "expert", split_axis=0, concat_axis=0, tiled=True)
+        flat = (quarter + 1) * model_width
+        got = lax.all_to_all(
+            send.reshape(n_expert, flat // 128, 128), "expert", split_axis=0, concat_axis=0, tiled=True
+        ).reshape(n_expert, 1, quarter + 1, model_width)
         got_rows = got[:, :, :quarter]
         got_kv = got[:, 0, quarter].reshape(n_expert, kv_cap, kv_row.shape[1])
     else:

time: 349 us -> 370 us (1.060)
  waiting for transfers between devices: 206 us -> 222 us
  local copies, waits for them, and re-layouts: 37.8 us -> 42.2 us
    ppermute x0 -> x3, waiting for transfers between devices: none -> 32.9 us  [expert_block(): down = lax.ppermute(held[0][1], 'dp', pairs)]
    all_to_all x1, waiting for transfers between devices: 43.9 us -> 26.6 us  [local_body(): lax.all_to_all(send.reshape(n_expert, flat // 128, 128), 'expert', split_...]
    ppermute x6, waiting for transfers between devices: 30.6 us -> 20.6 us  [dp_sum(): lax.ppermute(part, 'dp', [(i, (i + s) % n_dp) for i in range(n_dp)])]
    ppermute x3, waiting for transfers between devices: 41.9 us -> 51.2 us  [expert_block(): gate_up = lax.ppermute(held[0][0], 'dp', pairs)]
    ppermute x0 -> x3, starting transfers between devices: none -> 4.13 us  [expert_block(): down = lax.ppermute(held[0][1], 'dp', pairs)]
    reshape x0 -> x2, local copies, waits for them, and re-layouts: none -> 3.83 us  [the longest x1 2.42 us: local_body(): send.reshape(n_expert, flat // 128, 128)]
    unnamed x40 -> x46, local copies, waits for them, and re-layouts: 16.8 us -> 16.2 us
  transfers between devices with their start and end apart: 13 -> 15, of which waited for: 10 -> 12; matrix products, arithmetic and copies ran while one was open for 19% -> 14% of each run, Pallas kernels for 0% -> 0%
where the time goes in v4:
time: 370 us; the launch traced here: 368 us
  waiting for transfers between devices  222 us (60%)
  local copies, waits for them, and re-layouts  42.2 us (11%)
  matrix products  40.6 us (11%)
  starting transfers between devices  35.1 us (9%)
  between operations  14.5 us (4%)
  other arithmetic  13 us (4%)
    all_gather x1, waiting for transfers between devices, local_body(): lax.all_gather(jnp.stack([w_query, w_key, w_value, w_out]), 'expert', axi...  62.2 us
    ppermute x3, waiting for transfers between devices, expert_block(): gate_up = lax.ppermute(held[0][0], 'dp', pairs)  51.2 us
    ppermute x3, waiting for transfers between devices, expert_block(): down = lax.ppermute(held[0][1], 'dp', pairs)  32.9 us
    all_to_all x1, waiting for transfers between devices, local_body(): lax.all_to_all(contrib.astype(jnp.bfloat16), 'expert', split_axis=0, conc...  28.7 us
    all_to_all x1, waiting for transfers between devices, local_body(): lax.all_to_all(send.reshape(n_expert, flat // 128, 128), 'expert', split_...  26.6 us
    ppermute x6, waiting for transfers between devices, dp_sum(): lax.ppermute(part, 'dp', [(i, (i + s) % n_dp) for i in range(n_dp)])  20.6 us
    dot_general x4, matrix products, expert_block(): part = jnp.dot(active, down[e], preferred_element_type=jnp.float32)  16.5 us
    unnamed x46, local copies, waits for them, and re-layouts  16.2 us
  transfers between devices with their start and end apart: 15, of which 12 were waited for; matrix products, arithmetic and copies ran while one was open for 14% of the time, Pallas kernels for 0%

profile of v4, /device:TPU:2, one launch (start us, length us, event | category | flops | bytes accessed | tf_op | source)
XLA Modules:
  0.0 367.6 jit_solution(2934744610634595916)
XLA Ops:
  7.2 1.5 pad_maximum_fusion.2
  8.7 6.5 %copy.97 = bf16[2048,1024]{0,1:T(8,128)(2,1)} copy(bf16[2048,1024]{1,0:T(8,128)(2,1)} %param.23) | data formatting | bytes 8388608 | tf_op args[6]
  15.2 4.0 %fusion.113 = (bf16[2048,1,4,128]{0,3,2,1:T(8,128)(2,1)S(1)}, bf16[2048,1,4,128]{0,3,2,1:T(8,128)(2,1)}) fusion(bf16[2048,2,4,128]{0,3,2,1:T(8,128)(2,1)} %bitcast.171), kind=kLoop, calls=%fused_computation.184 | loop fusion | bytes 8388608 | tf_op jit(solution)/shard_map/slice | solution.py:149
  19.2 3.9 %copy.113 = bf16[2048,1,4,128]{3,0,2,1:T(8,128)(2,1)} copy(bf16[2048,1,4,128]{0,3,2,1:T(8,128)(2,1)} %get-tuple-element.5) | data formatting | bytes 4194304
  23.1 2.5 copy.112
  26.6 3.8 %gather_fusion.2 = s32[512]{0:T(512)S(1)} fusion(s32[64,64]{1,0:T(8,128)S(1)} %sub.50, s32[512]{0:T(512)S(1)} %reshape.327), kind=kCustom, calls=%fused_computation.2 | custom fusion | bytes 8192 | tf_op jit(solution)/shard_map/jit(take_along_axis)/gather | solution.py:25
  30.8 0.8 gather_fusion.3
  31.6 0.5 fusion.97
  32.9 0.6 bitcast_add_fusion
  33.9 62.2 %all-gather.2.cloned.1.call-done = bf16[4,2048,512]{2,1,0:T(8,128)(2,1)} async-done(((bf16[4,32,512]{2,1,0:T(8,128)(2,1)}), bf16[4,2048,512]{2,1,0:T(8,128)(2,1)}) %all-gather.2.cloned.1.call-update) | async-done | bytes 8388624 | tf_op jit(solution)/shard_map/all_gather | solution.py:130
  96.0 2.1 fusion.25
  98.2 2.1 fusion.24
  100.3 2.1 fusion.32
  102.5 4.2 %fusion.114 = (f32[4,64]{1,0:T(4,128)S(1)}, f32[4,64,2112]{2,1,0:T(8,128)}) fusion(bf16[64,4,128]{2,0,1:T(8,128)(2,1)S(1)} %copy_bitcast_fusion.1, bf16[2048,4,128]{2,0,1:T(8,128)(2,1)} %bitcast.175, pred[64,2112]{1,0:T(8,128)(4,1)S(1)} %pad_add_fusion, bf16[8,4,8,128]{3,2,1,0:T(8,128)(2,1)S(1)} %fusion.32), kind=kOutput, calls=%fused_computation.185 | convolution fusion | flops 144902208 | bytes 4527104 | tf_op jit(solution)/shard_map/sub | solution.py:163
  106.7 2.2 fusion.29
  108.9 2.3 convolution_convert_fusion.5
  111.2 2.8 collective-permute-start.2
  114.0 0.8 collective-permute-start.1
  114.8 0.9 collective-permute-start
  115.7 0.6 pad_clamp_fusion
  116.5 0.9 reshape_reshape.4
  117.5 8.2 %collective-permute-done.2 = bf16[64,2048]{1,0:T(8,128)(2,1)S(1)} collective-permute-done((bf16[64,2048]{1,0:T(8,128)(2,1)S(1)}, bf16[64,2048]{1,0:T(8,128)(2,1)S(1)}, u32[]{:S(2)}, u32[]{:S(2)}) %collective-permute-start.2) | collective-permute-done | bytes 262176 | tf_op jit(solution)/shard_map/ppermute | solution.py:58
  125.7 3.7 collective-permute-done
  129.5 2.1 gather_fusion
  131.7 1.8 multiply_reduce_fusion.1
  133.4 0.8 copy-done.1
  134.2 0.5 convolution_convert_fusion.4
  135.2 2.1 pad_maximum_fusion
  137.2 2.4 reshape.308
  139.6 7.5 %all-to-all-start = ((bf16[64,80,128]{2,1,0:T(8,128)(2,1)}), bf16[64,80,128]{2,1,0:T(8,128)(2,1)S(1)}, u32[]{:S(2)}, u32[]{:S(2)}) async-start(bf16[64,80,128]{2,1,0:T(8,128)(2,1)} %reshape.308), calls=%async_computation | async-start | bytes 2621440 | tf_op jit(solution)/shard_map/all_to_all | solution.py:195
  147.2 1.6 pad_maximum_fusion.1
  148.7 0.6 collective-permute-start.7
  149.3 0.8 collective-permute-start.5
  150.1 0.8 collective-permute-start.3
  150.9 2.5 collective-permute-start.8
  153.4 1.5 collective-permute-start.6
  154.9 26.6 %all-to-all-done = bf16[64,80,128]{2,1,0:T(8,128)(2,1)S(1)} async-done(((bf16[64,80,128]{2,1,0:T(8,128)(2,1)}), bf16[64,80,128]{2,1,0:T(8,128)(2,1)S(1)}, u32[]{:S(2)}, u32[]{:S(2)}) %all-to-all-start) | async-done | bytes 1310752 | tf_op jit(solution)/shard_map/all_to_all | solution.py:195
  181.5 1.4 reshape.309
  182.9 1.3 copy-done
  184.3 0.5 slice.106
  185.1 0.9 copy-done.4
  186.4 2.8 fusion.4
  189.3 8.3 %collective-permute-done.7 = bf16[2,1,2048,256]{3,2,1,0:T(8,128)(2,1)} collective-permute-done((bf16[2,1,2048,256]{3,2,1,0:T(8,128)(2,1)}, bf16[2,1,2048,256]{3,2,1,0:T(8,128)(2,1)}, u32[]{:S(2)}, u32[]{:S(2)}) %collective-permute-start.7) | collective-permute-done | bytes 2097184 | tf_op jit(solution)/shard_map/ppermute | solution.py:85
  197.7 2.4 fusion.33
  200.1 1.7 fusion.35
  201.7 43.0 %collective-permute-done.3 = bf16[2,1,2048,256]{3,2,1,0:T(8,128)(2,1)} collective-permute-done((bf16[2,1,2048,256]{3,2,1,0:T(8,128)(2,1)}, bf16[2,1,2048,256]{3,2,1,0:T(8,128)(2,1)}, u32[]{:S(2)}, u32[]{:S(2)}) %collective-permute-start.3) | collective-permute-done | bytes 2097184 | tf_op jit(solution)/shard_map/ppermute | solution.py:85
  244.7 2.4 fusion.37
  247.0 17.9 %collective-permute-done.8 = bf16[1,256,2048]{2,1,0:T(8,128)(2,1)} collective-permute-done((bf16[1,256,2048]{2,1,0:T(8,128)(2,1)}, bf16[1,256,2048]{2,1,0:T(8,128)(2,1)}, u32[]{:S(2)}, u32[]{:S(2)}) %collective-permute-start.8) | collective-permute-done | bytes 1048608 | tf_op jit(solution)/shard_map/ppermute | solution.py:86
  265.0 4.3 %fusion.11 = f32[256,2048]{1,0:T(8,128)} fusion(bf16[1,256,2048]{2,1,0:T(8,128)(2,1)} %collective-permute-done.8, f32[256,256]{1,0:T(8,128)} %fusion.33, bf16[256,2048]{1,0:T(8,128)(2,1)S(1)} %reshape_squeeze.3, bf16[2,1,2048,256]{3,2,1,0:T(8,128)(2,1)} %collective-permute-done.7), kind=kOutput, calls=%fused_computation.21 | convolution fusion | flops 538312704 | bytes 5505024 | tf_op jit(solution)/shard_map/dot_general | solution.py:96
  269.3 4.2 %fusion.10 = f32[256,2048]{1,0:T(8,128)} fusion(bf16[1,256,2048]{2,1,0:T(8,128)(2,1)} %collective-permute-done.6, f32[256,256]{1,0:T(8,128)S(1)} %fusion.35, bf16[256,2048]{1,0:T(8,128)(2,1)S(1)} %reshape_squeeze.3, bf16[2,1,2048,256]{3,2,1,0:T(8,128)(2,1)} %collective-permute-done.5), kind=kOutput, calls=%fused_computation.20 | convolution fusion | flops 538312704 | bytes 5505024 | tf_op jit(solution)/shard_map/dot_general | solution.py:96
  273.5 14.9 %collective-permute-done.4 = bf16[1,256,2048]{2,1,0:T(8,128)(2,1)} collective-permute-done((bf16[1,256,2048]{2,1,0:T(8,128)(2,1)}, bf16[1,256,2048]{2,1,0:T(8,128)(2,1)}, u32[]{:S(2)}, u32[]{:S(2)}) %collective-permute-start.4) | collective-permute-done | bytes 1048608 | tf_op jit(solution)/shard_map/ppermute | solution.py:86
  288.4 5.2 %fusion.9 = bf16[256,2048]{1,0:T(8,128)(2,1)} fusion(f32[256,2048]{1,0:T(8,128)} %fusion.11, f32[256,2048]{1,0:T(8,128)} %fusion.10, f32[256,2048]{1,0:T(8,128)S(1)} %fusion.4, bf16[1,256,2048]{2,1,0:T(8,128)(2,1)} %collective-permute-done.4, f32[256,256]{1,0:T(8,128)} %fusion.37, bf16[256,2048]{1,0:T(8,128)(2,1)S(1)} %reshape_squeeze.3, ...), kind=kOutput, calls=%fused_computation.19 | convolution fusion | flops 540409856 | bytes 10747904 | tf_op jit(solution)/shard_map/dot_general | solution.py:96
  293.6 2.3 convert_element_type.160
  295.9 10.7 %all-to-all-start.1 = ((bf16[64,1,4,2048]{3,2,1,0:T(4,128)(2,1)}), bf16[64,1,4,2048]{3,2,1,0:T(4,128)(2,1)S(1)}, u32[]{:S(2)}, u32[]{:S(2)}) async-start(bf16[64,1,4,2048]{3,2,1,0:T(4,128)(2,1)} %bitcast.46), calls=%async_computation.1 | async-start | bytes 2097152 | tf_op jit(solution)/shard_map/all_to_all | solution.py:204
  306.6 28.7 %all-to-all-done.1 = bf16[64,1,4,2048]{3,2,1,0:T(4,128)(2,1)S(1)} async-done(((bf16[64,1,4,2048]{3,2,1,0:T(4,128)(2,1)}), bf16[64,1,4,2048]{3,2,1,0:T(4,128)(2,1)S(1)}, u32[]{:S(2)}, u32[]{:S(2)}) %all-to-all-start.1) | async-done | bytes 1048608 | tf_op jit(solution)/shard_map/all_to_all | solution.py:204
  335.6 1.5 multiply_reduce_fusion
  337.1 5.1 %collective-permute-start.11 = (bf16[64,2048]{1,0:T(8,128)(2,1)S(1)}, bf16[64,2048]{1,0:T(8,128)(2,1)S(1)}, u32[]{:S(2)}, u32[]{:S(2)}) collective-permute-start(bf16[64,2048]{1,0:T(8,128)(2,1)S(1)} %multiply_reduce_fusion), channel_id=1, source_target_pairs={{0,192},{64,0},{128,64},{192,128},{1,193},{65,1},{129,65},{193,129... | collective-permute-start | bytes 786440 | tf_op jit(solution)/shard_map/ppermute | solution.py:58
  342.3 1.0 collective-permute-start.9
  343.2 3.2 slice_reduce_fusion
  346.4 0.8 reshape_reshape_squeeze.3
  347.2 5.3 %collective-permute-done.11 = bf16[64,2048]{1,0:T(8,128)(2,1)S(1)} collective-permute-done((bf16[64,2048]{1,0:T(8,128)(2,1)S(1)}, bf16[64,2048]{1,0:T(8,128)(2,1)S(1)}, u32[]{:S(2)}, u32[]{:S(2)}) %collective-permute-start.11) | collective-permute-done | bytes 262176 | tf_op jit(solution)/shard_map/ppermute | solution.py:58
  352.9 2.9 collective-permute-done.9
  356.1 2.3 gather_fusion.1
  358.4 2.4 fusion.52
  (87 shorter events, 5.2 us)
Async XLA Ops:
  7.2 88.9 %all-gather.2.cloned.1.call-start = ((), (), s32[]{:S(2)}) async-start(), calls=%async_computation.2 | async-start | bytes 8519680 | tf_op jit(solution)/shard_map/all_gather | solution.py:130
  23.1 2.6 copy-start.18
  23.1 2.7 copy-start.13
  23.1 2.9 copy-start.10
  26.6 5.6 %copy-start.19 = (s32[1,16]{1,0:T(1,128)S(1)}, s32[1,16]{1,0:T(1,128)}, u32[]{:S(2)}) copy-start(s32[1,16]{1,0:T(1,128)} %param.24) | copy-start | bytes 196
  26.6 5.8 %copy-start.15 = (s32[1,4]{1,0:T(1,128)S(1)}, s32[1,4]{1,0:T(1,128)}, u32[]{:S(2)}) copy-start(s32[1,4]{1,0:T(1,128)} %param.25) | copy-start | bytes 52
  26.6 6.1 %copy-start.7 = (bf16[64,2048]{1,0:T(8,128)(2,1)S(1)}, bf16[64,2048]{1,0:T(8,128)(2,1)}, u32[]{:S(2)}) copy-start(bf16[64,2048]{1,0:T(8,128)(2,1)} %param.17) | copy-start | bytes 786436
  26.6 69.4 %copy-start.17 = (f32[2048]{0:T(1024)S(1)}, f32[2048]{0:T(1024)}, u32[]{:S(2)}) copy-start(f32[2048]{0:T(1024)} %param.18) | copy-start | bytes 24580
  30.7 67.5 %copy-start.8 = (s32[64,8]{1,0:T(8,128)}, s32[64,8]{1,0:T(8,128)S(1)}, u32[]{:S(2)}) copy-start(s32[64,8]{1,0:T(8,128)S(1)} %copy.107) | copy-start | bytes 6148
  102.5 4.2 %copy-start.6 = (bf16[2048,1,4,128]{3,0,2,1:T(8,128)(2,1)S(1)}, bf16[2048,1,4,128]{3,0,2,1:T(8,128)(2,1)}, u32[]{:S(2)}) copy-start(bf16[2048,1,4,128]{3,0,2,1:T(8,128)(2,1)} %copy.113) | copy-start | bytes 6291460
  108.8 6.9 %copy-start.16 = (s32[4]{0:T(128)S(1)}, s32[4]{0:T(128)}, u32[]{:S(2)}) copy-start(s32[4]{0:T(128)} %fusion.97) | copy-start | bytes 52
  108.8 7.5 %copy-start.14 = (s32[64]{0:T(128)S(1)}, s32[64]{0:T(128)}, u32[]{:S(2)}) copy-start(s32[64]{0:T(128)} %bitcast_add_fusion) | copy-start | bytes 772
  111.2 14.4 %collective-permute-start.2 = (bf16[64,2048]{1,0:T(8,128)(2,1)S(1)}, bf16[64,2048]{1,0:T(8,128)(2,1)S(1)}, u32[]{:S(2)}, u32[]{:S(2)}) collective-permute-start(bf16[64,2048]{1,0:T(8,128)(2,1)S(1)} %convolution_convert_fusion.5), channel_id=1, source_target_pairs={{0,192},{64,0},{128,64},{192,128},{1,193},{65,1},{129,65},{193,129... | collective-permute-start | bytes 786440 | tf_op jit(solution)/shard_map/ppermute | solution.py:58
  114.0 11.6 %collective-permute-start.1 = (bf16[64,2048]{1,0:T(8,128)(2,1)S(1)}, bf16[64,2048]{1,0:T(8,128)(2,1)S(1)}, u32[]{:S(2)}, u32[]{:S(2)}) collective-permute-start(bf16[64,2048]{1,0:T(8,128)(2,1)S(1)} %convolution_convert_fusion.5), channel_id=1, source_target_pairs={{0,128},{64,192},{128,0},{192,64},{1,129},{65,193},{129,1},{193,65... | collective-permute-start | bytes 786440 | tf_op jit(solution)/shard_map/ppermute | solution.py:58
  114.8 14.5 %collective-permute-start = (bf16[64,2048]{1,0:T(8,128)(2,1)S(1)}, bf16[64,2048]{1,0:T(8,128)(2,1)S(1)}, u32[]{:S(2)}, u32[]{:S(2)}) collective-permute-start(bf16[64,2048]{1,0:T(8,128)(2,1)S(1)} %convolution_convert_fusion.5), channel_id=1, source_target_pairs={{0,64},{64,128},{128,192},{192,0},{1,65},{65,129},{129,193},{193,1... | collective-permute-start | bytes 786440 | tf_op jit(solution)/shard_map/ppermute | solution.py:58
  131.6 2.6 copy-start.11
  133.4 0.8 copy-start.1
  139.6 7.5 %copy-start.3 = (bf16[1,2048,256]{2,1,0:T(8,128)(2,1)S(1)}, bf16[1,2048,256]{2,1,0:T(8,128)(2,1)}, u32[]{:S(2)}) copy-start(bf16[1,2048,256]{2,1,0:T(8,128)(2,1)} %param.29) | copy-start | bytes 3145732
  139.6 7.5 %copy-start.5 = (bf16[1,2048,256]{2,1,0:T(8,128)(2,1)S(1)}, bf16[1,2048,256]{2,1,0:T(8,128)(2,1)}, u32[]{:S(2)}) copy-start(bf16[1,2048,256]{2,1,0:T(8,128)(2,1)} %param.30) | copy-start | bytes 3145732
  139.6 41.9 %all-to-all-start = ((bf16[64,80,128]{2,1,0:T(8,128)(2,1)}), bf16[64,80,128]{2,1,0:T(8,128)(2,1)S(1)}, u32[]{:S(2)}, u32[]{:S(2)}) async-start(bf16[64,80,128]{2,1,0:T(8,128)(2,1)} %reshape.308), calls=%async_computation | async-start | bytes 2621440 | tf_op jit(solution)/shard_map/all_to_all | solution.py:195
  148.7 48.8 %collective-permute-start.7 = (bf16[2,1,2048,256]{3,2,1,0:T(8,128)(2,1)}, bf16[2,1,2048,256]{3,2,1,0:T(8,128)(2,1)}, u32[]{:S(2)}, u32[]{:S(2)}) collective-permute-start(bf16[2,1,2048,256]{3,2,1,0:T(8,128)(2,1)} %pad_maximum_fusion.1), channel_id=1, source_target_pairs={{0,192},{64,0},{128,64},{192,128},{1,193},{65,1},{129,65},{193,129... | collective-permute-start | bytes 6291464 | tf_op jit(solution)/shard_map/ppermute | solution.py:85
  149.3 50.7 %collective-permute-start.5 = (bf16[2,1,2048,256]{3,2,1,0:T(8,128)(2,1)}, bf16[2,1,2048,256]{3,2,1,0:T(8,128)(2,1)}, u32[]{:S(2)}, u32[]{:S(2)}) collective-permute-start(bf16[2,1,2048,256]{3,2,1,0:T(8,128)(2,1)} %pad_maximum_fusion.1), channel_id=1, source_target_pairs={{0,128},{64,192},{128,0},{192,64},{1,129},{65,193},{129,1},{193,65... | collective-permute-start | bytes 6291464 | tf_op jit(solution)/shard_map/ppermute | solution.py:85
  150.1 94.6 %collective-permute-start.3 = (bf16[2,1,2048,256]{3,2,1,0:T(8,128)(2,1)}, bf16[2,1,2048,256]{3,2,1,0:T(8,128)(2,1)}, u32[]{:S(2)}, u32[]{:S(2)}) collective-permute-start(bf16[2,1,2048,256]{3,2,1,0:T(8,128)(2,1)} %pad_maximum_fusion.1), channel_id=1, source_target_pairs={{0,64},{64,128},{128,192},{192,0},{1,65},{65,129},{129,193},{193,1... | collective-permute-start | bytes 6291464 | tf_op jit(solution)/shard_map/ppermute | solution.py:85
  150.9 114.1 %collective-permute-start.8 = (bf16[1,256,2048]{2,1,0:T(8,128)(2,1)}, bf16[1,256,2048]{2,1,0:T(8,128)(2,1)}, u32[]{:S(2)}, u32[]{:S(2)}) collective-permute-start(bf16[1,256,2048]{2,1,0:T(8,128)(2,1)} %param.31), channel_id=1, source_target_pairs={{0,192},{64,0},{128,64},{192,128},{1,193},{65,1},{129,65},{193,129... | collective-permute-start | bytes 3145736 | tf_op jit(solution)/shard_map/ppermute | solution.py:86
  153.4 115.9 %collective-permute-start.6 = (bf16[1,256,2048]{2,1,0:T(8,128)(2,1)}, bf16[1,256,2048]{2,1,0:T(8,128)(2,1)}, u32[]{:S(2)}, u32[]{:S(2)}) collective-permute-start(bf16[1,256,2048]{2,1,0:T(8,128)(2,1)} %param.31), channel_id=1, source_target_pairs={{0,128},{64,192},{128,0},{192,64},{1,129},{65,193},{129,1},{193,65... | collective-permute-start | bytes 3145736 | tf_op jit(solution)/shard_map/ppermute | solution.py:86
  182.9 1.3 copy-start
  184.8 1.2 copy-start.4
  197.5 90.9 %collective-permute-start.4 = (bf16[1,256,2048]{2,1,0:T(8,128)(2,1)}, bf16[1,256,2048]{2,1,0:T(8,128)(2,1)}, u32[]{:S(2)}, u32[]{:S(2)}) collective-permute-start(bf16[1,256,2048]{2,1,0:T(8,128)(2,1)} %param.31), channel_id=1, source_target_pairs={{0,64},{64,128},{128,192},{192,0},{1,65},{65,129},{129,193},{193,1... | collective-permute-start | bytes 3145736 | tf_op jit(solution)/shard_map/ppermute | solution.py:86
  293.6 12.9 %copy-start.12 = (f32[64,8]{0,1:T(8,128)S(1)}, f32[64,8]{0,1:T(8,128)}, u32[]{:S(2)}) copy-start(f32[64,8]{0,1:T(8,128)} %param.33) | copy-start | bytes 6148
  295.9 39.7 %copy-start.9 = (s32[64,8]{1,0:T(8,128)S(1)}, s32[64,8]{1,0:T(8,128)}, u32[]{:S(2)}) copy-start(s32[64,8]{1,0:T(8,128)} %copy-done.8) | copy-start | bytes 6148
  295.9 39.4 %all-to-all-start.1 = ((bf16[64,1,4,2048]{3,2,1,0:T(4,128)(2,1)}), bf16[64,1,4,2048]{3,2,1,0:T(4,128)(2,1)S(1)}, u32[]{:S(2)}, u32[]{:S(2)}) async-start(bf16[64,1,4,2048]{3,2,1,0:T(4,128)(2,1)} %bitcast.46), calls=%async_computation.1 | async-start | bytes 2097152 | tf_op jit(solution)/shard_map/all_to_all | solution.py:204
  337.1 15.4 %collective-permute-start.11 = (bf16[64,2048]{1,0:T(8,128)(2,1)S(1)}, bf16[64,2048]{1,0:T(8,128)(2,1)S(1)}, u32[]{:S(2)}, u32[]{:S(2)}) collective-permute-start(bf16[64,2048]{1,0:T(8,128)(2,1)S(1)} %multiply_reduce_fusion), channel_id=1, source_target_pairs={{0,192},{64,0},{128,64},{192,128},{1,193},{65,1},{129,65},{193,129... | collective-permute-start | bytes 786440 | tf_op jit(solution)/shard_map/ppermute | solution.py:58
  342.3 10.7 %collective-permute-start.10 = (bf16[64,2048]{1,0:T(8,128)(2,1)S(1)}, bf16[64,2048]{1,0:T(8,128)(2,1)S(1)}, u32[]{:S(2)}, u32[]{:S(2)}) collective-permute-start(bf16[64,2048]{1,0:T(8,128)(2,1)S(1)} %multiply_reduce_fusion), channel_id=1, source_target_pairs={{0,128},{64,192},{128,0},{192,64},{1,129},{65,193},{129,1},{193,65... | collective-permute-start | bytes 786440 | tf_op jit(solution)/shard_map/ppermute | solution.py:58
  342.3 13.6 %collective-permute-start.9 = (bf16[64,2048]{1,0:T(8,128)(2,1)S(1)}, bf16[64,2048]{1,0:T(8,128)(2,1)S(1)}, u32[]{:S(2)}, u32[]{:S(2)}) collective-permute-start(bf16[64,2048]{1,0:T(8,128)(2,1)S(1)} %multiply_reduce_fusion), channel_id=1, source_target_pairs={{0,64},{64,128},{128,192},{192,0},{1,65},{65,129},{129,193},{193,1... | collective-permute-start | bytes 786440 | tf_op jit(solution)/shard_map/ppermute | solution.py:58
  356.1 2.3 copy-start.2
Sparse Core Ops, SparseCore 0:
  11.4 84.6 all-gather.1

commit v5 on v3

--- a/solution.py
+++ b/solution.py
@@ -58,12 +58,10 @@
         lax.ppermute(part, "dp", [(i, (i + s) % n_dp) for i in range(n_dp)])
         for s in range(1, n_dp)
     ]
-    held = jnp.stack(held).astype(jnp.float32)
-    order = (me - jnp.arange(n_dp, dtype=jnp.int32)) % n_dp
-    ordered = held[order]
-    total = ordered[0]
-    for j in range(1, n_dp):
-        total = total + ordered[j]
+    total = None
+    for j in range(n_dp):
+        term = lax.select_n((me - j) % n_dp, *held).astype(jnp.float32)
+        total = term if total is None else total + term
     return total
 
 
@@ -79,13 +77,11 @@
 def expert_block(routed, w_gate, w_up, w_down):
     n_dp = lax.axis_size("dp")
     sources, local_experts, slots, width = routed.shape
-    me_dp = lax.axis_index("dp")
-    down_all = lax.all_gather(w_down, "dp", axis=0, tiled=False)
     held = [(jnp.stack([w_gate, w_up]), w_down)]
     for s in range(1, n_dp):
         pairs = [(i, (i + s) % n_dp) for i in range(n_dp)]
         gate_up = lax.ppermute(held[0][0], "dp", pairs)
-        down = lax.dynamic_index_in_dim(down_all, (me_dp - s) % n_dp, 0, keepdims=False)
+        down = lax.ppermute(held[0][1], "dp", pairs)
         held.append((gate_up, down))
     outs = []
     for e in range(local_experts):
@@ -189,13 +185,14 @@
         n_expert, local_experts, quarter, model_width
     )
     kv_width = kv_cap * kv_row.shape[1]
-    if kv_width == model_width and local_experts == 1:
+    extra = kv_width // quarter
+    if local_experts == 1 and kv_width % quarter == 0 and extra % 128 == 0:
         send = jnp.concatenate(
-            [tok_buffer, kv_buffer.reshape(n_expert, 1, 1, model_width)], axis=2
+            [tok_buffer, kv_buffer.reshape(n_expert, 1, quarter, extra)], axis=3
         )
         got = lax.all_to_all(send, "expert", split_axis=0, concat_axis=0, tiled=True)
-        got_rows = got[:, :, :quarter]
-        got_kv = got[:, 0, quarter].reshape(n_expert, kv_cap, kv_row.shape[1])
+        got_rows = got[:, :, :, :model_width]
+        got_kv = got[:, :, :, model_width:].reshape(n_expert, kv_cap, kv_row.shape[1])
     else:
         got_rows = lax.all_to_all(tok_buffer, "expert", split_axis=0, concat_axis=0, tiled=True)
         got_kv = lax.all_to_all(kv_buffer, "expert", split_axis=0, concat_axis=0, tiled=True)

time: 349 us -> 359 us (1.029)
  waiting for transfers between devices: 206 us -> 229 us
  local copies, waits for them, and re-layouts: 37.8 us -> 29.8 us
  other arithmetic: 15.6 us -> 7.97 us
  starting transfers between devices: 31.7 us -> 35.7 us
    ppermute x0 -> x3, waiting for transfers between devices: none -> 37.7 us  [expert_block(): down = lax.ppermute(held[0][1], 'dp', pairs)]
    all_to_all x1, waiting for transfers between devices: 43.9 us -> 24.6 us  [local_body(): lax.all_to_all(send, 'expert', split_axis=0, concat_axis=0, tiled=True)]
    ppermute x3, waiting for transfers between devices: 41.9 us -> 55.1 us  [expert_block(): gate_up = lax.ppermute(held[0][0], 'dp', pairs)]
    ppermute x6, waiting for transfers between devices: 30.6 us -> 19.1 us  [dp_sum(): lax.ppermute(part, 'dp', [(i, (i + s) % n_dp) for i in range(n_dp)])]
    gather x2 -> x0, local copies, waits for them, and re-layouts: 4.07 us -> none  [dp_sum(): ordered = held[order]]
    ppermute x0 -> x3, starting transfers between devices: none -> 3.87 us  [expert_block(): down = lax.ppermute(held[0][1], 'dp', pairs)]
    unnamed x40 -> x38, local copies, waits for them, and re-layouts: 16.8 us -> 15.1 us
  transfers between devices with their start and end apart: 13 -> 15, of which waited for: 10 -> 10; matrix products, arithmetic and copies ran while one was open for 19% -> 13% of each run, Pallas kernels for 0% -> 0%
where the time goes in v5:
time: 359 us; the launch traced here: 358 us
  waiting for transfers between devices  229 us (64%)
  matrix products  41.4 us (12%)
  starting transfers between devices  35.7 us (10%)
  local copies, waits for them, and re-layouts  29.8 us (8%)
  between operations  14.5 us (4%)
  other arithmetic  7.97 us (2%)
    all_gather x1, waiting for transfers between devices, local_body(): lax.all_gather(jnp.stack([w_query, w_key, w_value, w_out]), 'expert', axi...  63.5 us
    ppermute x3, waiting for transfers between devices, expert_block(): gate_up = lax.ppermute(held[0][0], 'dp', pairs)  55.1 us
    ppermute x3, waiting for transfers between devices, expert_block(): down = lax.ppermute(held[0][1], 'dp', pairs)  37.7 us
    all_to_all x1, waiting for transfers between devices, local_body(): lax.all_to_all(contrib.astype(jnp.bfloat16), 'expert', split_axis=0, conc...  28.7 us
    all_to_all x1, waiting for transfers between devices, local_body(): lax.all_to_all(send, 'expert', split_axis=0, concat_axis=0, tiled=True)  24.6 us
    ppermute x6, waiting for transfers between devices, dp_sum(): lax.ppermute(part, 'dp', [(i, (i + s) % n_dp) for i in range(n_dp)])  19.1 us
    dot_general x4, matrix products, expert_block(): part = jnp.dot(active, down[e], preferred_element_type=jnp.float32)  16.6 us
    unnamed x38, local copies, waits for them, and re-layouts  15.1 us
  transfers between devices with their start and end apart: 15, of which 10 were waited for; matrix products, arithmetic and copies ran while one was open for 13% of the time, Pallas kernels for 0%

profile of v5, /device:TPU:2, one launch (start us, length us, event | category | flops | bytes accessed | tf_op | source)
XLA Modules:
  0.0 358.0 jit_solution(8005510522316782632)
XLA Ops:
  7.2 1.5 pad_maximum_fusion.2
  8.7 6.5 %copy.80 = bf16[2048,1024]{0,1:T(8,128)(2,1)} copy(bf16[2048,1024]{1,0:T(8,128)(2,1)} %param.23) | data formatting | bytes 8388608 | tf_op args[6]
  15.2 4.0 %fusion.107 = (bf16[2048,1,4,128]{0,3,2,1:T(8,128)(2,1)S(1)}, bf16[2048,1,4,128]{0,3,2,1:T(8,128)(2,1)}) fusion(bf16[2048,2,4,128]{0,3,2,1:T(8,128)(2,1)} %bitcast.148), kind=kLoop, calls=%fused_computation.163 | loop fusion | bytes 8388608 | tf_op jit(solution)/shard_map/slice | solution.py:147
  19.2 4.0 %copy.97 = bf16[2048,1,4,128]{3,0,2,1:T(8,128)(2,1)} copy(bf16[2048,1,4,128]{0,3,2,1:T(8,128)(2,1)} %get-tuple-element.5) | data formatting | bytes 4194304
  23.2 2.5 copy.96
  25.7 0.2 reduce-window.8
  26.1 0.2 convert_reduce_fusion
  26.6 3.8 %gather_fusion = s32[512]{0:T(512)S(1)} fusion(s32[64,64]{1,0:T(8,128)S(1)} %sub.48, s32[512]{0:T(512)S(1)} %reshape.240), kind=kCustom, calls=%fused_computation | custom fusion | bytes 8192 | tf_op jit(solution)/shard_map/jit(take_along_axis)/gather | solution.py:25
  30.8 0.8 gather_fusion.1
  32.0 0.2 fusion.47
  32.3 0.2 compare_and_fusion
  32.5 63.5 %all-gather.2.cloned.1.call-done = bf16[4,2048,512]{2,1,0:T(8,128)(2,1)} async-done(((bf16[4,32,512]{2,1,0:T(8,128)(2,1)}), bf16[4,2048,512]{2,1,0:T(8,128)(2,1)}) %all-gather.2.cloned.1.call-update) | async-done | bytes 8388624 | tf_op jit(solution)/shard_map/all_gather | solution.py:128
  96.0 2.1 fusion.25
  98.2 2.1 fusion.24
  100.3 2.1 fusion.32
  102.4 4.2 %fusion.108 = (f32[4,64]{1,0:T(4,128)S(1)}, f32[4,64,2112]{2,1,0:T(8,128)}) fusion(bf16[64,4,128]{2,0,1:T(8,128)(2,1)S(1)} %copy_bitcast_fusion.1, bf16[2048,4,128]{2,0,1:T(8,128)(2,1)} %bitcast.153, pred[64,2112]{1,0:T(8,128)(4,1)S(1)} %pad_add_fusion, bf16[8,4,8,128]{3,2,1,0:T(8,128)(2,1)S(1)} %fusion.32), kind=kOutput, calls=%fused_computation.164 | convolution fusion | flops 144902208 | bytes 4527104 | tf_op jit(solution)/shard_map/sub | solution.py:161
  106.6 2.2 fusion.29
  108.8 2.3 convolution_convert_fusion.5
  111.2 3.1 collective-permute-start.1
  114.3 1.1 collective-permute-start.2
  115.4 0.9 collective-permute-start
  116.3 0.2 fusion.52
  116.6 0.2 convolution_convert_fusion.6
  116.8 0.9 reshape_reshape.6
  117.7 4.2 %collective-permute-done.1 = bf16[64,2048]{1,0:T(8,128)(2,1)S(1)} collective-permute-done((bf16[64,2048]{1,0:T(8,128)(2,1)S(1)}, bf16[64,2048]{1,0:T(8,128)(2,1)S(1)}, u32[]{:S(2)}, u32[]{:S(2)}) %collective-permute-start.1) | collective-permute-done | bytes 262176 | tf_op jit(solution)/shard_map/ppermute | solution.py:58
  121.9 5.0 %collective-permute-done.2 = bf16[64,2048]{1,0:T(8,128)(2,1)S(1)} collective-permute-done((bf16[64,2048]{1,0:T(8,128)(2,1)S(1)}, bf16[64,2048]{1,0:T(8,128)(2,1)S(1)}, u32[]{:S(2)}, u32[]{:S(2)}) %collective-permute-start.2) | collective-permute-done | bytes 262176 | tf_op jit(solution)/shard_map/ppermute | solution.py:58
  126.9 0.5 multiply_reduce_fusion.1
  127.5 0.8 copy-done.1
  128.3 0.5 convolution_convert_fusion.4
  128.8 0.4 reshape.237
  129.2 1.8 pad_maximum_fusion.1
  131.0 7.5 %all-to-all-start = ((bf16[64,1,4,2560]{3,2,1,0:T(4,128)(2,1)}), bf16[64,1,4,2560]{3,2,1,0:T(4,128)(2,1)S(1)}, u32[]{:S(2)}, u32[]{:S(2)}) async-start(bf16[64,1,4,2560]{3,2,1,0:T(4,128)(2,1)} %pad_maximum_fusion.1), calls=%async_computation | async-start | bytes 2621440 | tf_op jit(solution)/shard_map/all_to_all | solution.py:193
  138.5 1.5 pad_maximum_fusion
  140.0 2.6 collective-permute-start.7
  142.7 0.9 collective-permute-start.5
  143.5 0.8 collective-permute-start.3
  144.4 2.4 collective-permute-start.8
  146.8 1.4 collective-permute-start.6
  148.2 24.6 %all-to-all-done = bf16[64,1,4,2560]{3,2,1,0:T(4,128)(2,1)S(1)} async-done(((bf16[64,1,4,2560]{3,2,1,0:T(4,128)(2,1)}), bf16[64,1,4,2560]{3,2,1,0:T(4,128)(2,1)S(1)}, u32[]{:S(2)}, u32[]{:S(2)}) %all-to-all-start) | async-done | bytes 1310752 | tf_op jit(solution)/shard_map/all_to_all | solution.py:193
  172.9 1.1 copy-done
  174.0 0.6 slice.66
  174.6 0.3 reshape_squeeze.3
  174.9 1.1 fusion.45
  176.0 2.9 fusion.4
  178.9 54.9 %collective-permute-done.7 = bf16[2,1,2048,256]{3,2,1,0:T(8,128)(2,1)} collective-permute-done((bf16[2,1,2048,256]{3,2,1,0:T(8,128)(2,1)}, bf16[2,1,2048,256]{3,2,1,0:T(8,128)(2,1)}, u32[]{:S(2)}, u32[]{:S(2)}) %collective-permute-start.7) | collective-permute-done | bytes 2097184 | tf_op jit(solution)/shard_map/ppermute | solution.py:83
  233.8 2.4 fusion.33
  236.2 1.7 fusion.35
  237.8 0.2 collective-permute-done.3
  238.0 2.4 fusion.37
  240.4 37.7 %collective-permute-done.8 = bf16[1,256,2048]{2,1,0:T(8,128)(2,1)} collective-permute-done((bf16[1,256,2048]{2,1,0:T(8,128)(2,1)}, bf16[1,256,2048]{2,1,0:T(8,128)(2,1)}, u32[]{:S(2)}, u32[]{:S(2)}) %collective-permute-start.8) | collective-permute-done | bytes 1048608 | tf_op jit(solution)/shard_map/ppermute | solution.py:84
  278.1 4.3 %fusion.11 = f32[256,2048]{1,0:T(8,128)} fusion(bf16[1,256,2048]{2,1,0:T(8,128)(2,1)} %collective-permute-done.8, f32[256,256]{1,0:T(8,128)} %fusion.33, bf16[256,2048]{1,0:T(8,128)(2,1)S(1)} %reshape_squeeze.3, bf16[2,1,2048,256]{3,2,1,0:T(8,128)(2,1)} %collective-permute-done.7), kind=kOutput, calls=%fused_computation.19 | convolution fusion | flops 538312704 | bytes 5505024 | tf_op jit(solution)/shard_map/dot_general | solution.py:94
  282.3 4.2 %fusion.10 = f32[256,2048]{1,0:T(8,128)} fusion(bf16[1,256,2048]{2,1,0:T(8,128)(2,1)} %collective-permute-done.6, f32[256,256]{1,0:T(8,128)S(1)} %fusion.35, bf16[256,2048]{1,0:T(8,128)(2,1)S(1)} %reshape_squeeze.3, bf16[2,1,2048,256]{3,2,1,0:T(8,128)(2,1)} %collective-permute-done.5), kind=kOutput, calls=%fused_computation.18 | convolution fusion | flops 538312704 | bytes 5505024 | tf_op jit(solution)/shard_map/dot_general | solution.py:94
  286.5 5.2 %fusion.9 = bf16[256,2048]{1,0:T(8,128)(2,1)} fusion(f32[256,2048]{1,0:T(8,128)} %fusion.11, f32[256,2048]{1,0:T(8,128)} %fusion.10, f32[256,2048]{1,0:T(8,128)S(1)} %fusion.4, bf16[1,256,2048]{2,1,0:T(8,128)(2,1)} %collective-permute-done.4, f32[256,256]{1,0:T(8,128)} %fusion.37, bf16[256,2048]{1,0:T(8,128)(2,1)S(1)} %reshape_squeeze.3, ...), kind=kOutput, calls=%fused_computation.17 | convolution fusion | flops 540409856 | bytes 10747904 | tf_op jit(solution)/shard_map/dot_general | solution.py:94
  291.8 2.3 convert_element_type.171
  294.0 10.3 %all-to-all-start.1 = ((bf16[64,1,4,2048]{3,2,1,0:T(4,128)(2,1)}), bf16[64,1,4,2048]{3,2,1,0:T(4,128)(2,1)S(1)}, u32[]{:S(2)}, u32[]{:S(2)}) async-start(bf16[64,1,4,2048]{3,2,1,0:T(4,128)(2,1)} %bitcast.42), calls=%async_computation.1 | async-start | bytes 2097152 | tf_op jit(solution)/shard_map/all_to_all | solution.py:200
  304.4 28.7 %all-to-all-done.1 = bf16[64,1,4,2048]{3,2,1,0:T(4,128)(2,1)S(1)} async-done(((bf16[64,1,4,2048]{3,2,1,0:T(4,128)(2,1)}), bf16[64,1,4,2048]{3,2,1,0:T(4,128)(2,1)S(1)}, u32[]{:S(2)}, u32[]{:S(2)}) %all-to-all-start.1) | async-done | bytes 1048608 | tf_op jit(solution)/shard_map/all_to_all | solution.py:200
  333.1 0.3 reshape.259
  333.4 1.5 multiply_reduce_fusion
  335.0 3.7 %collective-permute-start.11 = (bf16[64,2048]{1,0:T(8,128)(2,1)S(1)}, bf16[64,2048]{1,0:T(8,128)(2,1)S(1)}, u32[]{:S(2)}, u32[]{:S(2)}) collective-permute-start(bf16[64,2048]{1,0:T(8,128)(2,1)S(1)} %multiply_reduce_fusion), channel_id=1, source_target_pairs={{0,192},{64,0},{128,64},{192,128},{1,193},{65,1},{129,65},{193,129... | collective-permute-start | bytes 786440 | tf_op jit(solution)/shard_map/ppermute | solution.py:58
  338.7 0.8 collective-permute-start.9
  339.5 0.9 reshape_reshape.7
  340.4 5.3 %collective-permute-done.10 = bf16[64,2048]{1,0:T(8,128)(2,1)S(1)} collective-permute-done((bf16[64,2048]{1,0:T(8,128)(2,1)S(1)}, bf16[64,2048]{1,0:T(8,128)(2,1)S(1)}, u32[]{:S(2)}, u32[]{:S(2)}) %collective-permute-start.10) | collective-permute-done | bytes 262176 | tf_op jit(solution)/shard_map/ppermute | solution.py:58
  345.7 4.5 %collective-permute-done.11 = bf16[64,2048]{1,0:T(8,128)(2,1)S(1)} collective-permute-done((bf16[64,2048]{1,0:T(8,128)(2,1)S(1)}, bf16[64,2048]{1,0:T(8,128)(2,1)S(1)}, u32[]{:S(2)}, u32[]{:S(2)}) %collective-permute-start.11) | collective-permute-done | bytes 262176 | tf_op jit(solution)/shard_map/ppermute | solution.py:58
  350.2 1.0 add_convert_fusion
  (72 shorter events, 1.8 us)
Async XLA Ops:
  7.2 88.8 %all-gather.2.cloned.1.call-start = ((), (), s32[]{:S(2)}) async-start(), calls=%async_computation.2 | async-start | bytes 8519680 | tf_op jit(solution)/shard_map/all_gather | solution.py:128
  23.2 2.6 copy-start.14
  23.2 2.7 copy-start.11
  23.2 2.9 copy-start.8
  26.6 5.1 %copy-start.15 = (s32[1,16]{1,0:T(1,128)S(1)}, s32[1,16]{1,0:T(1,128)}, u32[]{:S(2)}) copy-start(s32[1,16]{1,0:T(1,128)} %param.24) | copy-start | bytes 196
  26.6 5.3 %copy-start.12 = (s32[1,4]{1,0:T(1,128)S(1)}, s32[1,4]{1,0:T(1,128)}, u32[]{:S(2)}) copy-start(s32[1,4]{1,0:T(1,128)} %param.25) | copy-start | bytes 52
  26.6 5.4 %copy-start.6 = (bf16[64,2048]{1,0:T(8,128)(2,1)S(1)}, bf16[64,2048]{1,0:T(8,128)(2,1)}, u32[]{:S(2)}) copy-start(bf16[64,2048]{1,0:T(8,128)(2,1)} %param.17) | copy-start | bytes 786436
  26.6 69.4 %copy-start.13 = (f32[2048]{0:T(1024)S(1)}, f32[2048]{0:T(1024)}, u32[]{:S(2)}) copy-start(f32[2048]{0:T(1024)} %param.18) | copy-start | bytes 24580
  102.4 4.2 %copy-start.5 = (bf16[2048,1,4,128]{3,0,2,1:T(8,128)(2,1)S(1)}, bf16[2048,1,4,128]{3,0,2,1:T(8,128)(2,1)}, u32[]{:S(2)}) copy-start(bf16[2048,1,4,128]{3,0,2,1:T(8,128)(2,1)} %copy.97) | copy-start | bytes 6291460
  108.8 19.5 %copy-start.9 = (f32[2048]{0:T(1024)S(1)}, f32[2048]{0:T(1024)}, u32[]{:S(2)}) copy-start(f32[2048]{0:T(1024)} %param.28) | copy-start | bytes 24580
  111.2 10.8 %collective-permute-start.1 = (bf16[64,2048]{1,0:T(8,128)(2,1)S(1)}, bf16[64,2048]{1,0:T(8,128)(2,1)S(1)}, u32[]{:S(2)}, u32[]{:S(2)}) collective-permute-start(bf16[64,2048]{1,0:T(8,128)(2,1)S(1)} %convolution_convert_fusion.5), channel_id=1, source_target_pairs={{0,128},{64,192},{128,0},{192,64},{1,129},{65,193},{129,1},{193,65... | collective-permute-start | bytes 786440 | tf_op jit(solution)/shard_map/ppermute | solution.py:58
  114.3 12.7 %collective-permute-start.2 = (bf16[64,2048]{1,0:T(8,128)(2,1)S(1)}, bf16[64,2048]{1,0:T(8,128)(2,1)S(1)}, u32[]{:S(2)}, u32[]{:S(2)}) collective-permute-start(bf16[64,2048]{1,0:T(8,128)(2,1)S(1)} %convolution_convert_fusion.5), channel_id=1, source_target_pairs={{0,192},{64,0},{128,64},{192,128},{1,193},{65,1},{129,65},{193,129... | collective-permute-start | bytes 786440 | tf_op jit(solution)/shard_map/ppermute | solution.py:58
  115.4 11.5 %collective-permute-start = (bf16[64,2048]{1,0:T(8,128)(2,1)S(1)}, bf16[64,2048]{1,0:T(8,128)(2,1)S(1)}, u32[]{:S(2)}, u32[]{:S(2)}) collective-permute-start(bf16[64,2048]{1,0:T(8,128)(2,1)S(1)} %convolution_convert_fusion.5), channel_id=1, source_target_pairs={{0,64},{64,128},{128,192},{192,0},{1,65},{65,129},{129,193},{193,1... | collective-permute-start | bytes 786440 | tf_op jit(solution)/shard_map/ppermute | solution.py:58
  127.4 0.8 copy-start.1
  127.4 1.8 copy-start.7
  129.2 9.3 %copy-start.3 = (bf16[1,2048,256]{2,1,0:T(8,128)(2,1)S(1)}, bf16[1,2048,256]{2,1,0:T(8,128)(2,1)}, u32[]{:S(2)}) copy-start(bf16[1,2048,256]{2,1,0:T(8,128)(2,1)} %param.29) | copy-start | bytes 3145732
  131.0 7.5 %copy-start.4 = (bf16[1,2048,256]{2,1,0:T(8,128)(2,1)S(1)}, bf16[1,2048,256]{2,1,0:T(8,128)(2,1)}, u32[]{:S(2)}) copy-start(bf16[1,2048,256]{2,1,0:T(8,128)(2,1)} %param.30) | copy-start | bytes 3145732
  131.0 41.9 %all-to-all-start = ((bf16[64,1,4,2560]{3,2,1,0:T(4,128)(2,1)}), bf16[64,1,4,2560]{3,2,1,0:T(4,128)(2,1)S(1)}, u32[]{:S(2)}, u32[]{:S(2)}) async-start(bf16[64,1,4,2560]{3,2,1,0:T(4,128)(2,1)} %pad_maximum_fusion.1), calls=%async_computation | async-start | bytes 2621440 | tf_op jit(solution)/shard_map/all_to_all | solution.py:193
  140.0 93.8 %collective-permute-start.7 = (bf16[2,1,2048,256]{3,2,1,0:T(8,128)(2,1)}, bf16[2,1,2048,256]{3,2,1,0:T(8,128)(2,1)}, u32[]{:S(2)}, u32[]{:S(2)}) collective-permute-start(bf16[2,1,2048,256]{3,2,1,0:T(8,128)(2,1)} %pad_maximum_fusion), channel_id=1, source_target_pairs={{0,192},{64,0},{128,64},{192,128},{1,193},{65,1},{129,65},{193,129... | collective-permute-start | bytes 6291464 | tf_op jit(solution)/shard_map/ppermute | solution.py:83
  142.7 93.5 %collective-permute-start.5 = (bf16[2,1,2048,256]{3,2,1,0:T(8,128)(2,1)}, bf16[2,1,2048,256]{3,2,1,0:T(8,128)(2,1)}, u32[]{:S(2)}, u32[]{:S(2)}) collective-permute-start(bf16[2,1,2048,256]{3,2,1,0:T(8,128)(2,1)} %pad_maximum_fusion), channel_id=1, source_target_pairs={{0,128},{64,192},{128,0},{192,64},{1,129},{65,193},{129,1},{193,65... | collective-permute-start | bytes 6291464 | tf_op jit(solution)/shard_map/ppermute | solution.py:83
  143.5 94.5 %collective-permute-start.3 = (bf16[2,1,2048,256]{3,2,1,0:T(8,128)(2,1)}, bf16[2,1,2048,256]{3,2,1,0:T(8,128)(2,1)}, u32[]{:S(2)}, u32[]{:S(2)}) collective-permute-start(bf16[2,1,2048,256]{3,2,1,0:T(8,128)(2,1)} %pad_maximum_fusion), channel_id=1, source_target_pairs={{0,64},{64,128},{128,192},{192,0},{1,65},{65,129},{129,193},{193,1... | collective-permute-start | bytes 6291464 | tf_op jit(solution)/shard_map/ppermute | solution.py:83
  144.4 133.7 %collective-permute-start.8 = (bf16[1,256,2048]{2,1,0:T(8,128)(2,1)}, bf16[1,256,2048]{2,1,0:T(8,128)(2,1)}, u32[]{:S(2)}, u32[]{:S(2)}) collective-permute-start(bf16[1,256,2048]{2,1,0:T(8,128)(2,1)} %param.31), channel_id=1, source_target_pairs={{0,192},{64,0},{128,64},{192,128},{1,193},{65,1},{129,65},{193,129... | collective-permute-start | bytes 3145736 | tf_op jit(solution)/shard_map/ppermute | solution.py:84
  146.8 135.6 %collective-permute-start.6 = (bf16[1,256,2048]{2,1,0:T(8,128)(2,1)}, bf16[1,256,2048]{2,1,0:T(8,128)(2,1)}, u32[]{:S(2)}, u32[]{:S(2)}) collective-permute-start(bf16[1,256,2048]{2,1,0:T(8,128)(2,1)} %param.31), channel_id=1, source_target_pairs={{0,128},{64,192},{128,0},{192,64},{1,129},{65,193},{129,1},{193,65... | collective-permute-start | bytes 3145736 | tf_op jit(solution)/shard_map/ppermute | solution.py:84
  172.9 1.1 copy-start
  233.8 52.7 %collective-permute-start.4 = (bf16[1,256,2048]{2,1,0:T(8,128)(2,1)}, bf16[1,256,2048]{2,1,0:T(8,128)(2,1)}, u32[]{:S(2)}, u32[]{:S(2)}) collective-permute-start(bf16[1,256,2048]{2,1,0:T(8,128)(2,1)} %param.31), channel_id=1, source_target_pairs={{0,64},{64,128},{128,192},{192,0},{1,65},{65,129},{129,193},{193,1... | collective-permute-start | bytes 3145736 | tf_op jit(solution)/shard_map/ppermute | solution.py:84
  291.8 12.6 %copy-start.10 = (f32[64,8]{0,1:T(8,128)S(1)}, f32[64,8]{0,1:T(8,128)}, u32[]{:S(2)}) copy-start(f32[64,8]{0,1:T(8,128)} %param.33) | copy-start | bytes 6148
  294.0 39.1 %all-to-all-start.1 = ((bf16[64,1,4,2048]{3,2,1,0:T(4,128)(2,1)}), bf16[64,1,4,2048]{3,2,1,0:T(4,128)(2,1)S(1)}, u32[]{:S(2)}, u32[]{:S(2)}) async-start(bf16[64,1,4,2048]{3,2,1,0:T(4,128)(2,1)} %bitcast.42), calls=%async_computation.1 | async-start | bytes 2097152 | tf_op jit(solution)/shard_map/all_to_all | solution.py:200
  333.4 6.1 %slice-start = ((bf16[64,1,4,2560]{3,2,1,0:T(4,128)(2,1)}), bf16[64,1,4,512]{3,2,1,0:T(4,128)(2,1)S(1)}, s32[]{:S(2)}) async-start(bf16[64,1,4,2560]{3,2,1,0:T(4,128)(2,1)} %copy-done), calls=%async_computation.3 | async-start | bytes 524288 | tf_op jit(solution)/shard_map/slice | solution.py:195
  333.4 16.8 %copy-start.2 = (f32[64,2048]{1,0:T(8,128)S(1)}, f32[64,2048]{1,0:T(8,128)}, u32[]{:S(2)}) copy-start(f32[64,2048]{1,0:T(8,128)} %copy-done.1) | copy-start | bytes 1572868
  334.9 10.8 %collective-permute-start.10 = (bf16[64,2048]{1,0:T(8,128)(2,1)S(1)}, bf16[64,2048]{1,0:T(8,128)(2,1)S(1)}, u32[]{:S(2)}, u32[]{:S(2)}) collective-permute-start(bf16[64,2048]{1,0:T(8,128)(2,1)S(1)} %multiply_reduce_fusion), channel_id=1, source_target_pairs={{0,128},{64,192},{128,0},{192,64},{1,129},{65,193},{129,1},{193,65... | collective-permute-start | bytes 786440 | tf_op jit(solution)/shard_map/ppermute | solution.py:58
  335.0 15.2 %collective-permute-start.11 = (bf16[64,2048]{1,0:T(8,128)(2,1)S(1)}, bf16[64,2048]{1,0:T(8,128)(2,1)S(1)}, u32[]{:S(2)}, u32[]{:S(2)}) collective-permute-start(bf16[64,2048]{1,0:T(8,128)(2,1)S(1)} %multiply_reduce_fusion), channel_id=1, source_target_pairs={{0,192},{64,0},{128,64},{192,128},{1,193},{65,1},{129,65},{193,129... | collective-permute-start | bytes 786440 | tf_op jit(solution)/shard_map/ppermute | solution.py:58
  338.7 11.5 %collective-permute-start.9 = (bf16[64,2048]{1,0:T(8,128)(2,1)S(1)}, bf16[64,2048]{1,0:T(8,128)(2,1)S(1)}, u32[]{:S(2)}, u32[]{:S(2)}) collective-permute-start(bf16[64,2048]{1,0:T(8,128)(2,1)S(1)} %multiply_reduce_fusion), channel_id=1, source_target_pairs={{0,64},{64,128},{128,192},{192,0},{1,65},{65,129},{129,193},{193,1... | collective-permute-start | bytes 786440 | tf_op jit(solution)/shard_map/ppermute | solution.py:58
Sparse Core Ops, SparseCore 0:
  11.4 84.6 all-gather.1

commit v6 on v5

--- a/solution.py
+++ b/solution.py
@@ -83,17 +83,25 @@
         gate_up = lax.ppermute(held[0][0], "dp", pairs)
         down = lax.ppermute(held[0][1], "dp", pairs)
         held.append((gate_up, down))
+    gate_up_all = jnp.concatenate([gate_up for gate_up, _ in held], axis=-1)
+    block = held[0][1].shape[1]
     outs = []
     for e in range(local_experts):
         rows = routed[:, e].reshape(sources * slots, width)
-        total = None
-        for gate_up, down in held:
-            gate_proj = jnp.dot(rows, gate_up[0, e], preferred_element_type=jnp.float32)
-            up_proj = jnp.dot(rows, gate_up[1, e], preferred_element_type=jnp.float32)
-            active = (jax.nn.silu(gate_proj) * up_proj).astype(jnp.bfloat16)
-            part = jnp.dot(active, down[e], preferred_element_type=jnp.float32)
-            part = part.astype(jnp.bfloat16).astype(jnp.float32)
-            total = part if total is None else total + part
+        gate_proj = jnp.dot(rows, gate_up_all[0, e], preferred_element_type=jnp.float32)
+        up_proj = jnp.dot(rows, gate_up_all[1, e], preferred_element_type=jnp.float32)
+        active = (jax.nn.silu(gate_proj) * up_proj).astype(jnp.bfloat16)
+        down_all = jnp.stack([down[e] for _, down in held])
+        parts = jnp.einsum(
+            "rnf,nfd->nrd",
+            active.reshape(sources * slots, n_dp, block),
+            down_all,
+            preferred_element_type=jnp.float32,
+        )
+        parts = parts.astype(jnp.bfloat16).astype(jnp.float32)
+        total = parts[0]
+        for j in range(1, n_dp):
+            total = total + parts[j]
         outs.append(total.reshape(sources, slots, width))
     return jnp.stack(outs, axis=1)
 

time: 359 us -> 286 us (0.80)
  waiting for transfers between devices: 229 us -> 156 us
  matrix products: 41.4 us -> 27.9 us
  other arithmetic: 7.97 us -> 18.4 us
    ppermute x3, waiting for transfers between devices: 55.1 us -> 26.8 us  [expert_block(): gate_up = lax.ppermute(held[0][0], 'dp', pairs)]
    all_to_all x1, waiting for transfers between devices: 24.6 us -> 0.01 us  [local_body(): lax.all_to_all(send, 'expert', split_axis=0, concat_axis=0, tiled=True)]
    dot_general x8 -> x3, matrix products: 24.1 us -> 9.49 us  [the longest x1 3.9 us: expert_block(): jnp.dot(rows, gate_up_all[0, e], preferred_element_type=jnp.float32)]
    ppermute x3, waiting for transfers between devices: 37.7 us -> 27.6 us  [expert_block(): down = lax.ppermute(held[0][1], 'dp', pairs)]
    all_gather x1, waiting for transfers between devices: 63.5 us -> 56 us  [local_body(): lax.all_gather(jnp.stack([w_query, w_key, w_value, w_out]), 'expert', axi...]
    concatenate x0 -> x1, other arithmetic: none -> 6.9 us  [expert_block(): gate_up_all = jnp.concatenate([gate_up for gate_up, _ in held], axis=-1)]
    unnamed x38 -> x32, local copies, waits for them, and re-layouts: 15.1 us -> 14.2 us
  transfers between devices with their start and end apart: 15 -> 15, of which waited for: 10 -> 10; matrix products, arithmetic and copies ran while one was open for 13% -> 22% of each run, Pallas kernels for 0% -> 0%
where the time goes in v6:
time: 286 us; the launch traced here: 284 us
  waiting for transfers between devices  156 us (55%)
  starting transfers between devices  37.9 us (13%)
  local copies, waits for them, and re-layouts  29.7 us (10%)
  matrix products  27.9 us (10%)
  other arithmetic  18.4 us (6%)
  between operations  14.4 us (5%)
    all_gather x1, waiting for transfers between devices, local_body(): lax.all_gather(jnp.stack([w_query, w_key, w_value, w_out]), 'expert', axi...  56 us
    all_to_all x1, waiting for transfers between devices, local_body(): lax.all_to_all(contrib.astype(jnp.bfloat16), 'expert', split_axis=0, conc...  28.7 us
    ppermute x3, waiting for transfers between devices, expert_block(): down = lax.ppermute(held[0][1], 'dp', pairs)  27.6 us
    ppermute x3, waiting for transfers between devices, expert_block(): gate_up = lax.ppermute(held[0][0], 'dp', pairs)  26.8 us
    ppermute x6, waiting for transfers between devices, dp_sum(): lax.ppermute(part, 'dp', [(i, (i + s) % n_dp) for i in range(n_dp)])  16.5 us
    unnamed x32, local copies, waits for them, and re-layouts  14.2 us
    ppermute x6, starting transfers between devices, dp_sum(): lax.ppermute(part, 'dp', [(i, (i + s) % n_dp) for i in range(n_dp)])  10.9 us
    all_to_all x1, starting transfers between devices, local_body(): lax.all_to_all(contrib.astype(jnp.bfloat16), 'expert', split_axis=0, conc...  7.31 us
  transfers between devices with their start and end apart: 15, of which 10 were waited for; matrix products, arithmetic and copies ran while one was open for 22% of the time, Pallas kernels for 0%

profile of v6, /device:TPU:2, one launch (start us, length us, event | category | flops | bytes accessed | tf_op | source)
XLA Modules:
  0.0 284.0 jit_solution(6840577215661996203)
XLA Ops:
  7.2 1.5 pad_maximum_fusion.3
  8.7 3.1 %pad_maximum_fusion.1 = bf16[2,1,2048,256]{3,2,1,0:T(8,128)(2,1)} fusion(bf16[1,1,2048,256]{3,2,1,0:T(8,128)(2,1)} %bitcast.106, bf16[1,1,2048,256]{3,2,1,0:T(8,128)(2,1)} %bitcast.108), kind=kLoop, calls=%fused_computation.43 | loop fusion | flops 1048576 | bytes 4194304 | tf_op jit(solution)/shard_map/stack | solution.py:80
  11.8 1.6 collective-permute-start.3
  13.4 2.9 %collective-permute-start.4 = (bf16[2,1,2048,256]{3,2,1,0:T(8,128)(2,1)}, bf16[2,1,2048,256]{3,2,1,0:T(8,128)(2,1)}, u32[]{:S(2)}, u32[]{:S(2)}) collective-permute-start(bf16[2,1,2048,256]{3,2,1,0:T(8,128)(2,1)} %pad_maximum_fusion.1), channel_id=1, source_target_pairs={{0,128},{64,192},{128,0},{192,64},{1,129},{65,193},{129,1},{193,65... | collective-permute-start | bytes 6291464 | tf_op jit(solution)/shard_map/ppermute | solution.py:83
  16.3 6.5 %copy.84 = bf16[2048,1024]{0,1:T(8,128)(2,1)} copy(bf16[2048,1024]{1,0:T(8,128)(2,1)} %param.23) | data formatting | bytes 8388608 | tf_op args[6]
  22.7 4.0 %fusion.87 = (bf16[2048,1,4,128]{0,3,2,1:T(8,128)(2,1)}, bf16[2048,1,4,128]{0,3,2,1:T(8,128)(2,1)S(1)}) fusion(bf16[2048,2,4,128]{0,3,2,1:T(8,128)(2,1)} %bitcast.105), kind=kLoop, calls=%fused_computation.136 | loop fusion | bytes 8388608 | tf_op jit(solution)/shard_map/slice | solution.py:155
  26.7 3.9 %copy.101 = bf16[2048,1,4,128]{3,0,2,1:T(8,128)(2,1)} copy(bf16[2048,1,4,128]{0,3,2,1:T(8,128)(2,1)} %get-tuple-element.4) | data formatting | bytes 4194304
  30.7 2.5 copy.102
  33.3 0.2 reduce-window.8
  33.4 0.2 convert_reduce_fusion
  33.6 0.1 reduce_window_sum.24
  34.0 3.8 %gather_fusion = s32[512]{0:T(512)S(1)} fusion(s32[64,64]{1,0:T(8,128)S(1)} %sub.48, s32[512]{0:T(512)S(1)} %reshape.281), kind=kCustom, calls=%fused_computation | custom fusion | bytes 8192 | tf_op jit(solution)/shard_map/jit(take_along_axis)/gather | solution.py:25
  38.1 0.1 reduce_window_sum.25
  38.3 0.8 gather_fusion.1
  39.5 0.2 fusion.37
  39.8 0.2 compare_and_fusion
  40.0 56.0 %all-gather.2.cloned.1.call-done = bf16[4,2048,512]{2,1,0:T(8,128)(2,1)} async-done(((bf16[4,32,512]{2,1,0:T(8,128)(2,1)}), bf16[4,2048,512]{2,1,0:T(8,128)(2,1)}) %all-gather.2.cloned.1.call-update) | async-done | bytes 8388624 | tf_op jit(solution)/shard_map/all_gather | solution.py:136
  96.0 2.1 fusion.28
  98.2 2.1 fusion.29
  100.3 2.1 fusion.36
  102.5 4.2 %fusion.88 = (f32[4,64]{1,0:T(4,128)S(1)}, f32[4,64,2112]{2,1,0:T(8,128)}) fusion(bf16[64,4,128]{2,0,1:T(8,128)(2,1)S(1)} %copy_bitcast_fusion.1, bf16[2048,4,128]{2,0,1:T(8,128)(2,1)} %bitcast.113, pred[64,2112]{1,0:T(8,128)(4,1)S(1)} %pad_add_fusion, bf16[8,4,8,128]{3,2,1,0:T(8,128)(2,1)S(1)} %fusion.36), kind=kOutput, calls=%fused_computation.137 | convolution fusion | flops 144902208 | bytes 4527104 | tf_op jit(solution)/shard_map/sub | solution.py:169
  106.7 2.2 fusion.33
  108.8 2.3 convolution_convert_fusion.1
  111.2 1.6 collective-permute-start
  112.8 2.7 collective-permute-start.1
  115.5 1.4 collective-permute-start.2
  116.9 0.2 fusion.44
  117.2 0.2 convolution_convert_fusion.2
  117.4 0.2 reshape_reshape.6
  117.6 3.3 %collective-permute-done = bf16[64,2048]{1,0:T(8,128)(2,1)S(1)} collective-permute-done((bf16[64,2048]{1,0:T(8,128)(2,1)S(1)}, bf16[64,2048]{1,0:T(8,128)(2,1)S(1)}, u32[]{:S(2)}, u32[]{:S(2)}) %collective-permute-start) | collective-permute-done | bytes 262176 | tf_op jit(solution)/shard_map/ppermute | solution.py:58
  120.9 2.2 collective-permute-start.5
  123.2 4.3 %collective-permute-done.1 = bf16[64,2048]{1,0:T(8,128)(2,1)S(1)} collective-permute-done((bf16[64,2048]{1,0:T(8,128)(2,1)S(1)}, bf16[64,2048]{1,0:T(8,128)(2,1)S(1)}, u32[]{:S(2)}, u32[]{:S(2)}) %collective-permute-start.1) | collective-permute-done | bytes 262176 | tf_op jit(solution)/shard_map/ppermute | solution.py:58
  127.5 0.7 collective-permute-done.2
  128.2 0.5 multiply_reduce_fusion.1
  128.7 0.5 convolution_convert_fusion
  129.2 1.2 reshape.277
  130.4 3.0 %pad_maximum_fusion.2 = bf16[64,1,4,2560]{3,2,1,0:T(4,128)(2,1)} fusion(bf16[64,1,4,512]{3,2,1,0:T(4,128)(2,1)S(1)} %bitcast.114, bf16[64,1,4,2048]{3,2,1,0:T(4,128)(2,1)} %bitcast.111), kind=kLoop, calls=%fused_computation.44 | loop fusion | flops 2621440 | bytes 2621440 | tf_op jit(solution)/shard_map/concatenate | solution.py:198
  133.4 7.3 %all-to-all-start = ((bf16[64,1,4,2560]{3,2,1,0:T(4,128)(2,1)}), bf16[64,1,4,2560]{3,2,1,0:T(4,128)(2,1)S(1)}, u32[]{:S(2)}, u32[]{:S(2)}) async-start(bf16[64,1,4,2560]{3,2,1,0:T(4,128)(2,1)} %pad_maximum_fusion.2), calls=%async_computation | async-start | bytes 2621440 | tf_op jit(solution)/shard_map/all_to_all | solution.py:201
  140.8 1.6 collective-permute-start.6
  142.3 1.7 collective-permute-start.7
  144.0 2.4 collective-permute-start.8
  146.5 26.8 %collective-permute-done.5 = bf16[2,1,2048,256]{3,2,1,0:T(8,128)(2,1)} collective-permute-done((bf16[2,1,2048,256]{3,2,1,0:T(8,128)(2,1)}, bf16[2,1,2048,256]{3,2,1,0:T(8,128)(2,1)}, u32[]{:S(2)}, u32[]{:S(2)}) %collective-permute-start.5) | collective-permute-done | bytes 2097184 | tf_op jit(solution)/shard_map/ppermute | solution.py:83
  173.2 6.9 %pad_maximum_fusion = bf16[2,1,2048,1024]{3,2,1,0:T(8,128)(2,1)} fusion(bf16[2,1,2048,256]{3,2,1,0:T(8,128)(2,1)} %collective-permute-done.5, bf16[2,1,2048,256]{3,2,1,0:T(8,128)(2,1)} %collective-permute-done.4, bf16[2,1,2048,256]{3,2,1,0:T(8,128)(2,1)} %collective-permute-done.3, bf16[1,1,2048,256]{3,2,1,0:T(8,128)(2,1)S(1)} %bitcast.107, ...), kind=kLoop, calls=%fused_computation.3 | loop fusion | flops 41943040 | bytes 16777216 | tf_op jit(solution)/shard_map/concatenate | solution.py:86
  180.1 0.6 slice.66
  180.7 1.2 reshape_squeeze.3
  181.9 3.9 %fusion.4 = f32[256,1024]{1,0:T(8,128)S(1)} fusion(bf16[256,2048]{1,0:T(8,128)(2,1)} %reshape_squeeze.3, bf16[2,1,2048,1024]{3,2,1,0:T(8,128)(2,1)} %pad_maximum_fusion), kind=kOutput, calls=%fused_computation.10 | convolution fusion | flops 1073741824 | bytes 6291456 | tf_op jit(solution)/shard_map/dot_general | solution.py:91
  185.8 1.0 copy-done
  186.9 2.7 multiply_convert_fusion
  189.6 0.5 collective-permute-done.7
  190.0 27.2 %collective-permute-done.8 = bf16[1,256,2048]{2,1,0:T(8,128)(2,1)} collective-permute-done((bf16[1,256,2048]{2,1,0:T(8,128)(2,1)}, bf16[1,256,2048]{2,1,0:T(8,128)(2,1)}, u32[]{:S(2)}, u32[]{:S(2)}) %collective-permute-start.8) | collective-permute-done | bytes 1048608 | tf_op jit(solution)/shard_map/ppermute | solution.py:84
  217.2 2.9 %convert_convert_fusion = f32[4,256,2048]{2,1,0:T(8,128)S(1)} fusion(bf16[1,256,2048]{2,1,0:T(8,128)(2,1)} %collective-permute-done.8, bf16[1,256,2048]{2,1,0:T(8,128)(2,1)} %collective-permute-done.7, bf16[1,256,2048]{2,1,0:T(8,128)(2,1)} %collective-permute-done.6, bf16[1,256,2048]{2,1,0:T(8,128)(2,1)S(1)} %copy-done.9, ...), kind=kOutput, calls=%fused_computation.20 | convolution fusion | flops 1084227584 | bytes 13107200 | tf_op jit(solution)/shard_map/rnf,nfd->nrd/dot_general | solution.py:95
  220.1 0.7 fusion.23
  220.8 1.2 convert_element_type.135
  222.0 7.3 %all-to-all-start.1 = ((bf16[64,1,4,2048]{3,2,1,0:T(4,128)(2,1)}), bf16[64,1,4,2048]{3,2,1,0:T(4,128)(2,1)S(1)}, u32[]{:S(2)}, u32[]{:S(2)}) async-start(bf16[64,1,4,2048]{3,2,1,0:T(4,128)(2,1)} %bitcast.110), calls=%async_computation.1 | async-start | bytes 2097152 | tf_op jit(solution)/shard_map/all_to_all | solution.py:208
  229.4 28.7 %all-to-all-done.1 = bf16[64,1,4,2048]{3,2,1,0:T(4,128)(2,1)S(1)} async-done(((bf16[64,1,4,2048]{3,2,1,0:T(4,128)(2,1)}), bf16[64,1,4,2048]{3,2,1,0:T(4,128)(2,1)S(1)}, u32[]{:S(2)}, u32[]{:S(2)}) %all-to-all-start.1) | async-done | bytes 1048608 | tf_op jit(solution)/shard_map/all_to_all | solution.py:208
  258.1 1.1 reshape.300
  259.2 2.7 multiply_reduce_fusion
  261.9 3.1 %collective-permute-start.10 = (bf16[64,2048]{1,0:T(8,128)(2,1)S(1)}, bf16[64,2048]{1,0:T(8,128)(2,1)S(1)}, u32[]{:S(2)}, u32[]{:S(2)}) collective-permute-start(bf16[64,2048]{1,0:T(8,128)(2,1)S(1)} %multiply_reduce_fusion), channel_id=1, source_target_pairs={{0,128},{64,192},{128,0},{192,64},{1,129},{65,193},{129,1},{193,65... | collective-permute-start | bytes 786440 | tf_op jit(solution)/shard_map/ppermute | solution.py:58
  265.0 1.3 collective-permute-start.11
  266.3 0.7 collective-permute-start.9
  267.1 0.9 reshape_reshape.7
  268.0 4.7 %collective-permute-done.10 = bf16[64,2048]{1,0:T(8,128)(2,1)S(1)} collective-permute-done((bf16[64,2048]{1,0:T(8,128)(2,1)S(1)}, bf16[64,2048]{1,0:T(8,128)(2,1)S(1)}, u32[]{:S(2)}, u32[]{:S(2)}) %collective-permute-start.10) | collective-permute-done | bytes 262176 | tf_op jit(solution)/shard_map/ppermute | solution.py:58
  272.7 3.5 %collective-permute-done.11 = bf16[64,2048]{1,0:T(8,128)(2,1)S(1)} collective-permute-done((bf16[64,2048]{1,0:T(8,128)(2,1)S(1)}, bf16[64,2048]{1,0:T(8,128)(2,1)S(1)}, u32[]{:S(2)}, u32[]{:S(2)}) %collective-permute-start.11) | collective-permute-done | bytes 262176 | tf_op jit(solution)/shard_map/ppermute | solution.py:58
  276.2 1.0 add_convert_fusion
  (62 shorter events, 1.6 us)
Async XLA Ops:
  7.2 88.9 %all-gather.2.cloned.1.call-start = ((), (), s32[]{:S(2)}) async-start(), calls=%async_computation.2 | async-start | bytes 8519680 | tf_op jit(solution)/shard_map/all_gather | solution.py:136
  11.8 132.2 %collective-permute-start.3 = (bf16[2,1,2048,256]{3,2,1,0:T(8,128)(2,1)}, bf16[2,1,2048,256]{3,2,1,0:T(8,128)(2,1)}, u32[]{:S(2)}, u32[]{:S(2)}) collective-permute-start(bf16[2,1,2048,256]{3,2,1,0:T(8,128)(2,1)} %pad_maximum_fusion.1), channel_id=1, source_target_pairs={{0,64},{64,128},{128,192},{192,0},{1,65},{65,129},{129,193},{193,1... | collective-permute-start | bytes 6291464 | tf_op jit(solution)/shard_map/ppermute | solution.py:83
  13.4 133.1 %collective-permute-start.4 = (bf16[2,1,2048,256]{3,2,1,0:T(8,128)(2,1)}, bf16[2,1,2048,256]{3,2,1,0:T(8,128)(2,1)}, u32[]{:S(2)}, u32[]{:S(2)}) collective-permute-start(bf16[2,1,2048,256]{3,2,1,0:T(8,128)(2,1)} %pad_maximum_fusion.1), channel_id=1, source_target_pairs={{0,128},{64,192},{128,0},{192,64},{1,129},{65,193},{129,1},{193,65... | collective-permute-start | bytes 6291464 | tf_op jit(solution)/shard_map/ppermute | solution.py:83
  30.7 2.5 copy-start.4
  30.7 2.6 copy-start.11
  33.9 4.1 %copy-start.7 = (s32[64,1]{0,1:T(1,128)S(1)}, s32[64,1]{0,1:T(1,128)}, u32[]{:S(2)}) copy-start(s32[64,1]{0,1:T(1,128)} %param.27) | copy-start | bytes 772
  33.9 5.2 %copy-start.12 = (s32[1,16]{1,0:T(1,128)S(1)}, s32[1,16]{1,0:T(1,128)}, u32[]{:S(2)}) copy-start(s32[1,16]{1,0:T(1,128)} %param.24) | copy-start | bytes 196
  33.9 5.4 %copy-start.8 = (s32[1,4]{1,0:T(1,128)S(1)}, s32[1,4]{1,0:T(1,128)}, u32[]{:S(2)}) copy-start(s32[1,4]{1,0:T(1,128)} %param.25) | copy-start | bytes 52
  33.9 5.5 %copy-start.3 = (bf16[64,2048]{1,0:T(8,128)(2,1)S(1)}, bf16[64,2048]{1,0:T(8,128)(2,1)}, u32[]{:S(2)}) copy-start(bf16[64,2048]{1,0:T(8,128)(2,1)} %param.17) | copy-start | bytes 786436
  33.9 62.1 %copy-start.10 = (f32[2048]{0:T(1024)S(1)}, f32[2048]{0:T(1024)}, u32[]{:S(2)}) copy-start(f32[2048]{0:T(1024)} %param.18) | copy-start | bytes 24580
  102.4 4.2 %copy-start.2 = (bf16[2048,1,4,128]{3,0,2,1:T(8,128)(2,1)S(1)}, bf16[2048,1,4,128]{3,0,2,1:T(8,128)(2,1)}, u32[]{:S(2)}) copy-start(bf16[2048,1,4,128]{3,0,2,1:T(8,128)(2,1)} %copy.102) | copy-start | bytes 6291460
  108.8 19.8 %copy-start.5 = (f32[2048]{0:T(1024)S(1)}, f32[2048]{0:T(1024)}, u32[]{:S(2)}) copy-start(f32[2048]{0:T(1024)} %param.28) | copy-start | bytes 24580
  111.2 9.7 %collective-permute-start = (bf16[64,2048]{1,0:T(8,128)(2,1)S(1)}, bf16[64,2048]{1,0:T(8,128)(2,1)S(1)}, u32[]{:S(2)}, u32[]{:S(2)}) collective-permute-start(bf16[64,2048]{1,0:T(8,128)(2,1)S(1)} %convolution_convert_fusion.1), channel_id=1, source_target_pairs={{0,64},{64,128},{128,192},{192,0},{1,65},{65,129},{129,193},{193,1... | collective-permute-start | bytes 786440 | tf_op jit(solution)/shard_map/ppermute | solution.py:58
  112.8 14.8 %collective-permute-start.1 = (bf16[64,2048]{1,0:T(8,128)(2,1)S(1)}, bf16[64,2048]{1,0:T(8,128)(2,1)S(1)}, u32[]{:S(2)}, u32[]{:S(2)}) collective-permute-start(bf16[64,2048]{1,0:T(8,128)(2,1)S(1)} %convolution_convert_fusion.1), channel_id=1, source_target_pairs={{0,128},{64,192},{128,0},{192,64},{1,129},{65,193},{129,1},{193,65... | collective-permute-start | bytes 786440 | tf_op jit(solution)/shard_map/ppermute | solution.py:58
  115.5 12.7 %collective-permute-start.2 = (bf16[64,2048]{1,0:T(8,128)(2,1)S(1)}, bf16[64,2048]{1,0:T(8,128)(2,1)S(1)}, u32[]{:S(2)}, u32[]{:S(2)}) collective-permute-start(bf16[64,2048]{1,0:T(8,128)(2,1)S(1)} %convolution_convert_fusion.1), channel_id=1, source_target_pairs={{0,192},{64,0},{128,64},{192,128},{1,193},{65,1},{129,65},{193,129... | collective-permute-start | bytes 786440 | tf_op jit(solution)/shard_map/ppermute | solution.py:58
  120.9 52.3 %collective-permute-start.5 = (bf16[2,1,2048,256]{3,2,1,0:T(8,128)(2,1)}, bf16[2,1,2048,256]{3,2,1,0:T(8,128)(2,1)}, u32[]{:S(2)}, u32[]{:S(2)}) collective-permute-start(bf16[2,1,2048,256]{3,2,1,0:T(8,128)(2,1)} %pad_maximum_fusion.1), channel_id=1, source_target_pairs={{0,192},{64,0},{128,64},{192,128},{1,193},{65,1},{129,65},{193,129... | collective-permute-start | bytes 6291464 | tf_op jit(solution)/shard_map/ppermute | solution.py:83
  130.4 42.8 %copy-start.1 = (bf16[1,2048,256]{2,1,0:T(8,128)(2,1)S(1)}, bf16[1,2048,256]{2,1,0:T(8,128)(2,1)}, u32[]{:S(2)}) copy-start(bf16[1,2048,256]{2,1,0:T(8,128)(2,1)} %param.30) | copy-start | bytes 3145732
  133.4 46.7 %all-to-all-start = ((bf16[64,1,4,2560]{3,2,1,0:T(4,128)(2,1)}), bf16[64,1,4,2560]{3,2,1,0:T(4,128)(2,1)S(1)}, u32[]{:S(2)}, u32[]{:S(2)}) async-start(bf16[64,1,4,2560]{3,2,1,0:T(4,128)(2,1)} %pad_maximum_fusion.2), calls=%async_computation | async-start | bytes 2621440 | tf_op jit(solution)/shard_map/all_to_all | solution.py:201
  140.8 48.8 %collective-permute-start.6 = (bf16[1,256,2048]{2,1,0:T(8,128)(2,1)}, bf16[1,256,2048]{2,1,0:T(8,128)(2,1)}, u32[]{:S(2)}, u32[]{:S(2)}) collective-permute-start(bf16[1,256,2048]{2,1,0:T(8,128)(2,1)} %param.31), channel_id=1, source_target_pairs={{0,64},{64,128},{128,192},{192,0},{1,65},{65,129},{129,193},{193,1... | collective-permute-start | bytes 3145736 | tf_op jit(solution)/shard_map/ppermute | solution.py:84
  142.3 47.7 %collective-permute-start.7 = (bf16[1,256,2048]{2,1,0:T(8,128)(2,1)}, bf16[1,256,2048]{2,1,0:T(8,128)(2,1)}, u32[]{:S(2)}, u32[]{:S(2)}) collective-permute-start(bf16[1,256,2048]{2,1,0:T(8,128)(2,1)} %param.31), channel_id=1, source_target_pairs={{0,128},{64,192},{128,0},{192,64},{1,129},{65,193},{129,1},{193,65... | collective-permute-start | bytes 3145736 | tf_op jit(solution)/shard_map/ppermute | solution.py:84
  144.0 73.2 %collective-permute-start.8 = (bf16[1,256,2048]{2,1,0:T(8,128)(2,1)}, bf16[1,256,2048]{2,1,0:T(8,128)(2,1)}, u32[]{:S(2)}, u32[]{:S(2)}) collective-permute-start(bf16[1,256,2048]{2,1,0:T(8,128)(2,1)} %param.31), channel_id=1, source_target_pairs={{0,192},{64,0},{128,64},{192,128},{1,193},{65,1},{129,65},{193,129... | collective-permute-start | bytes 3145736 | tf_op jit(solution)/shard_map/ppermute | solution.py:84
  181.9 4.9 %copy-start = (bf16[2,1,2048,1024]{3,2,1,0:T(8,128)(2,1)S(1)}, bf16[2,1,2048,1024]{3,2,1,0:T(8,128)(2,1)}, u32[]{:S(2)}) copy-start(bf16[2,1,2048,1024]{3,2,1,0:T(8,128)(2,1)} %pad_maximum_fusion) | copy-start | bytes 25165828
  186.9 30.4 %copy-start.9 = (bf16[1,256,2048]{2,1,0:T(8,128)(2,1)S(1)}, bf16[1,256,2048]{2,1,0:T(8,128)(2,1)}, u32[]{:S(2)}) copy-start(bf16[1,256,2048]{2,1,0:T(8,128)(2,1)} %param.31) | copy-start | bytes 3145732
  220.8 8.6 %copy-start.6 = (f32[64,8]{0,1:T(8,128)S(1)}, f32[64,8]{0,1:T(8,128)}, u32[]{:S(2)}) copy-start(f32[64,8]{0,1:T(8,128)} %param.33) | copy-start | bytes 6148
  222.0 36.1 %all-to-all-start.1 = ((bf16[64,1,4,2048]{3,2,1,0:T(4,128)(2,1)}), bf16[64,1,4,2048]{3,2,1,0:T(4,128)(2,1)S(1)}, u32[]{:S(2)}, u32[]{:S(2)}) async-start(bf16[64,1,4,2048]{3,2,1,0:T(4,128)(2,1)} %bitcast.110), calls=%async_computation.1 | async-start | bytes 2097152 | tf_op jit(solution)/shard_map/all_to_all | solution.py:208
  261.9 10.8 %collective-permute-start.10 = (bf16[64,2048]{1,0:T(8,128)(2,1)S(1)}, bf16[64,2048]{1,0:T(8,128)(2,1)S(1)}, u32[]{:S(2)}, u32[]{:S(2)}) collective-permute-start(bf16[64,2048]{1,0:T(8,128)(2,1)S(1)} %multiply_reduce_fusion), channel_id=1, source_target_pairs={{0,128},{64,192},{128,0},{192,64},{1,129},{65,193},{129,1},{193,65... | collective-permute-start | bytes 786440 | tf_op jit(solution)/shard_map/ppermute | solution.py:58
  265.0 11.1 %collective-permute-start.11 = (bf16[64,2048]{1,0:T(8,128)(2,1)S(1)}, bf16[64,2048]{1,0:T(8,128)(2,1)S(1)}, u32[]{:S(2)}, u32[]{:S(2)}) collective-permute-start(bf16[64,2048]{1,0:T(8,128)(2,1)S(1)} %multiply_reduce_fusion), channel_id=1, source_target_pairs={{0,192},{64,0},{128,64},{192,128},{1,193},{65,1},{129,65},{193,129... | collective-permute-start | bytes 786440 | tf_op jit(solution)/shard_map/ppermute | solution.py:58
  266.3 9.9 %collective-permute-start.9 = (bf16[64,2048]{1,0:T(8,128)(2,1)S(1)}, bf16[64,2048]{1,0:T(8,128)(2,1)S(1)}, u32[]{:S(2)}, u32[]{:S(2)}) collective-permute-start(bf16[64,2048]{1,0:T(8,128)(2,1)S(1)} %multiply_reduce_fusion), channel_id=1, source_target_pairs={{0,64},{64,128},{128,192},{192,0},{1,65},{65,129},{129,193},{193,1... | collective-permute-start | bytes 786440 | tf_op jit(solution)/shard_map/ppermute | solution.py:58
Sparse Core Ops, SparseCore 0:
  11.4 84.6 all-gather.1

commit v7 on v6

--- a/solution.py
+++ b/solution.py
@@ -136,19 +136,13 @@
     stacked = lax.all_gather(
         jnp.stack([w_query, w_key, w_value, w_out]), "expert", axis=1, tiled=True
     )
-    full_query, full_key, full_value, full_out = (
-        stacked[0],
-        stacked[1],
-        stacked[2],
-        stacked[3],
-    )
+    full_out = stacked[3]
     resid_in = tokens.astype(jnp.float32)
     normed = norm_rows(resid_in, attn_gain)
-    queries = jnp.dot(normed, full_query, preferred_element_type=jnp.float32).astype(jnp.bfloat16)
-    new_keys = jnp.dot(normed, full_key, preferred_element_type=jnp.float32).astype(jnp.bfloat16)
-    new_values = jnp.dot(normed, full_value, preferred_element_type=jnp.float32).astype(
-        jnp.bfloat16
-    )
+    projected = jnp.einsum(
+        "td,wdc->wtc", normed, stacked[:3], preferred_element_type=jnp.float32
+    ).astype(jnp.bfloat16)
+    queries, new_keys, new_values = projected[0], projected[1], projected[2]
     cache_count = cache.shape[0]
     split_cache = cache.reshape(cache_count, 2, head_group, HD)
     all_keys = jnp.concatenate(

time: 286 us -> 283 us (0.990)
    dot_general x3 -> x1, matrix products: 6.34 us -> 4.04 us  [local_body(): jnp.einsum('td,wdc->wtc', normed, stacked[:3], preferred_element_type=jnp...]
where the time goes in v7:
time: 283 us; the launch traced here: 282 us
  waiting for transfers between devices  156 us (55%)
  starting transfers between devices  37.9 us (13%)
  local copies, waits for them, and re-layouts  29.8 us (11%)
  matrix products  25.6 us (9%)
  other arithmetic  18.4 us (7%)
  between operations  14.5 us (5%)
    all_gather x1, waiting for transfers between devices, local_body(): lax.all_gather(jnp.stack([w_query, w_key, w_value, w_out]), 'expert', axi...  56 us
    all_to_all x1, waiting for transfers between devices, local_body(): lax.all_to_all(contrib.astype(jnp.bfloat16), 'expert', split_axis=0, conc...  28.7 us
    ppermute x3, waiting for transfers between devices, expert_block(): down = lax.ppermute(held[0][1], 'dp', pairs)  27.6 us
    ppermute x3, waiting for transfers between devices, expert_block(): gate_up = lax.ppermute(held[0][0], 'dp', pairs)  26.8 us
    ppermute x6, waiting for transfers between devices, dp_sum(): lax.ppermute(part, 'dp', [(i, (i + s) % n_dp) for i in range(n_dp)])  16.5 us
    unnamed x32, local copies, waits for them, and re-layouts  14.2 us
    ppermute x6, starting transfers between devices, dp_sum(): lax.ppermute(part, 'dp', [(i, (i + s) % n_dp) for i in range(n_dp)])  10.9 us
    all_to_all x1, starting transfers between devices, local_body(): lax.all_to_all(send, 'expert', split_axis=0, concat_axis=0, tiled=True)  7.3 us
  transfers between devices with their start and end apart: 15, of which 10 were waited for; matrix products, arithmetic and copies ran while one was open for 22% of the time, Pallas kernels for 0%

profile of v7, /device:TPU:2, one launch (start us, length us, event | category | flops | bytes accessed | tf_op | source)
XLA Modules:
  0.0 281.8 jit_solution(9260365484401371391)
XLA Ops:
  7.2 1.5 pad_maximum_fusion.3
  8.7 3.1 %pad_maximum_fusion.1 = bf16[2,1,2048,256]{3,2,1,0:T(8,128)(2,1)} fusion(bf16[1,1,2048,256]{3,2,1,0:T(8,128)(2,1)} %bitcast.76, bf16[1,1,2048,256]{3,2,1,0:T(8,128)(2,1)} %bitcast.78), kind=kLoop, calls=%fused_computation.39 | loop fusion | flops 1048576 | bytes 4194304 | tf_op jit(solution)/shard_map/stack | solution.py:80
  11.8 1.6 collective-permute-start.3
  13.4 2.9 %collective-permute-start.4 = (bf16[2,1,2048,256]{3,2,1,0:T(8,128)(2,1)}, bf16[2,1,2048,256]{3,2,1,0:T(8,128)(2,1)}, u32[]{:S(2)}, u32[]{:S(2)}) collective-permute-start(bf16[2,1,2048,256]{3,2,1,0:T(8,128)(2,1)} %pad_maximum_fusion.1), channel_id=1, source_target_pairs={{0,128},{64,192},{128,0},{192,64},{1,129},{65,193},{129,1},{193,65... | collective-permute-start | bytes 6291464 | tf_op jit(solution)/shard_map/ppermute | solution.py:83
  16.3 6.5 %copy.84 = bf16[2048,1024]{0,1:T(8,128)(2,1)} copy(bf16[2048,1024]{1,0:T(8,128)(2,1)} %param.23) | data formatting | bytes 8388608 | tf_op args[6]
  22.7 4.0 %fusion.86 = (bf16[2048,1,4,128]{0,3,2,1:T(8,128)(2,1)}, bf16[2048,1,4,128]{0,3,2,1:T(8,128)(2,1)S(1)}) fusion(bf16[2048,2,4,128]{0,3,2,1:T(8,128)(2,1)} %bitcast.75), kind=kLoop, calls=%fused_computation.131 | loop fusion | bytes 8388608 | tf_op jit(solution)/shard_map/slice | solution.py:149
  26.7 3.9 %copy.101 = bf16[2048,1,4,128]{3,0,2,1:T(8,128)(2,1)} copy(bf16[2048,1,4,128]{0,3,2,1:T(8,128)(2,1)} %get-tuple-element.4) | data formatting | bytes 4194304
  30.7 2.5 copy.102
  33.3 0.2 reduce-window.8
  33.4 0.2 convert_reduce_fusion
  33.6 0.1 reduce_window_sum.24
  33.8 0.1 reshape.269
  34.0 3.8 %gather_fusion = s32[512]{0:T(512)S(1)} fusion(s32[64,64]{1,0:T(8,128)S(1)} %sub.48, s32[512]{0:T(512)S(1)} %reshape.269), kind=kCustom, calls=%fused_computation | custom fusion | bytes 8192 | tf_op jit(solution)/shard_map/jit(take_along_axis)/gather | solution.py:25
  38.1 0.1 reduce_window_sum.25
  38.3 0.8 gather_fusion.1
  39.5 0.2 fusion.38
  39.8 0.2 compare_and_fusion
  40.0 56.0 %all-gather.2.cloned.1.call-done = bf16[4,2048,512]{2,1,0:T(8,128)(2,1)} async-done(((bf16[4,32,512]{2,1,0:T(8,128)(2,1)}), bf16[4,2048,512]{2,1,0:T(8,128)(2,1)}) %all-gather.2.cloned.1.call-update) | async-done | bytes 8388624 | tf_op jit(solution)/shard_map/all_gather | solution.py:136
  96.0 4.0 %fusion.29 = bf16[3,64,512]{2,1,0:T(8,128)(2,1)S(1)} fusion(bf16[4,2048,512]{2,1,0:T(8,128)(2,1)} %all-gather.2.cloned.1.call-done, bf16[64,2048]{1,0:T(8,128)(2,1)S(1)} %copy-done.3, f32[2048]{0:T(1024)S(1)} %copy-done.10, f32[64]{0:T(128)S(1)} %add_rsqrt_fusion.1), kind=kOutput, calls=%fused_computation.43 | convolution fusion | flops 403275776 | bytes 6758656 | tf_op jit(solution)/shard_map/td,wdc->wtc/dot_general | solution.py:142
  100.3 4.2 %fusion.87 = (f32[4,64]{1,0:T(4,128)S(1)}, f32[4,64,2112]{2,1,0:T(8,128)}) fusion(bf16[64,4,128]{2,0,1:T(8,128)(2,1)S(1)} %copy.88, bf16[2048,4,128]{2,0,1:T(8,128)(2,1)} %bitcast.83, pred[64,2112]{1,0:T(8,128)(4,1)S(1)} %pad_add_fusion, bf16[64,4,128]{2,1,0:T(4,128)(2,1)S(1)} %reshape_squeeze.13), kind=kOutput, calls=%fused_computation.132 | convolution fusion | flops 144902208 | bytes 4527104 | tf_op jit(solution)/shard_map/sub | solution.py:163
  104.5 2.2 fusion.35
  106.6 2.3 convolution_convert_fusion.1
  109.0 1.6 collective-permute-start
  110.5 2.7 collective-permute-start.1
  113.3 1.4 collective-permute-start.2
  114.7 0.2 fusion.45
  115.0 0.2 convolution_convert_fusion.2
  115.2 0.2 reshape_reshape.6
  115.4 3.3 %collective-permute-done = bf16[64,2048]{1,0:T(8,128)(2,1)S(1)} collective-permute-done((bf16[64,2048]{1,0:T(8,128)(2,1)S(1)}, bf16[64,2048]{1,0:T(8,128)(2,1)S(1)}, u32[]{:S(2)}, u32[]{:S(2)}) %collective-permute-start) | collective-permute-done | bytes 262176 | tf_op jit(solution)/shard_map/ppermute | solution.py:58
  118.7 2.2 collective-permute-start.5
  121.0 4.3 %collective-permute-done.1 = bf16[64,2048]{1,0:T(8,128)(2,1)S(1)} collective-permute-done((bf16[64,2048]{1,0:T(8,128)(2,1)S(1)}, bf16[64,2048]{1,0:T(8,128)(2,1)S(1)}, u32[]{:S(2)}, u32[]{:S(2)}) %collective-permute-start.1) | collective-permute-done | bytes 262176 | tf_op jit(solution)/shard_map/ppermute | solution.py:58
  125.3 0.6 collective-permute-done.2
  126.0 0.5 multiply_reduce_fusion.1
  126.5 0.5 convolution_convert_fusion
  127.0 1.2 reshape.265
  128.2 3.0 %pad_maximum_fusion.2 = bf16[64,1,4,2560]{3,2,1,0:T(4,128)(2,1)} fusion(bf16[64,1,4,512]{3,2,1,0:T(4,128)(2,1)S(1)} %bitcast.84, bf16[64,1,4,2048]{3,2,1,0:T(4,128)(2,1)} %bitcast.81), kind=kLoop, calls=%fused_computation.40 | loop fusion | flops 2621440 | bytes 2621440 | tf_op jit(solution)/shard_map/concatenate | solution.py:192
  131.2 7.3 %all-to-all-start = ((bf16[64,1,4,2560]{3,2,1,0:T(4,128)(2,1)}), bf16[64,1,4,2560]{3,2,1,0:T(4,128)(2,1)S(1)}, u32[]{:S(2)}, u32[]{:S(2)}) async-start(bf16[64,1,4,2560]{3,2,1,0:T(4,128)(2,1)} %pad_maximum_fusion.2), calls=%async_computation | async-start | bytes 2621440 | tf_op jit(solution)/shard_map/all_to_all | solution.py:195
  138.5 1.6 collective-permute-start.6
  140.1 1.7 collective-permute-start.7
  141.8 2.4 collective-permute-start.8
  144.3 26.8 %collective-permute-done.5 = bf16[2,1,2048,256]{3,2,1,0:T(8,128)(2,1)} collective-permute-done((bf16[2,1,2048,256]{3,2,1,0:T(8,128)(2,1)}, bf16[2,1,2048,256]{3,2,1,0:T(8,128)(2,1)}, u32[]{:S(2)}, u32[]{:S(2)}) %collective-permute-start.5) | collective-permute-done | bytes 2097184 | tf_op jit(solution)/shard_map/ppermute | solution.py:83
  171.0 6.9 %pad_maximum_fusion = bf16[2,1,2048,1024]{3,2,1,0:T(8,128)(2,1)} fusion(bf16[2,1,2048,256]{3,2,1,0:T(8,128)(2,1)} %collective-permute-done.5, bf16[2,1,2048,256]{3,2,1,0:T(8,128)(2,1)} %collective-permute-done.4, bf16[2,1,2048,256]{3,2,1,0:T(8,128)(2,1)} %collective-permute-done.3, bf16[1,1,2048,256]{3,2,1,0:T(8,128)(2,1)S(1)} %bitcast.77, ...), kind=kLoop, calls=%fused_computation.3 | loop fusion | flops 41943040 | bytes 16777216 | tf_op jit(solution)/shard_map/concatenate | solution.py:86
  177.9 0.6 slice.71
  178.5 1.2 reshape_squeeze.15
  179.7 3.9 %fusion.6 = f32[256,1024]{1,0:T(8,128)S(1)} fusion(bf16[256,2048]{1,0:T(8,128)(2,1)} %reshape_squeeze.15, bf16[2,1,2048,1024]{3,2,1,0:T(8,128)(2,1)} %pad_maximum_fusion), kind=kOutput, calls=%fused_computation.12 | convolution fusion | flops 1073741824 | bytes 6291456 | tf_op jit(solution)/shard_map/dot_general | solution.py:91
  183.6 1.0 copy-done
  184.6 2.7 multiply_convert_fusion
  187.4 0.5 collective-permute-done.7
  187.8 27.2 %collective-permute-done.8 = bf16[1,256,2048]{2,1,0:T(8,128)(2,1)} collective-permute-done((bf16[1,256,2048]{2,1,0:T(8,128)(2,1)}, bf16[1,256,2048]{2,1,0:T(8,128)(2,1)}, u32[]{:S(2)}, u32[]{:S(2)}) %collective-permute-start.8) | collective-permute-done | bytes 1048608 | tf_op jit(solution)/shard_map/ppermute | solution.py:84
  215.0 2.9 %convert_convert_fusion = f32[4,256,2048]{2,1,0:T(8,128)S(1)} fusion(bf16[1,256,2048]{2,1,0:T(8,128)(2,1)} %collective-permute-done.8, bf16[1,256,2048]{2,1,0:T(8,128)(2,1)} %collective-permute-done.7, bf16[1,256,2048]{2,1,0:T(8,128)(2,1)} %collective-permute-done.6, bf16[1,256,2048]{2,1,0:T(8,128)(2,1)S(1)} %copy-done.9, ...), kind=kOutput, calls=%fused_computation.22 | convolution fusion | flops 1084227584 | bytes 13107200 | tf_op jit(solution)/shard_map/rnf,nfd->nrd/dot_general | solution.py:95
  217.9 0.7 fusion.25
  218.6 1.2 convert_element_type.131
  219.8 7.3 %all-to-all-start.1 = ((bf16[64,1,4,2048]{3,2,1,0:T(4,128)(2,1)}), bf16[64,1,4,2048]{3,2,1,0:T(4,128)(2,1)S(1)}, u32[]{:S(2)}, u32[]{:S(2)}) async-start(bf16[64,1,4,2048]{3,2,1,0:T(4,128)(2,1)} %bitcast.80), calls=%async_computation.1 | async-start | bytes 2097152 | tf_op jit(solution)/shard_map/all_to_all | solution.py:202
  227.2 28.7 %all-to-all-done.1 = bf16[64,1,4,2048]{3,2,1,0:T(4,128)(2,1)S(1)} async-done(((bf16[64,1,4,2048]{3,2,1,0:T(4,128)(2,1)}), bf16[64,1,4,2048]{3,2,1,0:T(4,128)(2,1)S(1)}, u32[]{:S(2)}, u32[]{:S(2)}) %all-to-all-start.1) | async-done | bytes 1048608 | tf_op jit(solution)/shard_map/all_to_all | solution.py:202
  255.9 1.1 reshape.289
  257.0 2.7 multiply_reduce_fusion
  259.7 3.1 %collective-permute-start.10 = (bf16[64,2048]{1,0:T(8,128)(2,1)S(1)}, bf16[64,2048]{1,0:T(8,128)(2,1)S(1)}, u32[]{:S(2)}, u32[]{:S(2)}) collective-permute-start(bf16[64,2048]{1,0:T(8,128)(2,1)S(1)} %multiply_reduce_fusion), channel_id=1, source_target_pairs={{0,128},{64,192},{128,0},{192,64},{1,129},{65,193},{129,1},{193,65... | collective-permute-start | bytes 786440 | tf_op jit(solution)/shard_map/ppermute | solution.py:58
  262.8 1.3 collective-permute-start.11
  264.1 0.7 collective-permute-start.9
  264.8 0.1 slice.78
  264.9 0.9 reshape_reshape.7
  265.8 4.7 %collective-permute-done.10 = bf16[64,2048]{1,0:T(8,128)(2,1)S(1)} collective-permute-done((bf16[64,2048]{1,0:T(8,128)(2,1)S(1)}, bf16[64,2048]{1,0:T(8,128)(2,1)S(1)}, u32[]{:S(2)}, u32[]{:S(2)}) %collective-permute-start.10) | collective-permute-done | bytes 262176 | tf_op jit(solution)/shard_map/ppermute | solution.py:58
  270.5 3.5 %collective-permute-done.11 = bf16[64,2048]{1,0:T(8,128)(2,1)S(1)} collective-permute-done((bf16[64,2048]{1,0:T(8,128)(2,1)S(1)}, bf16[64,2048]{1,0:T(8,128)(2,1)S(1)}, u32[]{:S(2)}, u32[]{:S(2)}) %collective-permute-start.11) | collective-permute-done | bytes 262176 | tf_op jit(solution)/shard_map/ppermute | solution.py:58
  274.0 1.0 add_convert_fusion
  (64 shorter events, 1.5 us)
Async XLA Ops:
  7.2 88.9 %all-gather.2.cloned.1.call-start = ((), (), s32[]{:S(2)}) async-start(), calls=%async_computation.2 | async-start | bytes 8519680 | tf_op jit(solution)/shard_map/all_gather | solution.py:136
  11.8 130.0 %collective-permute-start.3 = (bf16[2,1,2048,256]{3,2,1,0:T(8,128)(2,1)}, bf16[2,1,2048,256]{3,2,1,0:T(8,128)(2,1)}, u32[]{:S(2)}, u32[]{:S(2)}) collective-permute-start(bf16[2,1,2048,256]{3,2,1,0:T(8,128)(2,1)} %pad_maximum_fusion.1), channel_id=1, source_target_pairs={{0,64},{64,128},{128,192},{192,0},{1,65},{65,129},{129,193},{193,1... | collective-permute-start | bytes 6291464 | tf_op jit(solution)/shard_map/ppermute | solution.py:83
  13.4 130.9 %collective-permute-start.4 = (bf16[2,1,2048,256]{3,2,1,0:T(8,128)(2,1)}, bf16[2,1,2048,256]{3,2,1,0:T(8,128)(2,1)}, u32[]{:S(2)}, u32[]{:S(2)}) collective-permute-start(bf16[2,1,2048,256]{3,2,1,0:T(8,128)(2,1)} %pad_maximum_fusion.1), channel_id=1, source_target_pairs={{0,128},{64,192},{128,0},{192,64},{1,129},{65,193},{129,1},{193,65... | collective-permute-start | bytes 6291464 | tf_op jit(solution)/shard_map/ppermute | solution.py:83
  30.7 2.5 copy-start.4
  30.7 2.6 copy-start.11
  33.9 4.1 %copy-start.7 = (s32[64,1]{0,1:T(1,128)S(1)}, s32[64,1]{0,1:T(1,128)}, u32[]{:S(2)}) copy-start(s32[64,1]{0,1:T(1,128)} %param.27) | copy-start | bytes 772
  33.9 5.2 %copy-start.12 = (s32[1,16]{1,0:T(1,128)S(1)}, s32[1,16]{1,0:T(1,128)}, u32[]{:S(2)}) copy-start(s32[1,16]{1,0:T(1,128)} %param.24) | copy-start | bytes 196
  33.9 5.4 %copy-start.8 = (s32[1,4]{1,0:T(1,128)S(1)}, s32[1,4]{1,0:T(1,128)}, u32[]{:S(2)}) copy-start(s32[1,4]{1,0:T(1,128)} %param.25) | copy-start | bytes 52
  33.9 5.5 %copy-start.3 = (bf16[64,2048]{1,0:T(8,128)(2,1)S(1)}, bf16[64,2048]{1,0:T(8,128)(2,1)}, u32[]{:S(2)}) copy-start(bf16[64,2048]{1,0:T(8,128)(2,1)} %param.17) | copy-start | bytes 786436
  33.9 62.1 %copy-start.10 = (f32[2048]{0:T(1024)S(1)}, f32[2048]{0:T(1024)}, u32[]{:S(2)}) copy-start(f32[2048]{0:T(1024)} %param.18) | copy-start | bytes 24580
  100.2 4.2 %copy-start.2 = (bf16[2048,1,4,128]{3,0,2,1:T(8,128)(2,1)S(1)}, bf16[2048,1,4,128]{3,0,2,1:T(8,128)(2,1)}, u32[]{:S(2)}) copy-start(bf16[2048,1,4,128]{3,0,2,1:T(8,128)(2,1)} %copy.102) | copy-start | bytes 6291460
  106.6 19.8 %copy-start.5 = (f32[2048]{0:T(1024)S(1)}, f32[2048]{0:T(1024)}, u32[]{:S(2)}) copy-start(f32[2048]{0:T(1024)} %param.28) | copy-start | bytes 24580
  109.0 9.8 %collective-permute-start = (bf16[64,2048]{1,0:T(8,128)(2,1)S(1)}, bf16[64,2048]{1,0:T(8,128)(2,1)S(1)}, u32[]{:S(2)}, u32[]{:S(2)}) collective-permute-start(bf16[64,2048]{1,0:T(8,128)(2,1)S(1)} %convolution_convert_fusion.1), channel_id=1, source_target_pairs={{0,64},{64,128},{128,192},{192,0},{1,65},{65,129},{129,193},{193,1... | collective-permute-start | bytes 786440 | tf_op jit(solution)/shard_map/ppermute | solution.py:58
  110.5 14.8 %collective-permute-start.1 = (bf16[64,2048]{1,0:T(8,128)(2,1)S(1)}, bf16[64,2048]{1,0:T(8,128)(2,1)S(1)}, u32[]{:S(2)}, u32[]{:S(2)}) collective-permute-start(bf16[64,2048]{1,0:T(8,128)(2,1)S(1)} %convolution_convert_fusion.1), channel_id=1, source_target_pairs={{0,128},{64,192},{128,0},{192,64},{1,129},{65,193},{129,1},{193,65... | collective-permute-start | bytes 786440 | tf_op jit(solution)/shard_map/ppermute | solution.py:58
  113.3 12.7 %collective-permute-start.2 = (bf16[64,2048]{1,0:T(8,128)(2,1)S(1)}, bf16[64,2048]{1,0:T(8,128)(2,1)S(1)}, u32[]{:S(2)}, u32[]{:S(2)}) collective-permute-start(bf16[64,2048]{1,0:T(8,128)(2,1)S(1)} %convolution_convert_fusion.1), channel_id=1, source_target_pairs={{0,192},{64,0},{128,64},{192,128},{1,193},{65,1},{129,65},{193,129... | collective-permute-start | bytes 786440 | tf_op jit(solution)/shard_map/ppermute | solution.py:58
  118.7 52.3 %collective-permute-start.5 = (bf16[2,1,2048,256]{3,2,1,0:T(8,128)(2,1)}, bf16[2,1,2048,256]{3,2,1,0:T(8,128)(2,1)}, u32[]{:S(2)}, u32[]{:S(2)}) collective-permute-start(bf16[2,1,2048,256]{3,2,1,0:T(8,128)(2,1)} %pad_maximum_fusion.1), channel_id=1, source_target_pairs={{0,192},{64,0},{128,64},{192,128},{1,193},{65,1},{129,65},{193,129... | collective-permute-start | bytes 6291464 | tf_op jit(solution)/shard_map/ppermute | solution.py:83
  128.2 42.8 %copy-start.1 = (bf16[1,2048,256]{2,1,0:T(8,128)(2,1)S(1)}, bf16[1,2048,256]{2,1,0:T(8,128)(2,1)}, u32[]{:S(2)}) copy-start(bf16[1,2048,256]{2,1,0:T(8,128)(2,1)} %param.30) | copy-start | bytes 3145732
  131.2 46.7 %all-to-all-start = ((bf16[64,1,4,2560]{3,2,1,0:T(4,128)(2,1)}), bf16[64,1,4,2560]{3,2,1,0:T(4,128)(2,1)S(1)}, u32[]{:S(2)}, u32[]{:S(2)}) async-start(bf16[64,1,4,2560]{3,2,1,0:T(4,128)(2,1)} %pad_maximum_fusion.2), calls=%async_computation | async-start | bytes 2621440 | tf_op jit(solution)/shard_map/all_to_all | solution.py:195
  138.5 48.8 %collective-permute-start.6 = (bf16[1,256,2048]{2,1,0:T(8,128)(2,1)}, bf16[1,256,2048]{2,1,0:T(8,128)(2,1)}, u32[]{:S(2)}, u32[]{:S(2)}) collective-permute-start(bf16[1,256,2048]{2,1,0:T(8,128)(2,1)} %param.31), channel_id=1, source_target_pairs={{0,64},{64,128},{128,192},{192,0},{1,65},{65,129},{129,193},{193,1... | collective-permute-start | bytes 3145736 | tf_op jit(solution)/shard_map/ppermute | solution.py:84
  140.1 47.7 %collective-permute-start.7 = (bf16[1,256,2048]{2,1,0:T(8,128)(2,1)}, bf16[1,256,2048]{2,1,0:T(8,128)(2,1)}, u32[]{:S(2)}, u32[]{:S(2)}) collective-permute-start(bf16[1,256,2048]{2,1,0:T(8,128)(2,1)} %param.31), channel_id=1, source_target_pairs={{0,128},{64,192},{128,0},{192,64},{1,129},{65,193},{129,1},{193,65... | collective-permute-start | bytes 3145736 | tf_op jit(solution)/shard_map/ppermute | solution.py:84
  141.8 73.2 %collective-permute-start.8 = (bf16[1,256,2048]{2,1,0:T(8,128)(2,1)}, bf16[1,256,2048]{2,1,0:T(8,128)(2,1)}, u32[]{:S(2)}, u32[]{:S(2)}) collective-permute-start(bf16[1,256,2048]{2,1,0:T(8,128)(2,1)} %param.31), channel_id=1, source_target_pairs={{0,192},{64,0},{128,64},{192,128},{1,193},{65,1},{129,65},{193,129... | collective-permute-start | bytes 3145736 | tf_op jit(solution)/shard_map/ppermute | solution.py:84
  179.7 4.9 %copy-start = (bf16[2,1,2048,1024]{3,2,1,0:T(8,128)(2,1)S(1)}, bf16[2,1,2048,1024]{3,2,1,0:T(8,128)(2,1)}, u32[]{:S(2)}) copy-start(bf16[2,1,2048,1024]{3,2,1,0:T(8,128)(2,1)} %pad_maximum_fusion) | copy-start | bytes 25165828
  184.6 30.4 %copy-start.9 = (bf16[1,256,2048]{2,1,0:T(8,128)(2,1)S(1)}, bf16[1,256,2048]{2,1,0:T(8,128)(2,1)}, u32[]{:S(2)}) copy-start(bf16[1,256,2048]{2,1,0:T(8,128)(2,1)} %param.31) | copy-start | bytes 3145732
  218.6 8.6 %copy-start.6 = (f32[64,8]{0,1:T(8,128)S(1)}, f32[64,8]{0,1:T(8,128)}, u32[]{:S(2)}) copy-start(f32[64,8]{0,1:T(8,128)} %param.33) | copy-start | bytes 6148
  219.8 36.1 %all-to-all-start.1 = ((bf16[64,1,4,2048]{3,2,1,0:T(4,128)(2,1)}), bf16[64,1,4,2048]{3,2,1,0:T(4,128)(2,1)S(1)}, u32[]{:S(2)}, u32[]{:S(2)}) async-start(bf16[64,1,4,2048]{3,2,1,0:T(4,128)(2,1)} %bitcast.80), calls=%async_computation.1 | async-start | bytes 2097152 | tf_op jit(solution)/shard_map/all_to_all | solution.py:202
  259.7 10.8 %collective-permute-start.10 = (bf16[64,2048]{1,0:T(8,128)(2,1)S(1)}, bf16[64,2048]{1,0:T(8,128)(2,1)S(1)}, u32[]{:S(2)}, u32[]{:S(2)}) collective-permute-start(bf16[64,2048]{1,0:T(8,128)(2,1)S(1)} %multiply_reduce_fusion), channel_id=1, source_target_pairs={{0,128},{64,192},{128,0},{192,64},{1,129},{65,193},{129,1},{193,65... | collective-permute-start | bytes 786440 | tf_op jit(solution)/shard_map/ppermute | solution.py:58
  262.8 11.1 %collective-permute-start.11 = (bf16[64,2048]{1,0:T(8,128)(2,1)S(1)}, bf16[64,2048]{1,0:T(8,128)(2,1)S(1)}, u32[]{:S(2)}, u32[]{:S(2)}) collective-permute-start(bf16[64,2048]{1,0:T(8,128)(2,1)S(1)} %multiply_reduce_fusion), channel_id=1, source_target_pairs={{0,192},{64,0},{128,64},{192,128},{1,193},{65,1},{129,65},{193,129... | collective-permute-start | bytes 786440 | tf_op jit(solution)/shard_map/ppermute | solution.py:58
  264.1 9.9 %collective-permute-start.9 = (bf16[64,2048]{1,0:T(8,128)(2,1)S(1)}, bf16[64,2048]{1,0:T(8,128)(2,1)S(1)}, u32[]{:S(2)}, u32[]{:S(2)}) collective-permute-start(bf16[64,2048]{1,0:T(8,128)(2,1)S(1)} %multiply_reduce_fusion), channel_id=1, source_target_pairs={{0,64},{64,128},{128,192},{192,0},{1,65},{65,129},{129,193},{193,1... | collective-permute-start | bytes 786440 | tf_op jit(solution)/shard_map/ppermute | solution.py:58
Sparse Core Ops, SparseCore 0:
  11.4 84.6 all-gather.1

commit v8 on v7

--- a/solution.py
+++ b/solution.py
@@ -202,14 +202,14 @@
     returned = lax.all_to_all(
         contrib.astype(jnp.bfloat16), "expert", split_axis=0, concat_axis=0, tiled=True
     ).reshape(experts_all * quarter, model_width)
-    back_pick = (
-        q_slot.reshape(-1)[:, None]
-        == jnp.arange(experts_all * quarter, dtype=jnp.int32)[None, :]
-    ).astype(jnp.bfloat16)
-    picked = jnp.dot(back_pick, returned, preferred_element_type=jnp.float32).reshape(
-        row_count, top_count, model_width
-    )
-    moe_part = jnp.sum(picked * gate_weights[:, :, None], axis=1)
+    hits = q_slot[:, :, None] == jnp.arange(experts_all * quarter, dtype=jnp.int32)[None, None, :]
+    weighting = jnp.sum(jnp.where(hits, gate_weights[:, :, None], 0.0), axis=1)
+    moe_part = jnp.dot(
+        weighting,
+        returned.astype(jnp.float32),
+        precision=lax.Precision.HIGHEST,
+        preferred_element_type=jnp.float32,
+    )
     moe_total = dp_sum(moe_part.astype(jnp.bfloat16))
     out = (residual + moe_total).astype(jnp.bfloat16)
     new_rows = got_kv.reshape(n_expert * kv_cap, kv_row.shape[1])

time: 283 us -> 283 us (level)
  no operation moved by 1% of the time
where the time goes in v8:
time: 283 us; the launch traced here: 281 us
  waiting for transfers between devices  155 us (55%)
  starting transfers between devices  37.9 us (13%)
  local copies, waits for them, and re-layouts  29.8 us (11%)
  matrix products  24.8 us (9%)
  other arithmetic  18.6 us (7%)
  between operations  14.5 us (5%)
    all_gather x1, waiting for transfers between devices, local_body(): lax.all_gather(jnp.stack([w_query, w_key, w_value, w_out]), 'expert', axi...  56 us
    all_to_all x1, waiting for transfers between devices, local_body(): lax.all_to_all(contrib.astype(jnp.bfloat16), 'expert', split_axis=0, conc...  28.4 us
    ppermute x3, waiting for transfers between devices, expert_block(): down = lax.ppermute(held[0][1], 'dp', pairs)  27.6 us
    ppermute x3, waiting for transfers between devices, expert_block(): gate_up = lax.ppermute(held[0][0], 'dp', pairs)  26.8 us
    ppermute x6, waiting for transfers between devices, dp_sum(): lax.ppermute(part, 'dp', [(i, (i + s) % n_dp) for i in range(n_dp)])  16.5 us
    unnamed x32, local copies, waits for them, and re-layouts  14.2 us
    ppermute x6, starting transfers between devices, dp_sum(): lax.ppermute(part, 'dp', [(i, (i + s) % n_dp) for i in range(n_dp)])  10.9 us
    all_to_all x1, starting transfers between devices, local_body(): lax.all_to_all(send, 'expert', split_axis=0, concat_axis=0, tiled=True)  7.31 us
  transfers between devices with their start and end apart: 15, of which 10 were waited for; matrix products, arithmetic and copies ran while one was open for 22% of the time, Pallas kernels for 0%

profile of v8, /device:TPU:2, one launch (start us, length us, event | category | flops | bytes accessed | tf_op | source)
XLA Modules:
  0.0 281.0 jit_solution(14240901156447549017)
XLA Ops:
  7.2 1.5 pad_maximum_fusion.3
  8.7 3.1 %pad_maximum_fusion.1 = bf16[2,1,2048,256]{3,2,1,0:T(8,128)(2,1)} fusion(bf16[1,1,2048,256]{3,2,1,0:T(8,128)(2,1)} %bitcast.74, bf16[1,1,2048,256]{3,2,1,0:T(8,128)(2,1)} %bitcast.76), kind=kLoop, calls=%fused_computation.39 | loop fusion | flops 1048576 | bytes 4194304 | tf_op jit(solution)/shard_map/stack | solution.py:80
  11.8 1.6 collective-permute-start.3
  13.4 2.9 %collective-permute-start.4 = (bf16[2,1,2048,256]{3,2,1,0:T(8,128)(2,1)}, bf16[2,1,2048,256]{3,2,1,0:T(8,128)(2,1)}, u32[]{:S(2)}, u32[]{:S(2)}) collective-permute-start(bf16[2,1,2048,256]{3,2,1,0:T(8,128)(2,1)} %pad_maximum_fusion.1), channel_id=1, source_target_pairs={{0,128},{64,192},{128,0},{192,64},{1,129},{65,193},{129,1},{193,65... | collective-permute-start | bytes 6291464 | tf_op jit(solution)/shard_map/ppermute | solution.py:83
  16.3 6.5 %copy.84 = bf16[2048,1024]{0,1:T(8,128)(2,1)} copy(bf16[2048,1024]{1,0:T(8,128)(2,1)} %param.23) | data formatting | bytes 8388608 | tf_op args[6]
  22.7 4.0 %fusion.83 = (bf16[2048,1,4,128]{0,3,2,1:T(8,128)(2,1)}, bf16[2048,1,4,128]{0,3,2,1:T(8,128)(2,1)S(1)}) fusion(bf16[2048,2,4,128]{0,3,2,1:T(8,128)(2,1)} %bitcast.73), kind=kLoop, calls=%fused_computation.130 | loop fusion | bytes 8388608 | tf_op jit(solution)/shard_map/slice | solution.py:149
  26.7 3.9 %copy.101 = bf16[2048,1,4,128]{3,0,2,1:T(8,128)(2,1)} copy(bf16[2048,1,4,128]{0,3,2,1:T(8,128)(2,1)} %get-tuple-element.4) | data formatting | bytes 4194304
  30.7 2.5 copy.102
  33.3 0.2 reduce-window.8
  33.4 0.2 convert_reduce_fusion
  33.6 0.1 reduce_window_sum.24
  34.0 3.8 %gather_fusion = s32[512]{0:T(512)S(1)} fusion(s32[64,64]{1,0:T(8,128)S(1)} %sub.48, s32[512]{0:T(512)S(1)} %reshape.247), kind=kCustom, calls=%fused_computation | custom fusion | bytes 8192 | tf_op jit(solution)/shard_map/jit(take_along_axis)/gather | solution.py:25
  38.1 0.1 reduce_window_sum.25
  38.3 0.8 gather_fusion.1
  39.5 0.2 fusion.38
  39.8 0.2 compare_and_fusion
  40.0 56.0 %all-gather.2.cloned.1.call-done = bf16[4,2048,512]{2,1,0:T(8,128)(2,1)} async-done(((bf16[4,32,512]{2,1,0:T(8,128)(2,1)}), bf16[4,2048,512]{2,1,0:T(8,128)(2,1)}) %all-gather.2.cloned.1.call-update) | async-done | bytes 8388624 | tf_op jit(solution)/shard_map/all_gather | solution.py:136
  96.0 4.0 %fusion.29 = bf16[3,64,512]{2,1,0:T(8,128)(2,1)S(1)} fusion(bf16[4,2048,512]{2,1,0:T(8,128)(2,1)} %all-gather.2.cloned.1.call-done, bf16[64,2048]{1,0:T(8,128)(2,1)S(1)} %copy-done.3, f32[2048]{0:T(1024)S(1)} %copy-done.10, f32[64]{0:T(128)S(1)} %add_rsqrt_fusion.1), kind=kOutput, calls=%fused_computation.43 | convolution fusion | flops 403275776 | bytes 6758656 | tf_op jit(solution)/shard_map/td,wdc->wtc/dot_general | solution.py:142
  100.2 4.2 %fusion.84 = (f32[4,64]{1,0:T(4,128)S(1)}, f32[4,64,2112]{2,1,0:T(8,128)}) fusion(bf16[64,4,128]{2,0,1:T(8,128)(2,1)S(1)} %copy.88, bf16[2048,4,128]{2,0,1:T(8,128)(2,1)} %bitcast.81, pred[64,2112]{1,0:T(8,128)(4,1)S(1)} %pad_add_fusion, bf16[64,4,128]{2,1,0:T(4,128)(2,1)S(1)} %reshape_squeeze.13), kind=kOutput, calls=%fused_computation.131 | convolution fusion | flops 144902208 | bytes 4527104 | tf_op jit(solution)/shard_map/sub | solution.py:163
  104.5 2.2 fusion.35
  106.6 2.3 convolution_convert_fusion.2
  109.0 1.6 collective-permute-start
  110.5 2.7 collective-permute-start.1
  113.3 1.4 collective-permute-start.2
  114.7 0.2 fusion.43
  115.0 0.2 convolution_convert_fusion.3
  115.2 0.2 reshape_reshape.6
  115.4 3.3 %collective-permute-done = bf16[64,2048]{1,0:T(8,128)(2,1)S(1)} collective-permute-done((bf16[64,2048]{1,0:T(8,128)(2,1)S(1)}, bf16[64,2048]{1,0:T(8,128)(2,1)S(1)}, u32[]{:S(2)}, u32[]{:S(2)}) %collective-permute-start) | collective-permute-done | bytes 262176 | tf_op jit(solution)/shard_map/ppermute | solution.py:58
  118.7 2.3 collective-permute-start.5
  121.0 4.3 %collective-permute-done.1 = bf16[64,2048]{1,0:T(8,128)(2,1)S(1)} collective-permute-done((bf16[64,2048]{1,0:T(8,128)(2,1)S(1)}, bf16[64,2048]{1,0:T(8,128)(2,1)S(1)}, u32[]{:S(2)}, u32[]{:S(2)}) %collective-permute-start.1) | collective-permute-done | bytes 262176 | tf_op jit(solution)/shard_map/ppermute | solution.py:58
  125.3 0.7 collective-permute-done.2
  126.0 0.5 multiply_reduce_fusion
  126.5 0.5 convolution_convert_fusion
  127.0 1.2 reshape.243
  128.2 3.0 %pad_maximum_fusion.2 = bf16[64,1,4,2560]{3,2,1,0:T(4,128)(2,1)} fusion(bf16[64,1,4,512]{3,2,1,0:T(4,128)(2,1)S(1)} %bitcast.82, bf16[64,1,4,2048]{3,2,1,0:T(4,128)(2,1)} %bitcast.79), kind=kLoop, calls=%fused_computation.40 | loop fusion | flops 2621440 | bytes 2621440 | tf_op jit(solution)/shard_map/concatenate | solution.py:192
  131.2 7.3 %all-to-all-start = ((bf16[64,1,4,2560]{3,2,1,0:T(4,128)(2,1)}), bf16[64,1,4,2560]{3,2,1,0:T(4,128)(2,1)S(1)}, u32[]{:S(2)}, u32[]{:S(2)}) async-start(bf16[64,1,4,2560]{3,2,1,0:T(4,128)(2,1)} %pad_maximum_fusion.2), calls=%async_computation | async-start | bytes 2621440 | tf_op jit(solution)/shard_map/all_to_all | solution.py:195
  138.5 1.6 collective-permute-start.6
  140.1 1.7 collective-permute-start.7
  141.8 2.4 collective-permute-start.8
  144.2 26.8 %collective-permute-done.5 = bf16[2,1,2048,256]{3,2,1,0:T(8,128)(2,1)} collective-permute-done((bf16[2,1,2048,256]{3,2,1,0:T(8,128)(2,1)}, bf16[2,1,2048,256]{3,2,1,0:T(8,128)(2,1)}, u32[]{:S(2)}, u32[]{:S(2)}) %collective-permute-start.5) | collective-permute-done | bytes 2097184 | tf_op jit(solution)/shard_map/ppermute | solution.py:83
  171.0 6.9 %pad_maximum_fusion = bf16[2,1,2048,1024]{3,2,1,0:T(8,128)(2,1)} fusion(bf16[2,1,2048,256]{3,2,1,0:T(8,128)(2,1)} %collective-permute-done.5, bf16[2,1,2048,256]{3,2,1,0:T(8,128)(2,1)} %collective-permute-done.4, bf16[2,1,2048,256]{3,2,1,0:T(8,128)(2,1)} %collective-permute-done.3, bf16[1,1,2048,256]{3,2,1,0:T(8,128)(2,1)S(1)} %bitcast.75, ...), kind=kLoop, calls=%fused_computation.3 | loop fusion | flops 41943040 | bytes 16777216 | tf_op jit(solution)/shard_map/concatenate | solution.py:86
  177.9 0.6 slice.71
  178.5 1.2 reshape_squeeze.15
  179.7 3.9 %fusion.6 = f32[256,1024]{1,0:T(8,128)S(1)} fusion(bf16[256,2048]{1,0:T(8,128)(2,1)} %reshape_squeeze.15, bf16[2,1,2048,1024]{3,2,1,0:T(8,128)(2,1)} %pad_maximum_fusion), kind=kOutput, calls=%fused_computation.12 | convolution fusion | flops 1073741824 | bytes 6291456 | tf_op jit(solution)/shard_map/dot_general | solution.py:91
  183.6 1.0 copy-done
  184.6 2.7 multiply_convert_fusion
  187.4 0.5 collective-permute-done.7
  187.8 27.2 %collective-permute-done.8 = bf16[1,256,2048]{2,1,0:T(8,128)(2,1)} collective-permute-done((bf16[1,256,2048]{2,1,0:T(8,128)(2,1)}, bf16[1,256,2048]{2,1,0:T(8,128)(2,1)}, u32[]{:S(2)}, u32[]{:S(2)}) %collective-permute-start.8) | collective-permute-done | bytes 1048608 | tf_op jit(solution)/shard_map/ppermute | solution.py:84
  215.0 2.9 %convert_convert_fusion = f32[4,256,2048]{2,1,0:T(8,128)S(1)} fusion(bf16[1,256,2048]{2,1,0:T(8,128)(2,1)} %collective-permute-done.8, bf16[1,256,2048]{2,1,0:T(8,128)(2,1)} %collective-permute-done.7, bf16[1,256,2048]{2,1,0:T(8,128)(2,1)} %collective-permute-done.6, bf16[1,256,2048]{2,1,0:T(8,128)(2,1)S(1)} %copy-done.9, ...), kind=kOutput, calls=%fused_computation.21 | convolution fusion | flops 1084227584 | bytes 13107200 | tf_op jit(solution)/shard_map/rnf,nfd->nrd/dot_general | solution.py:95
  217.9 0.7 fusion.25
  218.6 1.2 convert_element_type.131
  219.8 7.3 %all-to-all-start.1 = ((bf16[64,1,4,2048]{3,2,1,0:T(4,128)(2,1)}), bf16[64,1,4,2048]{3,2,1,0:T(4,128)(2,1)S(1)}, u32[]{:S(2)}, u32[]{:S(2)}) async-start(bf16[64,1,4,2048]{3,2,1,0:T(4,128)(2,1)} %bitcast.78), calls=%async_computation.1 | async-start | bytes 2097152 | tf_op jit(solution)/shard_map/all_to_all | solution.py:202
  227.2 0.2 select_reduce_fusion
  227.4 28.4 %all-to-all-done.1 = bf16[64,1,4,2048]{3,2,1,0:T(4,128)(2,1)S(1)} async-done(((bf16[64,1,4,2048]{3,2,1,0:T(4,128)(2,1)}), bf16[64,1,4,2048]{3,2,1,0:T(4,128)(2,1)S(1)}, u32[]{:S(2)}, u32[]{:S(2)}) %all-to-all-start.1) | async-done | bytes 1048608 | tf_op jit(solution)/shard_map/all_to_all | solution.py:202
  255.9 1.1 reshape.246
  257.0 1.9 convolution_convert_fusion.1
  258.9 3.1 %collective-permute-start.10 = (bf16[64,2048]{1,0:T(8,128)(2,1)S(1)}, bf16[64,2048]{1,0:T(8,128)(2,1)S(1)}, u32[]{:S(2)}, u32[]{:S(2)}) collective-permute-start(bf16[64,2048]{1,0:T(8,128)(2,1)S(1)} %convolution_convert_fusion.1), channel_id=1, source_target_pairs={{0,128},{64,192},{128,0},{192,64},{1,129},{65,193},{129,1},{193,65... | collective-permute-start | bytes 786440 | tf_op jit(solution)/shard_map/ppermute | solution.py:58
  262.0 1.3 collective-permute-start.11
  263.3 0.7 collective-permute-start.9
  264.0 0.1 slice.78
  264.1 0.9 reshape_reshape.7
  265.0 4.7 %collective-permute-done.10 = bf16[64,2048]{1,0:T(8,128)(2,1)S(1)} collective-permute-done((bf16[64,2048]{1,0:T(8,128)(2,1)S(1)}, bf16[64,2048]{1,0:T(8,128)(2,1)S(1)}, u32[]{:S(2)}, u32[]{:S(2)}) %collective-permute-start.10) | collective-permute-done | bytes 262176 | tf_op jit(solution)/shard_map/ppermute | solution.py:58
  269.7 3.5 %collective-permute-done.11 = bf16[64,2048]{1,0:T(8,128)(2,1)S(1)} collective-permute-done((bf16[64,2048]{1,0:T(8,128)(2,1)S(1)}, bf16[64,2048]{1,0:T(8,128)(2,1)S(1)}, u32[]{:S(2)}, u32[]{:S(2)}) %collective-permute-start.11) | collective-permute-done | bytes 262176 | tf_op jit(solution)/shard_map/ppermute | solution.py:58
  273.2 1.0 add_convert_fusion
  (65 shorter events, 1.6 us)
Async XLA Ops:
  7.2 88.9 %all-gather.2.cloned.1.call-start = ((), (), s32[]{:S(2)}) async-start(), calls=%async_computation.2 | async-start | bytes 8519680 | tf_op jit(solution)/shard_map/all_gather | solution.py:136
  11.8 130.0 %collective-permute-start.3 = (bf16[2,1,2048,256]{3,2,1,0:T(8,128)(2,1)}, bf16[2,1,2048,256]{3,2,1,0:T(8,128)(2,1)}, u32[]{:S(2)}, u32[]{:S(2)}) collective-permute-start(bf16[2,1,2048,256]{3,2,1,0:T(8,128)(2,1)} %pad_maximum_fusion.1), channel_id=1, source_target_pairs={{0,64},{64,128},{128,192},{192,0},{1,65},{65,129},{129,193},{193,1... | collective-permute-start | bytes 6291464 | tf_op jit(solution)/shard_map/ppermute | solution.py:83
  13.4 130.9 %collective-permute-start.4 = (bf16[2,1,2048,256]{3,2,1,0:T(8,128)(2,1)}, bf16[2,1,2048,256]{3,2,1,0:T(8,128)(2,1)}, u32[]{:S(2)}, u32[]{:S(2)}) collective-permute-start(bf16[2,1,2048,256]{3,2,1,0:T(8,128)(2,1)} %pad_maximum_fusion.1), channel_id=1, source_target_pairs={{0,128},{64,192},{128,0},{192,64},{1,129},{65,193},{129,1},{193,65... | collective-permute-start | bytes 6291464 | tf_op jit(solution)/shard_map/ppermute | solution.py:83
  30.7 2.5 copy-start.4
  30.7 2.6 copy-start.11
  33.9 4.1 %copy-start.7 = (s32[64,1]{0,1:T(1,128)S(1)}, s32[64,1]{0,1:T(1,128)}, u32[]{:S(2)}) copy-start(s32[64,1]{0,1:T(1,128)} %param.27) | copy-start | bytes 772
  33.9 5.2 %copy-start.12 = (s32[1,16]{1,0:T(1,128)S(1)}, s32[1,16]{1,0:T(1,128)}, u32[]{:S(2)}) copy-start(s32[1,16]{1,0:T(1,128)} %param.24) | copy-start | bytes 196
  33.9 5.4 %copy-start.8 = (s32[1,4]{1,0:T(1,128)S(1)}, s32[1,4]{1,0:T(1,128)}, u32[]{:S(2)}) copy-start(s32[1,4]{1,0:T(1,128)} %param.25) | copy-start | bytes 52
  33.9 5.5 %copy-start.3 = (bf16[64,2048]{1,0:T(8,128)(2,1)S(1)}, bf16[64,2048]{1,0:T(8,128)(2,1)}, u32[]{:S(2)}) copy-start(bf16[64,2048]{1,0:T(8,128)(2,1)} %param.17) | copy-start | bytes 786436
  33.9 62.1 %copy-start.10 = (f32[2048]{0:T(1024)S(1)}, f32[2048]{0:T(1024)}, u32[]{:S(2)}) copy-start(f32[2048]{0:T(1024)} %param.18) | copy-start | bytes 24580
  100.2 4.2 %copy-start.2 = (bf16[2048,1,4,128]{3,0,2,1:T(8,128)(2,1)S(1)}, bf16[2048,1,4,128]{3,0,2,1:T(8,128)(2,1)}, u32[]{:S(2)}) copy-start(bf16[2048,1,4,128]{3,0,2,1:T(8,128)(2,1)} %copy.102) | copy-start | bytes 6291460
  106.6 19.8 %copy-start.5 = (f32[2048]{0:T(1024)S(1)}, f32[2048]{0:T(1024)}, u32[]{:S(2)}) copy-start(f32[2048]{0:T(1024)} %param.28) | copy-start | bytes 24580
  109.0 9.7 %collective-permute-start = (bf16[64,2048]{1,0:T(8,128)(2,1)S(1)}, bf16[64,2048]{1,0:T(8,128)(2,1)S(1)}, u32[]{:S(2)}, u32[]{:S(2)}) collective-permute-start(bf16[64,2048]{1,0:T(8,128)(2,1)S(1)} %convolution_convert_fusion.2), channel_id=1, source_target_pairs={{0,64},{64,128},{128,192},{192,0},{1,65},{65,129},{129,193},{193,1... | collective-permute-start | bytes 786440 | tf_op jit(solution)/shard_map/ppermute | solution.py:58
  110.5 14.8 %collective-permute-start.1 = (bf16[64,2048]{1,0:T(8,128)(2,1)S(1)}, bf16[64,2048]{1,0:T(8,128)(2,1)S(1)}, u32[]{:S(2)}, u32[]{:S(2)}) collective-permute-start(bf16[64,2048]{1,0:T(8,128)(2,1)S(1)} %convolution_convert_fusion.2), channel_id=1, source_target_pairs={{0,128},{64,192},{128,0},{192,64},{1,129},{65,193},{129,1},{193,65... | collective-permute-start | bytes 786440 | tf_op jit(solution)/shard_map/ppermute | solution.py:58
  113.3 12.7 %collective-permute-start.2 = (bf16[64,2048]{1,0:T(8,128)(2,1)S(1)}, bf16[64,2048]{1,0:T(8,128)(2,1)S(1)}, u32[]{:S(2)}, u32[]{:S(2)}) collective-permute-start(bf16[64,2048]{1,0:T(8,128)(2,1)S(1)} %convolution_convert_fusion.2), channel_id=1, source_target_pairs={{0,192},{64,0},{128,64},{192,128},{1,193},{65,1},{129,65},{193,129... | collective-permute-start | bytes 786440 | tf_op jit(solution)/shard_map/ppermute | solution.py:58
  118.7 52.3 %collective-permute-start.5 = (bf16[2,1,2048,256]{3,2,1,0:T(8,128)(2,1)}, bf16[2,1,2048,256]{3,2,1,0:T(8,128)(2,1)}, u32[]{:S(2)}, u32[]{:S(2)}) collective-permute-start(bf16[2,1,2048,256]{3,2,1,0:T(8,128)(2,1)} %pad_maximum_fusion.1), channel_id=1, source_target_pairs={{0,192},{64,0},{128,64},{192,128},{1,193},{65,1},{129,65},{193,129... | collective-permute-start | bytes 6291464 | tf_op jit(solution)/shard_map/ppermute | solution.py:83
  128.2 42.8 %copy-start.1 = (bf16[1,2048,256]{2,1,0:T(8,128)(2,1)S(1)}, bf16[1,2048,256]{2,1,0:T(8,128)(2,1)}, u32[]{:S(2)}) copy-start(bf16[1,2048,256]{2,1,0:T(8,128)(2,1)} %param.30) | copy-start | bytes 3145732
  131.2 46.7 %all-to-all-start = ((bf16[64,1,4,2560]{3,2,1,0:T(4,128)(2,1)}), bf16[64,1,4,2560]{3,2,1,0:T(4,128)(2,1)S(1)}, u32[]{:S(2)}, u32[]{:S(2)}) async-start(bf16[64,1,4,2560]{3,2,1,0:T(4,128)(2,1)} %pad_maximum_fusion.2), calls=%async_computation | async-start | bytes 2621440 | tf_op jit(solution)/shard_map/all_to_all | solution.py:195
  138.5 48.8 %collective-permute-start.6 = (bf16[1,256,2048]{2,1,0:T(8,128)(2,1)}, bf16[1,256,2048]{2,1,0:T(8,128)(2,1)}, u32[]{:S(2)}, u32[]{:S(2)}) collective-permute-start(bf16[1,256,2048]{2,1,0:T(8,128)(2,1)} %param.31), channel_id=1, source_target_pairs={{0,64},{64,128},{128,192},{192,0},{1,65},{65,129},{129,193},{193,1... | collective-permute-start | bytes 3145736 | tf_op jit(solution)/shard_map/ppermute | solution.py:84
  140.1 47.7 %collective-permute-start.7 = (bf16[1,256,2048]{2,1,0:T(8,128)(2,1)}, bf16[1,256,2048]{2,1,0:T(8,128)(2,1)}, u32[]{:S(2)}, u32[]{:S(2)}) collective-permute-start(bf16[1,256,2048]{2,1,0:T(8,128)(2,1)} %param.31), channel_id=1, source_target_pairs={{0,128},{64,192},{128,0},{192,64},{1,129},{65,193},{129,1},{193,65... | collective-permute-start | bytes 3145736 | tf_op jit(solution)/shard_map/ppermute | solution.py:84
  141.8 73.2 %collective-permute-start.8 = (bf16[1,256,2048]{2,1,0:T(8,128)(2,1)}, bf16[1,256,2048]{2,1,0:T(8,128)(2,1)}, u32[]{:S(2)}, u32[]{:S(2)}) collective-permute-start(bf16[1,256,2048]{2,1,0:T(8,128)(2,1)} %param.31), channel_id=1, source_target_pairs={{0,192},{64,0},{128,64},{192,128},{1,193},{65,1},{129,65},{193,129... | collective-permute-start | bytes 3145736 | tf_op jit(solution)/shard_map/ppermute | solution.py:84
  179.7 4.9 %copy-start = (bf16[2,1,2048,1024]{3,2,1,0:T(8,128)(2,1)S(1)}, bf16[2,1,2048,1024]{3,2,1,0:T(8,128)(2,1)}, u32[]{:S(2)}) copy-start(bf16[2,1,2048,1024]{3,2,1,0:T(8,128)(2,1)} %pad_maximum_fusion) | copy-start | bytes 25165828
  184.6 30.4 %copy-start.9 = (bf16[1,256,2048]{2,1,0:T(8,128)(2,1)S(1)}, bf16[1,256,2048]{2,1,0:T(8,128)(2,1)}, u32[]{:S(2)}) copy-start(bf16[1,256,2048]{2,1,0:T(8,128)(2,1)} %param.31) | copy-start | bytes 3145732
  218.6 8.6 %copy-start.6 = (f32[64,8]{0,1:T(8,128)S(1)}, f32[64,8]{0,1:T(8,128)}, u32[]{:S(2)}) copy-start(f32[64,8]{0,1:T(8,128)} %param.33) | copy-start | bytes 6148
  219.8 36.1 %all-to-all-start.1 = ((bf16[64,1,4,2048]{3,2,1,0:T(4,128)(2,1)}), bf16[64,1,4,2048]{3,2,1,0:T(4,128)(2,1)S(1)}, u32[]{:S(2)}, u32[]{:S(2)}) async-start(bf16[64,1,4,2048]{3,2,1,0:T(4,128)(2,1)} %bitcast.78), calls=%async_computation.1 | async-start | bytes 2097152 | tf_op jit(solution)/shard_map/all_to_all | solution.py:202
  258.9 10.8 %collective-permute-start.10 = (bf16[64,2048]{1,0:T(8,128)(2,1)S(1)}, bf16[64,2048]{1,0:T(8,128)(2,1)S(1)}, u32[]{:S(2)}, u32[]{:S(2)}) collective-permute-start(bf16[64,2048]{1,0:T(8,128)(2,1)S(1)} %convolution_convert_fusion.1), channel_id=1, source_target_pairs={{0,128},{64,192},{128,0},{192,64},{1,129},{65,193},{129,1},{193,65... | collective-permute-start | bytes 786440 | tf_op jit(solution)/shard_map/ppermute | solution.py:58
  262.0 11.1 %collective-permute-start.11 = (bf16[64,2048]{1,0:T(8,128)(2,1)S(1)}, bf16[64,2048]{1,0:T(8,128)(2,1)S(1)}, u32[]{:S(2)}, u32[]{:S(2)}) collective-permute-start(bf16[64,2048]{1,0:T(8,128)(2,1)S(1)} %convolution_convert_fusion.1), channel_id=1, source_target_pairs={{0,192},{64,0},{128,64},{192,128},{1,193},{65,1},{129,65},{193,129... | collective-permute-start | bytes 786440 | tf_op jit(solution)/shard_map/ppermute | solution.py:58
  263.3 9.9 %collective-permute-start.9 = (bf16[64,2048]{1,0:T(8,128)(2,1)S(1)}, bf16[64,2048]{1,0:T(8,128)(2,1)S(1)}, u32[]{:S(2)}, u32[]{:S(2)}) collective-permute-start(bf16[64,2048]{1,0:T(8,128)(2,1)S(1)} %convolution_convert_fusion.1), channel_id=1, source_target_pairs={{0,64},{64,128},{128,192},{192,0},{1,65},{65,129},{129,193},{193,1... | collective-permute-start | bytes 786440 | tf_op jit(solution)/shard_map/ppermute | solution.py:58
Sparse Core Ops, SparseCore 0:
  11.4 84.6 all-gather.1
